TPU v7x, 512 devices: a whole 4x8x8 slice. The times are simulated.
512 devices in a mesh: feat: 16 (over x, z_hi, core), samp: 32 (over y, z_lo).
Axes of the slice: x: 4, y: 8, z: 8 (z_hi: 2, z_lo: 4; z = z_hi * 4 + z_lo), core: 2. Of those that a mesh axis runs over, the one named last changes fastest.
Arguments:
- tier_one: bfloat16 [8192, 12288], P('feat', 'samp')
- residuals: bfloat16 [12288, 128], P('samp'), may hold values from -6 to 6
- pair_list: int32 [3, 65536], P(None, 'feat'), may hold values from 0 to 8191, as said below
Outputs:
- scores: float32 [65536, 128], P(('feat', 'samp'))
Inputs may be any that keep to these rules, and one draw needn't show every extreme that they name: `pair_list`: rows 0 and 1 are feature indices, row 2 an operator id of 0 to 3; each descriptor's two features differ.
All inputs are finite; a program needn't handle non-finite values.
Results may differ from a plain program's by a relative error of at most 0.0031.
Values may be sent and summed in bfloat16 or wider, within the bound.
No kernel may reach another device: no remote copies, remote signals or barrier semaphores. Data moves between devices by JAX's collectives and lax.ppermute only.
A program may use at most 64 MiB of HBM per device.

v0:
```python
import math

import jax
import jax.numpy as jnp
from jax import lax
from jax.sharding import PartitionSpec as P

epsilon = 1e-05


def combine_rows(first_rows, second_rows, operator_id):
    first_rows = first_rows.astype(jnp.float32)
    second_rows = second_rows.astype(jnp.float32)
    quotient = first_rows / (1.0 + jnp.abs(second_rows))
    built = jnp.where(
        operator_id == 0,
        first_rows + second_rows,
        jnp.where(
            operator_id == 1,
            first_rows - second_rows,
            jnp.where(operator_id == 2, first_rows * second_rows, quotient),
        ),
    )
    return built.astype(jnp.bfloat16)


def descriptors(tier_one, pair_cols):
    first_rows = jnp.take(tier_one, pair_cols[0], axis=0)
    second_rows = jnp.take(tier_one, pair_cols[1], axis=0)
    return combine_rows(first_rows, second_rows, pair_cols[2][:, None])


def project_block(built, residuals):
    product = jnp.dot(built, residuals, preferred_element_type=jnp.float32)
    widened = built.astype(jnp.float32)
    return (product, jnp.sum(widened, axis=1), jnp.sum(widened * widened, axis=1))


def block_terms(tier_one, residuals, pair_cols):
    return project_block(descriptors(tier_one, pair_cols), residuals)


def finish(product, first_sums, square_sums, col_totals, sample_count):
    means = first_sums / sample_count
    variance = square_sums / sample_count - means * means
    centred = product - means[:, None] * col_totals[None, :]
    return centred * lax.rsqrt(variance + epsilon)[:, None] / math.sqrt(sample_count)


def per_device(tier_one, residuals, pair_list):
    local_pairs = pair_list.shape[1]
    width_k = residuals.shape[1]
    block_size = math.gcd(local_pairs, 1024)
    block_count = local_pairs // block_size
    grouped = pair_list.reshape(3, block_count, block_size).transpose(1, 0, 2)
    whole_rows = lax.all_gather(tier_one, "feat", axis=0, tiled=True)
    product, first_sums, square_sums = lax.map(
        lambda pair_cols: block_terms(whole_rows, residuals, pair_cols), grouped
    )
    product = product.reshape(local_pairs, width_k)
    first_sums = first_sums.reshape(local_pairs)
    square_sums = square_sums.reshape(local_pairs)
    col_totals = jnp.sum(residuals.astype(jnp.float32), axis=0)
    sample_count = residuals.shape[0] * lax.axis_size("samp")
    first_sums, square_sums, col_totals = lax.psum((first_sums, square_sums, col_totals), "samp")
    owned = lax.psum_scatter(product, "samp", scatter_dimension=0, tiled=True)
    owned_rows = owned.shape[0]
    row_start = lax.axis_index("samp") * owned_rows
    first_sums = lax.dynamic_slice_in_dim(first_sums, row_start, owned_rows, 0)
    square_sums = lax.dynamic_slice_in_dim(square_sums, row_start, owned_rows, 0)
    return finish(owned, first_sums, square_sums, col_totals, sample_count)


def solution(mesh):
    in_specs = (P("feat", "samp"), P("samp", None), P(None, "feat"))
    out_specs = P(("feat", "samp"), None)
    return jax.shard_map(
        per_device, mesh=mesh, in_specs=in_specs, out_specs=out_specs, check_vma=False
    )
```

profile of v0, /device:TPU:6, one launch (start us, length us, event | category | flops | bytes accessed | tf_op | source)
XLA Modules:
  0.0 361.1 jit_solution(16862348691693398649)
XLA Ops:
  6.5 0.0 all-gather.2.cloned.1.call-start
  6.5 0.7 all-gather.2.cloned.1.call-update
  7.3 0.0 reduce-scatter.2.cloned.1.call-start
  7.3 105.8 %all-gather.2.cloned.1.call-done = bf16[8192,384]{1,0:T(8,128)(2,1)} async-done(((bf16[512,384]{1,0:T(8,128)(2,1)}), bf16[8192,384]{1,0:T(8,128)(2,1)}) %all-gather.2.cloned.1.call-update) | async-done | bytes 6291472 | tf_op jit(solution)/shard_map/all_gather | solution.py:56
  113.1 78.5 %while.14 = (s32[]{:T(128)}, f32[4,1024,128]{2,1,0:T(8,128)}, f32[4,1024]{1,0:T(4,128)S(1)}, f32[4,1024]{1,0:T(4,128)S(1)}, s32[4,3,1024]{2,1,0:T(4,128)}, /*ind...) while((s32[]{:T(128)}, f32[4,1024,128]{2,1,0:T(8,128)}, ...), condition=%wide.region_3.5_spmd, body=%wide.region_0.4_spmd.sunk | while | flops 107762688 | bytes 7395525 | solution.py:57
  113.1 0.8 compare_reduce_fusion.4
  113.9 0.8 constant_dynamic-slice_fusion.4
  114.7 7.4 %gather_fusion = bf16[1024,384]{1,0:T(8,128)(2,1)S(1)} fusion(bf16[8192,384]{1,0:T(8,128)(2,1)} %get-tuple-element.169, s32[1024]{0:T(1024)S(1)} %fusion.20), kind=kCustom, calls=%fused_computation.1.clone.clone.1 | custom fusion | bytes 1576960 | tf_op jit(solution)/shard_map/while/body/eval_jaxpr/jit(_take)/gather | solution.py:29
  122.1 7.4 %gather_fusion.1 = bf16[1024,384]{1,0:T(8,128)(2,1)S(1)} fusion(bf16[8192,384]{1,0:T(8,128)(2,1)} %get-tuple-element.169, s32[1024]{0:T(1024)S(1)} %fusion.21), kind=kCustom, calls=%fused_computation.clone.clone.1 | custom fusion | bytes 1576960 | tf_op jit(solution)/shard_map/while/body/eval_jaxpr/jit(_take)/gather | solution.py:28
  129.5 0.0 copy-start
  129.5 1.9 fusion.22
  131.4 0.1 dynamic_update_slice.16
  131.4 0.1 dynamic_update_slice.17
  131.5 0.0 copy-done
  131.5 1.2 fusion.23
  132.7 0.8 compare_reduce_fusion.4
  133.5 0.8 constant_dynamic-slice_fusion.4
  134.3 7.4 %gather_fusion = bf16[1024,384]{1,0:T(8,128)(2,1)S(1)} fusion(bf16[8192,384]{1,0:T(8,128)(2,1)} %get-tuple-element.169, s32[1024]{0:T(1024)S(1)} %fusion.20), kind=kCustom, calls=%fused_computation.1.clone.clone.1 | custom fusion | bytes 1576960 | tf_op jit(solution)/shard_map/while/body/eval_jaxpr/jit(_take)/gather | solution.py:29
  141.7 7.4 %gather_fusion.1 = bf16[1024,384]{1,0:T(8,128)(2,1)S(1)} fusion(bf16[8192,384]{1,0:T(8,128)(2,1)} %get-tuple-element.169, s32[1024]{0:T(1024)S(1)} %fusion.21), kind=kCustom, calls=%fused_computation.clone.clone.1 | custom fusion | bytes 1576960 | tf_op jit(solution)/shard_map/while/body/eval_jaxpr/jit(_take)/gather | solution.py:28
  149.1 0.0 copy-start
  149.1 1.9 fusion.22
  151.0 0.1 dynamic_update_slice.16
  151.1 0.1 dynamic_update_slice.17
  151.1 0.0 copy-done
  151.1 1.2 fusion.23
  152.3 0.8 compare_reduce_fusion.4
  153.1 0.8 constant_dynamic-slice_fusion.4
  154.0 7.4 %gather_fusion = bf16[1024,384]{1,0:T(8,128)(2,1)S(1)} fusion(bf16[8192,384]{1,0:T(8,128)(2,1)} %get-tuple-element.169, s32[1024]{0:T(1024)S(1)} %fusion.20), kind=kCustom, calls=%fused_computation.1.clone.clone.1 | custom fusion | bytes 1576960 | tf_op jit(solution)/shard_map/while/body/eval_jaxpr/jit(_take)/gather | solution.py:29
  161.3 7.4 %gather_fusion.1 = bf16[1024,384]{1,0:T(8,128)(2,1)S(1)} fusion(bf16[8192,384]{1,0:T(8,128)(2,1)} %get-tuple-element.169, s32[1024]{0:T(1024)S(1)} %fusion.21), kind=kCustom, calls=%fused_computation.clone.clone.1 | custom fusion | bytes 1576960 | tf_op jit(solution)/shard_map/while/body/eval_jaxpr/jit(_take)/gather | solution.py:28
  168.7 0.0 copy-start
  168.7 1.9 fusion.22
  170.6 0.1 dynamic_update_slice.16
  170.7 0.1 dynamic_update_slice.17
  170.8 0.0 copy-done
  170.8 1.2 fusion.23
  171.9 0.8 compare_reduce_fusion.4
  172.7 0.8 constant_dynamic-slice_fusion.4
  173.5 7.4 %gather_fusion = bf16[1024,384]{1,0:T(8,128)(2,1)S(1)} fusion(bf16[8192,384]{1,0:T(8,128)(2,1)} %get-tuple-element.169, s32[1024]{0:T(1024)S(1)} %fusion.20), kind=kCustom, calls=%fused_computation.1.clone.clone.1 | custom fusion | bytes 1576960 | tf_op jit(solution)/shard_map/while/body/eval_jaxpr/jit(_take)/gather | solution.py:29
  180.9 7.4 %gather_fusion.1 = bf16[1024,384]{1,0:T(8,128)(2,1)S(1)} fusion(bf16[8192,384]{1,0:T(8,128)(2,1)} %get-tuple-element.169, s32[1024]{0:T(1024)S(1)} %fusion.21), kind=kCustom, calls=%fused_computation.clone.clone.1 | custom fusion | bytes 1576960 | tf_op jit(solution)/shard_map/while/body/eval_jaxpr/jit(_take)/gather | solution.py:28
  188.3 0.0 copy-start
  188.3 1.9 fusion.22
  190.2 0.1 dynamic_update_slice.16
  190.3 0.1 dynamic_update_slice.17
  190.4 0.0 copy-done
  190.4 1.2 fusion.23
  191.6 0.0 copy-start.1
  191.6 0.0 reduce-scatter.2.cloned.1.call-update
  191.6 0.9 copy-done.1
  192.4 0.1 convert_reduce_fusion.1
  192.5 151.1 %all-reduce = (f32[4096]{0:T(1024)S(1)}, f32[4096]{0:T(1024)S(1)}, f32[128]{0:T(128)S(1)}) all-reduce(f32[4096]{0:T(1024)S(1)} %get-tuple-element.77, f32[4096]{0:T(1024)S(1)} %get-tuple-element.78, f32[128]{0:T(128)S(1)} %convert_reduce_fusion.1), channel_id=1, replica_groups=mesh['feat'=16,'samp'=32] {'samp'}, use_global_device_ids=true, to_apply=%region_8.10 | all-reduce | flops 8320 | bytes 66560 | tf_op jit(solution)/shard_map/psum | solution.py:65
  343.6 0.1 dynamic-slice_multiply_fusion
  343.7 9.1 %reduce-scatter.2.cloned.1.call-done = f32[128,128]{1,0:T(8,128)} async-done(((f32[4096,128]{1,0:T(8,128)}), f32[128,128]{1,0:T(8,128)}) %reduce-scatter.2.cloned.1.call-update) | async-done | bytes 65552 | tf_op jit(solution)/shard_map/reduce_scatter | solution.py:66
  352.7 1.6 multiply_multiply_fusion
  (16 shorter events, 0.1 us)
Async XLA Ops:
  6.5 106.6 %all-gather.2.cloned.1.call-start = ((), (), s32[]{:S(2)}) async-start(), calls=%async_computation.1 | async-start | bytes 6684672 | tf_op jit(solution)/shard_map/all_gather | solution.py:56
  7.3 345.5 %reduce-scatter.2.cloned.1.call-start = ((), (), s32[]{:S(2)}) async-start(), calls=%async_computation.2 | async-start | bytes 2162688 | tf_op jit(solution)/shard_map/reduce_scatter | solution.py:66
  129.5 2.1 copy-start
  149.1 2.1 copy-start
  168.7 2.1 copy-start
  188.3 2.1 copy-start
  191.6 0.9 copy-start.1
Sparse Core Ops, SparseCore 0:
  10.6 102.4 all-gather.1
  191.7 160.9 reduce-scatter.1
where the time goes:
time: 362 us; the launch traced here: 361 us
  blocking collectives  151 us (42%)
  waiting for transfers between devices  116 us (32%)
  local copies, waits for them, and re-layouts  63.7 us (18%)
  between operations  13.4 us (4%)
  other arithmetic  12.4 us (3%)
  matrix products  4.72 us (1%)
    psum x1, blocking collectives, per_device(): lax.psum((first_sums, square_sums, col_totals), 'samp')  151 us
    all_gather x1, waiting for transfers between devices, per_device(): whole_rows = lax.all_gather(tier_one, 'feat', axis=0, tiled=True)  106 us
    gather x4, local copies, waits for them, and re-layouts, descriptors(): second_rows = jnp.take(tier_one, pair_cols[1], axis=0)  29.5 us
    gather x4, local copies, waits for them, and re-layouts, descriptors(): first_rows = jnp.take(tier_one, pair_cols[0], axis=0)  29.5 us
    reduce_scatter x1, waiting for transfers between devices, per_device(): owned = lax.psum_scatter(product, 'samp', scatter_dimension=0, tiled=True)  9.07 us
    reduce_sum x4, other arithmetic, project_block(): jnp.sum(widened * widened, axis=1)  7.52 us
  transfers between devices with their start and end apart: 2, of which 2 were waited for; matrix products, arithmetic and copies ran while one was open for 0% of the time, Pallas kernels for 0%

commit v1 on v0

v1 whole, which is shorter than its diff:
```python
import math

import jax
import jax.numpy as jnp
import numpy as np
from jax import lax
from jax.sharding import Mesh
from jax.sharding import PartitionSpec as P

epsilon = 1e-05

FEAT_AXES = ("x", "zh", "c")
SAMP_AXES = ("y", "zl")
EXTRA_ROWS = 8


def combine_rows(first_rows, second_rows, operator_id):
    first_rows = first_rows.astype(jnp.float32)
    second_rows = second_rows.astype(jnp.float32)
    quotient = first_rows / (1.0 + jnp.abs(second_rows))
    built = jnp.where(
        operator_id == 0,
        first_rows + second_rows,
        jnp.where(
            operator_id == 1,
            first_rows - second_rows,
            jnp.where(operator_id == 2, first_rows * second_rows, quotient),
        ),
    )
    return built.astype(jnp.bfloat16)


def finish(product, first_sums, square_sums, col_totals, sample_count):
    means = first_sums / sample_count
    variance = square_sums / sample_count - means * means
    centred = product - means[:, None] * col_totals[None, :]
    return centred * lax.rsqrt(variance + epsilon)[:, None] / math.sqrt(sample_count)


def per_device(tier_one, residuals, pair_list):
    local_rows = tier_one.shape[0]
    local_pairs = pair_list.shape[1]
    width_k = residuals.shape[1]
    n_x = lax.axis_size("x")
    n_zh = lax.axis_size("zh")
    n_y = lax.axis_size("y")
    n_zl = lax.axis_size("zl")
    n_samp = n_y * n_zl
    sample_count = residuals.shape[0] * n_samp

    rows = lax.all_gather(tier_one, "zh", axis=0, tiled=True)
    rows = lax.all_gather(rows, "x", axis=0, tiled=True)
    rows = lax.all_gather(rows, "c", axis=0, tiled=True)

    def position(g):
        f, r = g // local_rows, g % local_rows
        x, zh, c = f // (2 * n_zh), (f // 2) % n_zh, f % 2
        return ((c * n_x + x) * n_zh + zh) * local_rows + r

    first = jnp.take(rows, position(pair_list[0]), axis=0)
    second = jnp.take(rows, position(pair_list[1]), axis=0)
    built = combine_rows(first, second, pair_list[2][:, None])

    product = jnp.dot(built, residuals, preferred_element_type=jnp.float32)
    widened = built.astype(jnp.float32)
    first_sums = jnp.sum(widened, axis=1)
    square_sums = jnp.sum(widened * widened, axis=1)
    col_part = jnp.sum(residuals.astype(jnp.float32), axis=0)

    blocks = local_pairs // width_k
    block_rows = width_k + EXTRA_ROWS
    packed = jnp.concatenate(
        [
            product.reshape(blocks, width_k, width_k),
            jnp.broadcast_to(col_part[None, None, :], (blocks, 1, width_k)),
            first_sums.reshape(blocks, 1, width_k),
            square_sums.reshape(blocks, 1, width_k),
            jnp.zeros((blocks, EXTRA_ROWS - 3, width_k), jnp.float32),
        ],
        axis=1,
    ).reshape(blocks * block_rows, width_k)
    owned = lax.psum_scatter(packed, "y", scatter_dimension=0, tiled=True)
    owned = lax.psum_scatter(owned, "zl", scatter_dimension=0, tiled=True)

    return finish(
        owned[:width_k], owned[width_k + 1], owned[width_k + 2], owned[width_k],
        sample_count,
    )


def solution(mesh):
    n_feat, n_samp = mesh.devices.shape
    n_c, n_zh = 2, 2
    n_x = n_feat // (n_c * n_zh)
    n_zl = 4
    n_y = n_samp // n_zl
    devices = np.asarray(mesh.devices).reshape(n_x, n_zh, n_c, n_y, n_zl)
    fine = Mesh(devices, FEAT_AXES + SAMP_AXES)
    in_specs = (P(FEAT_AXES, SAMP_AXES), P(SAMP_AXES, None), P(None, FEAT_AXES))
    out_specs = P(FEAT_AXES + SAMP_AXES, None)
    return jax.shard_map(
        per_device, mesh=fine, in_specs=in_specs, out_specs=out_specs, check_vma=False
    )
```

time: 362 us -> 274 us (0.76)
  blocking collectives: 151 us -> 21.1 us
  waiting for transfers between devices: 116 us -> 183 us
  local copies, waits for them, and re-layouts: 63.7 us -> 43.8 us
  matrix products: 4.72 us -> 0.97 us
    psum x1 -> x0, blocking collectives: 151 us -> none  [per_device(): lax.psum((first_sums, square_sums, col_totals), 'samp')]
    unnamed x2 -> x5, waiting for transfers between devices: 0.73 us -> 56.7 us
    reduce_scatter x1, waiting for transfers between devices: 9.07 us -> 46.4 us  [per_device(): owned = lax.psum_scatter(packed, 'y', scatter_dimension=0, tiled=True)]
    all_gather x1 -> x2, waiting for transfers between devices: 106 us -> 79.6 us  [the longest x1 50.9 us: per_device(): rows = lax.all_gather(rows, 'x', axis=0, tiled=True)]
    all_gather x0 -> x1, blocking collectives: none -> 21.1 us  [per_device(): rows = lax.all_gather(tier_one, 'zh', axis=0, tiled=True)]
    gather x8 -> x2, local copies, waits for them, and re-layouts: 58.9 us -> 37.9 us  [the longest x1 20.3 us: per_device(): second = jnp.take(rows, position(pair_list[1]), axis=0)]
    concatenate x0 -> x1, local copies, waits for them, and re-layouts: none -> 3.83 us  [per_device(): jnp.concatenate([product.reshape(blocks, width_k, width_k), jnp.broadcast...]
    dot_general x4 -> x1, matrix products: 4.72 us -> 0.97 us  [per_device(): product = jnp.dot(built, residuals, preferred_element_type=jnp.float32)]
  transfers between devices with their start and end apart: 2 -> 4, of which waited for: 2 -> 4; matrix products, arithmetic and copies ran while one was open for 0% -> 1% of each run, Pallas kernels for 0% -> 0%
where the time goes in v1:
time: 274 us
  waiting for transfers between devices  183 us (67%)
  local copies, waits for them, and re-layouts  43.8 us (16%)
  blocking collectives  21.1 us (8%)
  between operations  13.9 us (5%)
  other arithmetic  11.3 us (4%)
    unnamed x5, waiting for transfers between devices  56.7 us
    all_gather x1, waiting for transfers between devices, per_device(): rows = lax.all_gather(rows, 'x', axis=0, tiled=True)  50.9 us
    reduce_scatter x1, waiting for transfers between devices, per_device(): owned = lax.psum_scatter(packed, 'y', scatter_dimension=0, tiled=True)  46.4 us
    all_gather x1, waiting for transfers between devices, per_device(): rows = lax.all_gather(rows, 'c', axis=0, tiled=True)  28.6 us
    all_gather x1, blocking collectives, per_device(): rows = lax.all_gather(tier_one, 'zh', axis=0, tiled=True)  21.1 us
    gather x1, local copies, waits for them, and re-layouts, per_device(): second = jnp.take(rows, position(pair_list[1]), axis=0)  20.3 us
    gather x1, local copies, waits for them, and re-layouts, per_device(): first = jnp.take(rows, position(pair_list[0]), axis=0)  17.6 us
    reduce_sum x1, other arithmetic, per_device(): square_sums = jnp.sum(widened * widened, axis=1)  8.66 us
  transfers between devices with their start and end apart: 4, of which 4 were waited for; matrix products, arithmetic and copies ran while one was open for 1% of the time, Pallas kernels for 0%

profile of v1, /device:TPU:6, one launch (start us, length us, event | category | flops | bytes accessed | tf_op | source)
XLA Modules:
  0.0 273.7 jit_solution(8182790167703745683)
XLA Ops:
  6.5 0.0 copy-start
  6.5 0.0 copy-start.1
  6.5 0.0 all-gather.3.cloned.1.call-start
  6.5 21.1 %all_gather.9 = bf16[1024,384]{1,0:T(8,128)(2,1)} all-gather(bf16[512,384]{1,0:T(8,128)(2,1)} %param.5), channel_id=1, replica_groups=mesh['x'=4,'zh'=2,'c'=2,'y'=8,'zl'=4] {'zh'}, dimensions={0}, use_global_device_ids=true | all-gather | bytes 1179648 | tf_op jit(solution)/shard_map/all_gather | solution.py:51
  27.6 0.0 all-gather.3.cloned.1.call-update
  27.6 0.0 all-gather.5.cloned.1.call-start
  27.7 50.9 %all-gather.3.cloned.1.call-done = bf16[4096,384]{1,0:T(8,128)(2,1)} async-done(((bf16[1024,384]{1,0:T(8,128)(2,1)}), bf16[4096,384]{1,0:T(8,128)(2,1)}) %all-gather.3.cloned.1.call-update) | async-done | bytes 3145744 | tf_op jit(solution)/shard_map/all_gather | solution.py:52
  78.6 0.0 all-gather.5.cloned.1.call-update
  78.6 0.0 reduce-scatter.2.cloned.1.call-start
  78.7 0.0 copy-done
  78.7 0.1 convert_reduce_fusion.1
  78.8 0.0 copy-done.1
  78.8 0.2 compare_reduce_fusion.2
  79.0 0.1 compare_and_fusion
  79.1 28.6 %all-gather.5.cloned.1.call-done = bf16[8192,384]{1,0:T(8,128)(2,1)} async-done(((bf16[4096,384]{1,0:T(8,128)(2,1)}), bf16[8192,384]{1,0:T(8,128)(2,1)}) %all-gather.5.cloned.1.call-update) | async-done | bytes 6291472 | tf_op jit(solution)/shard_map/all_gather | solution.py:53
  107.7 17.6 %gather_fusion = bf16[4096,384]{1,0:T(8,128)(2,1)S(1)} fusion(bf16[8192,384]{1,0:T(8,128)(2,1)} %all-gather.5.cloned.1.call-done, s32[4096]{0:T(1024)S(1)} %broadcast_clamp_fusion.1), kind=kCustom, calls=%fused_computation.clone | custom fusion | bytes 6307840 | tf_op jit(solution)/shard_map/jit(_take)/gather | solution.py:60
  125.4 20.3 %gather_fusion.1 = bf16[4096,384]{1,0:T(8,128)(2,1)} fusion(bf16[8192,384]{1,0:T(8,128)(2,1)} %all-gather.5.cloned.1.call-done, s32[4096]{0:T(1024)S(1)} %broadcast_clamp_fusion), kind=kCustom, calls=%fused_computation.1.clone | custom fusion | bytes 6307840 | tf_op jit(solution)/shard_map/jit(_take)/gather | solution.py:61
  145.6 8.7 %fusion = (f32[4096]{0:T(1024)S(1)}, f32[4096]{0:T(1024)S(1)}, bf16[4096,384]{1,0:T(8,128)(2,1)S(1)}) fusion(pred[4096]{0:T(1024)(128)(4,1)S(1)} %get-tuple-element.10, pred[4096]{0:T(1024)(128)(4,1)S(1)} %get-tuple-element.9, bf16[4096,384]{1,0:T(8,128)(2,1)} %gather_fusion.1, pred[4096]{0:T(1024)(128)(4,1)S(1)} %get-tuple-element.16, ...), kind=kLoop, calls=%fused_computation.9 | loop fusion | flops 28303360 | bytes 9490432 | tf_op jit(solution)/shard_map/reduce_sum | solution.py:67
  154.3 1.0 fusion.43
  155.3 3.8 %concatenate.3 = f32[32,136,128]{2,1,0:T(8,128)} concatenate(f32[32,128,128]{2,1,0:T(8,128)S(1)} %bitcast.20, f32[32,1,128]{2,1,0:T(1,128)S(1)} %broadcast_in_dim.41, f32[32,1,128]{2,1,0:T(1,128)S(1)} %bitcast.23, f32[32,1,128]{2,1,0:T(1,128)S(1)} %bitcast.22, f32[32,5,128]{2,1,0:T(8,128)S(1)} %broadcast_in_dim.42), dimensions={1} | concatenate | bytes 4456448 | tf_op jit(solution)/shard_map/concatenate | solution.py:72
  159.2 0.0 reduce-scatter.2.cloned.1.call-update
  159.2 0.0 all-reduce.3.cloned.1.call-start
  159.2 46.4 %reduce-scatter.2.cloned.1.call-done = f32[544,128]{1,0:T(8,128)} async-done(((f32[4352,128]{1,0:T(8,128)}), f32[544,128]{1,0:T(8,128)}) %reduce-scatter.2.cloned.1.call-update) | async-done | bytes 278544 | tf_op jit(solution)/shard_map/reduce_scatter | solution.py:82
  205.6 0.0 all-reduce.3.cloned.1.call-update
  205.6 1.3 dynamic-slice
  207.6 56.6 %all-reduce.3.cloned.1.call-done = f32[544,128]{1,0:T(8,128)} async-done(((f32[544,128]{1,0:T(8,128)}), f32[544,128]{1,0:T(8,128)}) %all-reduce.3.cloned.1.call-update) | async-done | bytes 278544
  264.2 0.7 fusion.39
  264.8 0.8 add_rsqrt_fusion
  265.6 1.6 fusion.7
  (5 shorter events, 0.1 us)
Async XLA Ops:
  6.5 72.2 %copy-start = (bf16[384,128]{1,0:T(8,128)(2,1)S(1)}, bf16[384,128]{1,0:T(8,128)(2,1)}, u32[]{:S(2)}) copy-start(bf16[384,128]{1,0:T(8,128)(2,1)} %param.6) | copy-start | bytes 294916
  6.5 72.2 %copy-start.1 = (s32[3,4096]{1,0:T(4,128)S(1)}, s32[3,4096]{1,0:T(4,128)}, u32[]{:S(2)}) copy-start(s32[3,4096]{1,0:T(4,128)} %param.7) | copy-start | bytes 147460
  6.5 72.1 %all-gather.3.cloned.1.call-start = ((), (), s32[]{:S(2)}) async-start(), calls=%async_computation.1 | async-start | bytes 3932160 | tf_op jit(solution)/shard_map/all_gather | solution.py:52
  27.6 80.1 %all-gather.5.cloned.1.call-start = ((), (), s32[]{:S(2)}) async-start(), calls=%async_computation.2 | async-start | bytes 9437184 | tf_op jit(solution)/shard_map/all_gather | solution.py:53
  78.6 127.0 %reduce-scatter.2.cloned.1.call-start = ((), (), s32[]{:S(2)}) async-start(), calls=%async_computation.3 | async-start | bytes 2506752 | tf_op jit(solution)/shard_map/reduce_scatter | solution.py:82
  159.2 105.0 %all-reduce.3.cloned.1.call-start = ((), (), s32[]{:S(2)}) async-start(), calls=%async_computation.4 | async-start | bytes 557056
Sparse Core Ops, SparseCore 0:
  27.7 50.8 all-gather.2
  80.7 26.9 all-gather.4
  159.3 46.2 reduce-scatter.1
  208.7 55.4 all-reduce.2

commit v2 on v1

--- a/solution.py
+++ b/solution.py
@@ -50,12 +50,15 @@
 
     rows = lax.all_gather(tier_one, "zh", axis=0, tiled=True)
     rows = lax.all_gather(rows, "x", axis=0, tiled=True)
-    rows = lax.all_gather(rows, "c", axis=0, tiled=True)
+    other = lax.ppermute(rows, "c", perm=[(0, 1), (1, 0)])
+    rows = jnp.concatenate([rows, other], axis=0)
+    my_c = lax.axis_index("c")
 
     def position(g):
         f, r = g // local_rows, g % local_rows
         x, zh, c = f // (2 * n_zh), (f // 2) % n_zh, f % 2
-        return ((c * n_x + x) * n_zh + zh) * local_rows + r
+        half = (c != my_c).astype(jnp.int32)
+        return ((half * n_x + x) * n_zh + zh) * local_rows + r
 
     first = jnp.take(rows, position(pair_list[0]), axis=0)
     second = jnp.take(rows, position(pair_list[1]), axis=0)
@@ -80,7 +83,15 @@
         axis=1,
     ).reshape(blocks * block_rows, width_k)
     owned = lax.psum_scatter(packed, "y", scatter_dimension=0, tiled=True)
-    owned = lax.psum_scatter(owned, "zl", scatter_dimension=0, tiled=True)
+    my_zl = lax.axis_index("zl")
+    total = lax.dynamic_slice_in_dim(owned, my_zl * block_rows, block_rows, 0)
+    for shift in range(1, n_zl):
+        dest = (my_zl + shift) % n_zl
+        piece = lax.dynamic_slice_in_dim(owned, dest * block_rows, block_rows, 0)
+        total = total + lax.ppermute(
+            piece, "zl", perm=[(i, (i + shift) % n_zl) for i in range(n_zl)]
+        )
+    owned = total
 
     return finish(
         owned[:width_k], owned[width_k + 1], owned[width_k + 2], owned[width_k],

time: 274 us -> 214 us (0.78)
  waiting for transfers between devices: 183 us -> 103 us
  starting transfers between devices: 0.12 us -> 12.6 us
  local copies, waits for them, and re-layouts: 43.8 us -> 49.6 us
    unnamed x5 -> x2, waiting for transfers between devices: 56.7 us -> 0.03 us
    all_gather x1 -> x0, waiting for transfers between devices: 28.6 us -> none  [per_device(): rows = lax.all_gather(rows, 'c', axis=0, tiled=True)]
    ppermute x0 -> x4, starting transfers between devices: none -> 12.5 us  [the longest x3 10.6 us: per_device(): lax.ppermute(piece, 'zl', perm=[(i, (i + shift) % n_zl) for i in range(n_...]
    ppermute x0 -> x4, waiting for transfers between devices: none -> 5.03 us  [the longest x3 5.03 us: per_device(): lax.ppermute(piece, 'zl', perm=[(i, (i + shift) % n_zl) for i in range(n_...]
  transfers between devices with their start and end apart: 4 -> 6, of which waited for: 4 -> 4; matrix products, arithmetic and copies ran while one was open for 1% -> 3% of each run, Pallas kernels for 0% -> 0%
where the time goes in v2:
time: 214 us; the launch traced here: 213 us
  waiting for transfers between devices  103 us (48%)
  local copies, waits for them, and re-layouts  49.6 us (23%)
  blocking collectives  20.9 us (10%)
  between operations  13.6 us (6%)
  starting transfers between devices  12.6 us (6%)
  other arithmetic  12.4 us (6%)
    all_gather x1, waiting for transfers between devices, per_device(): rows = lax.all_gather(rows, 'x', axis=0, tiled=True)  50.9 us
    reduce_scatter x1, waiting for transfers between devices, per_device(): owned = lax.psum_scatter(packed, 'y', scatter_dimension=0, tiled=True)  47.1 us
    all_gather x1, blocking collectives, per_device(): rows = lax.all_gather(tier_one, 'zh', axis=0, tiled=True)  20.9 us
    gather x1, local copies, waits for them, and re-layouts, per_device(): first = jnp.take(rows, position(pair_list[0]), axis=0)  20.3 us
    gather x1, local copies, waits for them, and re-layouts, per_device(): second = jnp.take(rows, position(pair_list[1]), axis=0)  17.6 us
    ppermute x3, starting transfers between devices, per_device(): lax.ppermute(piece, 'zl', perm=[(i, (i + shift) % n_zl) for i in range(n_...  10.6 us
    reduce_sum x1, other arithmetic, per_device(): square_sums = jnp.sum(widened * widened, axis=1)  8.65 us
    ppermute x3, waiting for transfers between devices, per_device(): lax.ppermute(piece, 'zl', perm=[(i, (i + shift) % n_zl) for i in range(n_...  5.03 us
  transfers between devices with their start and end apart: 6, of which 4 were waited for; matrix products, arithmetic and copies ran while one was open for 3% of the time, Pallas kernels for 0%

profile of v2, /device:TPU:6, one launch (start us, length us, event | category | flops | bytes accessed | tf_op | source)
XLA Modules:
  0.0 213.1 jit_solution(7331356729516595955)
XLA Ops:
  6.5 0.0 all-gather.2.cloned.1.call-start
  6.5 20.9 %all_gather.6 = bf16[1024,384]{1,0:T(8,128)(2,1)} all-gather(bf16[512,384]{1,0:T(8,128)(2,1)} %param.5), channel_id=1, replica_groups=mesh['x'=4,'zh'=2,'c'=2,'y'=8,'zl'=4] {'zh'}, dimensions={0}, use_global_device_ids=true | all-gather | bytes 1179648 | tf_op jit(solution)/shard_map/all_gather | solution.py:51
  27.5 0.0 all-gather.2.cloned.1.call-update
  27.5 0.0 reduce-scatter.2.cloned.1.call-start
  27.5 50.9 %all-gather.2.cloned.1.call-done = bf16[4096,384]{1,0:T(8,128)(2,1)} async-done(((bf16[1024,384]{1,0:T(8,128)(2,1)}), bf16[4096,384]{1,0:T(8,128)(2,1)}) %all-gather.2.cloned.1.call-update) | async-done | bytes 3145744 | tf_op jit(solution)/shard_map/all_gather | solution.py:52
  78.5 1.9 collective-permute-start
  80.4 1.0 convert_reduce_fusion.1
  81.4 1.0 compare_reduce_fusion.2
  82.4 0.9 fusion.34
  83.3 0.1 compare_and_fusion
  83.4 3.9 %constant_dynamic-update-slice_fusion.1 = bf16[8192,384]{1,0:T(8,128)(2,1)} fusion(bf16[4096,384]{1,0:T(8,128)(2,1)} %all-gather.2.cloned.1.call-done), kind=kLoop, calls=%fused_computation.88 | loop fusion | bytes 6291456
  87.3 0.0 collective-permute-done
  87.3 2.0 constant_dynamic-update-slice_fusion
  89.3 17.6 %gather_fusion.1 = bf16[4096,384]{1,0:T(8,128)(2,1)S(1)} fusion(bf16[8192,384]{1,0:T(8,128)(2,1)} %constant_dynamic-update-slice_fusion, s32[4096]{0:T(1024)S(1)} %broadcast_clamp_fusion), kind=kCustom, calls=%fused_computation.1.clone | custom fusion | bytes 6307840 | tf_op jit(solution)/shard_map/jit(_take)/gather | solution.py:64
  107.0 20.3 %gather_fusion = bf16[4096,384]{1,0:T(8,128)(2,1)} fusion(bf16[8192,384]{1,0:T(8,128)(2,1)} %constant_dynamic-update-slice_fusion, s32[4096]{0:T(1024)S(1)} %broadcast_clamp_fusion.1), kind=kCustom, calls=%fused_computation.clone | custom fusion | bytes 6307840 | tf_op jit(solution)/shard_map/jit(_take)/gather | solution.py:63
  127.3 0.0 copy-start
  127.3 8.7 %fusion = (f32[4096]{0:T(1024)S(1)}, f32[4096]{0:T(1024)S(1)}, bf16[4096,384]{1,0:T(8,128)(2,1)S(1)}) fusion(pred[4096]{0:T(1024)(128)(4,1)S(1)} %get-tuple-element.10, pred[4096]{0:T(1024)(128)(4,1)S(1)} %get-tuple-element.9, bf16[4096,384]{1,0:T(8,128)(2,1)S(1)} %gather_fusion.1, pred[4096]{0:T(1024)(128)(4,1)S(1)} %get-tuple-element.14, ...), kind=kLoop, calls=%fused_computation.9 | loop fusion | flops 28303360 | bytes 9490432 | tf_op jit(solution)/shard_map/reduce_sum | solution.py:70
  135.9 0.0 copy-done
  135.9 1.0 fusion.35
  137.0 3.8 %concatenate.7 = f32[32,136,128]{2,1,0:T(8,128)} concatenate(f32[32,128,128]{2,1,0:T(8,128)S(1)} %bitcast.20, f32[32,1,128]{2,1,0:T(1,128)S(1)} %broadcast_in_dim.41, f32[32,1,128]{2,1,0:T(1,128)S(1)} %bitcast.23, f32[32,1,128]{2,1,0:T(1,128)S(1)} %bitcast.22, f32[32,5,128]{2,1,0:T(8,128)S(1)} %broadcast_in_dim.42), dimensions={1} | concatenate | bytes 4456448 | tf_op jit(solution)/shard_map/concatenate | solution.py:75
  140.8 0.0 reduce-scatter.2.cloned.1.call-update
  140.9 47.1 %reduce-scatter.2.cloned.1.call-done = f32[544,128]{1,0:T(8,128)} async-done(((f32[4352,128]{1,0:T(8,128)}), f32[544,128]{1,0:T(8,128)}) %reduce-scatter.2.cloned.1.call-update) | async-done | bytes 278544 | tf_op jit(solution)/shard_map/reduce_scatter | solution.py:85
  188.0 1.0 constant_dynamic-slice_fusion.2
  188.9 5.7 %collective-permute-start.3 = (f32[136,128]{1,0:T(8,128)S(1)}, f32[136,128]{1,0:T(8,128)S(1)}, u32[]{:S(2)}, u32[]{:S(2)}) collective-permute-start(f32[136,128]{1,0:T(8,128)S(1)} %get-tuple-element.17), channel_id=1, source_target_pairs={{0,3},{1,0},{2,1},{3,2},{4,7},{5,4},{6,5},{7,6},{8,11},{9,8},{10,9... | collective-permute-start | bytes 208904 | tf_op jit(solution)/shard_map/ppermute | solution.py:91
  194.7 1.9 collective-permute-start.2
  196.6 3.0 %collective-permute-start.1 = (f32[136,128]{1,0:T(8,128)S(1)}, f32[136,128]{1,0:T(8,128)S(1)}, u32[]{:S(2)}, u32[]{:S(2)}) collective-permute-start(f32[136,128]{1,0:T(8,128)S(1)} %get-tuple-element.16), channel_id=1, source_target_pairs={{0,1},{1,2},{2,3},{3,0},{4,5},{5,6},{6,7},{7,4},{8,9},{9,10},{10,1... | collective-permute-start | bytes 208904 | tf_op jit(solution)/shard_map/ppermute | solution.py:91
  199.6 0.0 collective-permute-done.3
  199.6 2.2 %collective-permute-done.2 = f32[136,128]{1,0:T(8,128)S(1)} collective-permute-done((f32[136,128]{1,0:T(8,128)S(1)}, f32[136,128]{1,0:T(8,128)S(1)}, u32[]{:S(2)}, u32[]{:S(2)}) %collective-permute-start.2) | collective-permute-done | bytes 69664 | tf_op jit(solution)/shard_map/ppermute | solution.py:91
  201.8 2.8 %collective-permute-done.1 = f32[136,128]{1,0:T(8,128)S(1)} collective-permute-done((f32[136,128]{1,0:T(8,128)S(1)}, f32[136,128]{1,0:T(8,128)S(1)}, u32[]{:S(2)}, u32[]{:S(2)}) %collective-permute-start.1) | collective-permute-done | bytes 69664 | tf_op jit(solution)/shard_map/ppermute | solution.py:91
  204.6 0.9 add_add_fusion
  205.6 0.7 fusion.7
  (6 shorter events, 0.0 us)
Async XLA Ops:
  6.5 71.9 %all-gather.2.cloned.1.call-start = ((), (), s32[]{:S(2)}) async-start(), calls=%async_computation.1 | async-start | bytes 3932160 | tf_op jit(solution)/shard_map/all_gather | solution.py:52
  27.5 160.5 %reduce-scatter.2.cloned.1.call-start = ((), (), s32[]{:S(2)}) async-start(), calls=%async_computation.2 | async-start | bytes 2506752 | tf_op jit(solution)/shard_map/reduce_scatter | solution.py:85
  78.5 8.8 %collective-permute-start = (bf16[4096,384]{1,0:T(8,128)(2,1)}, bf16[4096,384]{1,0:T(8,128)(2,1)S(1)}, u32[]{:S(2)}, u32[]{:S(2)}) collective-permute-start(bf16[4096,384]{1,0:T(8,128)(2,1)} %all-gather.2.cloned.1.call-done), channel_id=1, source_target_pairs={{0,32},{32,0},{1,33},{33,1},{2,34},{34,2},{3,35},{35,3},{4,36},{36... | collective-permute-start | bytes 9437192 | tf_op jit(solution)/shard_map/ppermute | solution.py:53
  127.3 8.7 %copy-start = (bf16[384,128]{1,0:T(8,128)(2,1)S(1)}, bf16[384,128]{1,0:T(8,128)(2,1)}, u32[]{:S(2)}) copy-start(bf16[384,128]{1,0:T(8,128)(2,1)} %param.6) | copy-start | bytes 294916
  188.9 10.7 %collective-permute-start.3 = (f32[136,128]{1,0:T(8,128)S(1)}, f32[136,128]{1,0:T(8,128)S(1)}, u32[]{:S(2)}, u32[]{:S(2)}) collective-permute-start(f32[136,128]{1,0:T(8,128)S(1)} %get-tuple-element.17), channel_id=1, source_target_pairs={{0,3},{1,0},{2,1},{3,2},{4,7},{5,4},{6,5},{7,6},{8,11},{9,8},{10,9... | collective-permute-start | bytes 208904 | tf_op jit(solution)/shard_map/ppermute | solution.py:91
  194.7 7.1 %collective-permute-start.2 = (f32[136,128]{1,0:T(8,128)S(1)}, f32[136,128]{1,0:T(8,128)S(1)}, u32[]{:S(2)}, u32[]{:S(2)}) collective-permute-start(f32[136,128]{1,0:T(8,128)S(1)} %get-tuple-element.18), channel_id=1, source_target_pairs={{0,2},{1,3},{2,0},{3,1},{4,6},{5,7},{6,4},{7,5},{8,10},{9,11},{10,... | collective-permute-start | bytes 208904 | tf_op jit(solution)/shard_map/ppermute | solution.py:91
  196.6 8.0 %collective-permute-start.1 = (f32[136,128]{1,0:T(8,128)S(1)}, f32[136,128]{1,0:T(8,128)S(1)}, u32[]{:S(2)}, u32[]{:S(2)}) collective-permute-start(f32[136,128]{1,0:T(8,128)S(1)} %get-tuple-element.16), channel_id=1, source_target_pairs={{0,1},{1,2},{2,3},{3,0},{4,5},{5,6},{6,7},{7,4},{8,9},{9,10},{10,1... | collective-permute-start | bytes 208904 | tf_op jit(solution)/shard_map/ppermute | solution.py:91
Sparse Core Ops, SparseCore 0:
  27.6 50.8 all-gather.1
  140.9 46.9 reduce-scatter.1

commit v3 on v2

--- a/solution.py
+++ b/solution.py
@@ -48,26 +48,46 @@
     n_samp = n_y * n_zl
     sample_count = residuals.shape[0] * n_samp
 
-    rows = lax.all_gather(tier_one, "zh", axis=0, tiled=True)
-    rows = lax.all_gather(rows, "x", axis=0, tiled=True)
-    other = lax.ppermute(rows, "c", perm=[(0, 1), (1, 0)])
-    rows = jnp.concatenate([rows, other], axis=0)
+    my_zh = lax.axis_index("zh")
     my_c = lax.axis_index("c")
 
     def position(g):
         f, r = g // local_rows, g % local_rows
         x, zh, c = f // (2 * n_zh), (f // 2) % n_zh, f % 2
-        half = (c != my_c).astype(jnp.int32)
-        return ((half * n_x + x) * n_zh + zh) * local_rows + r
+        c_half = (c != my_c).astype(jnp.int32)
+        zh_half = (zh != my_zh).astype(jnp.int32)
+        return ((c_half * n_x + x) * n_zh + zh_half) * local_rows + r
 
-    first = jnp.take(rows, position(pair_list[0]), axis=0)
-    second = jnp.take(rows, position(pair_list[1]), axis=0)
-    built = combine_rows(first, second, pair_list[2][:, None])
+    first_pos = position(pair_list[0])
+    second_pos = position(pair_list[1])
+    operator_id = pair_list[2][:, None]
 
-    product = jnp.dot(built, residuals, preferred_element_type=jnp.float32)
-    widened = built.astype(jnp.float32)
-    first_sums = jnp.sum(widened, axis=1)
-    square_sums = jnp.sum(widened * widened, axis=1)
+    local_samples = tier_one.shape[1]
+    chunk = 128 if local_samples % 128 == 0 else local_samples
+    product = first_sums = square_sums = None
+    for start in range(0, local_samples, chunk):
+        part = tier_one[:, start:start + chunk]
+        part = jnp.concatenate(
+            [part, lax.ppermute(part, "zh", perm=[(0, 1), (1, 0)])], axis=0
+        )
+        part = lax.all_gather(part, "x", axis=0, tiled=True)
+        part = jnp.concatenate(
+            [part, lax.ppermute(part, "c", perm=[(0, 1), (1, 0)])], axis=0
+        )
+        first = jnp.take(part, first_pos, axis=0)
+        second = jnp.take(part, second_pos, axis=0)
+        built = combine_rows(first, second, operator_id)
+        res_part = residuals[start:start + chunk]
+        step_product = jnp.dot(built, res_part, preferred_element_type=jnp.float32)
+        widened = built.astype(jnp.float32)
+        step_first = jnp.sum(widened, axis=1)
+        step_square = jnp.sum(widened * widened, axis=1)
+        if product is None:
+            product, first_sums, square_sums = step_product, step_first, step_square
+        else:
+            product = product + step_product
+            first_sums = first_sums + step_first
+            square_sums = square_sums + step_square
     col_part = jnp.sum(residuals.astype(jnp.float32), axis=0)
 
     blocks = local_pairs // width_k

time: 214 us -> 305 us (1.43)
  local copies, waits for them, and re-layouts: 49.6 us -> 107 us
  starting transfers between devices: 12.6 us -> 46.7 us
  blocking collectives: 20.9 us -> 0 us
  waiting for transfers between devices: 103 us -> 120 us
    gather x2 -> x6, local copies, waits for them, and re-layouts: 37.9 us -> 90.9 us  [the longest x3 47.1 us: per_device(): second = jnp.take(part, second_pos, axis=0)]
    ppermute x1 -> x6, starting transfers between devices: 1.91 us -> 35.2 us  [the longest x3 29.5 us: per_device(): lax.ppermute(part, 'zh', perm=[(0, 1), (1, 0)])]
    all_gather x1 -> x0, blocking collectives: 20.9 us -> none  [per_device(): rows = lax.all_gather(tier_one, 'zh', axis=0, tiled=True)]
    ppermute x1 -> x6, waiting for transfers between devices: 0.01 us -> 11.7 us  [the longest x3 11.7 us: per_device(): lax.ppermute(part, 'zh', perm=[(0, 1), (1, 0)])]
    all_gather x1 -> x3, waiting for transfers between devices: 50.9 us -> 58.9 us  [per_device(): part = lax.all_gather(part, 'x', axis=0, tiled=True)]
  transfers between devices with their start and end apart: 6 -> 13, of which waited for: 4 -> 8; matrix products, arithmetic and copies ran while one was open for 3% -> 24% of each run, Pallas kernels for 0% -> 0%
where the time goes in v3:
time: 305 us; the launch traced here: 304 us
  waiting for transfers between devices  120 us (39%)
  local copies, waits for them, and re-layouts  107 us (35%)
  starting transfers between devices  46.7 us (15%)
  other arithmetic  14.8 us (5%)
  between operations  13.4 us (4%)
    all_gather x3, waiting for transfers between devices, per_device(): part = lax.all_gather(part, 'x', axis=0, tiled=True)  58.9 us
    gather x3, local copies, waits for them, and re-layouts, per_device(): second = jnp.take(part, second_pos, axis=0)  47.1 us
    reduce_scatter x1, waiting for transfers between devices, per_device(): owned = lax.psum_scatter(packed, 'y', scatter_dimension=0, tiled=True)  46.5 us
    gather x3, local copies, waits for them, and re-layouts, per_device(): first = jnp.take(part, first_pos, axis=0)  43.9 us
    ppermute x3, starting transfers between devices, per_device(): lax.ppermute(part, 'zh', perm=[(0, 1), (1, 0)])  29.5 us
    ppermute x3, waiting for transfers between devices, per_device(): lax.ppermute(part, 'zh', perm=[(0, 1), (1, 0)])  11.7 us
    ppermute x3, starting transfers between devices, per_device(): lax.ppermute(piece, 'zl', perm=[(i, (i + shift) % n_zl) for i in range(n_...  11.4 us
    reduce_sum x1, other arithmetic, per_device(): step_square = jnp.sum(widened * widened, axis=1)  10.6 us
  transfers between devices with their start and end apart: 13, of which 8 were waited for; matrix products, arithmetic and copies ran while one was open for 24% of the time, Pallas kernels for 0%

profile of v3, /device:TPU:6, one launch (start us, length us, event | category | flops | bytes accessed | tf_op | source)
XLA Modules:
  0.0 303.7 jit_solution(5692009375292623839)
XLA Ops:
  6.5 0.0 copy-start.1
  6.5 0.0 copy-start
  6.5 0.0 all-gather.4.cloned.1.call-start
  6.5 1.1 fusion.54
  7.6 10.9 %collective-permute-start = (bf16[512,128]{1,0:T(8,128)(2,1)S(1)}, bf16[512,128]{1,0:T(8,128)(2,1)S(1)}, u32[]{:S(2)}, u32[]{:S(2)}) collective-permute-start(bf16[512,128]{1,0:T(8,128)(2,1)S(1)} %get-tuple-element.23), channel_id=1, source_target_pairs={{0,64},{64,0},{1,65},{65,1},{2,66},{66,2},{3,67},{67,3},{4,68},{68... | collective-permute-start | bytes 393224 | tf_op jit(solution)/shard_map/ppermute | solution.py:71
  18.6 3.6 %collective-permute-done = bf16[512,128]{1,0:T(8,128)(2,1)S(1)} collective-permute-done((bf16[512,128]{1,0:T(8,128)(2,1)S(1)}, bf16[512,128]{1,0:T(8,128)(2,1)S(1)}, u32[]{:S(2)}, u32[]{:S(2)}) %collective-permute-start) | collective-permute-done | bytes 131104 | tf_op jit(solution)/shard_map/ppermute | solution.py:71
  22.1 0.7 pad_maximum_fusion
  22.9 0.0 all-gather.4.cloned.1.call-update
  22.9 0.0 all-gather.6.cloned.1.call-start
  22.9 10.3 %collective-permute-start.2 = (bf16[512,128]{1,0:T(8,128)(2,1)S(1)}, bf16[512,128]{1,0:T(8,128)(2,1)S(1)}, u32[]{:S(2)}, u32[]{:S(2)}) collective-permute-start(bf16[512,128]{1,0:T(8,128)(2,1)S(1)} %get-tuple-element.24), channel_id=1, source_target_pairs={{0,64},{64,0},{1,65},{65,1},{2,66},{66,2},{3,67},{67,3},{4,68},{68... | collective-permute-start | bytes 393224 | tf_op jit(solution)/shard_map/ppermute | solution.py:71
  33.2 4.5 %collective-permute-done.2 = bf16[512,128]{1,0:T(8,128)(2,1)S(1)} collective-permute-done((bf16[512,128]{1,0:T(8,128)(2,1)S(1)}, bf16[512,128]{1,0:T(8,128)(2,1)S(1)}, u32[]{:S(2)}, u32[]{:S(2)}) %collective-permute-start.2) | collective-permute-done | bytes 131104 | tf_op jit(solution)/shard_map/ppermute | solution.py:71
  37.8 0.7 pad_maximum_fusion.1
  38.5 0.0 all-gather.6.cloned.1.call-update
  38.5 0.0 all-gather.8.cloned.1.call-start
  38.6 8.3 %collective-permute-start.4 = (bf16[512,128]{1,0:T(8,128)(2,1)S(1)}, bf16[512,128]{1,0:T(8,128)(2,1)S(1)}, u32[]{:S(2)}, u32[]{:S(2)}) collective-permute-start(bf16[512,128]{1,0:T(8,128)(2,1)S(1)} %get-tuple-element.22), channel_id=1, source_target_pairs={{0,64},{64,0},{1,65},{65,1},{2,66},{66,2},{3,67},{67,3},{4,68},{68... | collective-permute-start | bytes 393224 | tf_op jit(solution)/shard_map/ppermute | solution.py:71
  46.9 0.0 copy-done.1
  46.9 0.0 copy-done
  46.9 0.1 convert_reduce_fusion.3
  47.0 0.2 compare_reduce_fusion.2
  47.1 3.6 %collective-permute-done.4 = bf16[512,128]{1,0:T(8,128)(2,1)S(1)} collective-permute-done((bf16[512,128]{1,0:T(8,128)(2,1)S(1)}, bf16[512,128]{1,0:T(8,128)(2,1)S(1)}, u32[]{:S(2)}, u32[]{:S(2)}) %collective-permute-start.4) | collective-permute-done | bytes 131104 | tf_op jit(solution)/shard_map/ppermute | solution.py:71
  50.7 0.7 pad_maximum_fusion.2
  51.5 0.0 all-gather.8.cloned.1.call-update
  51.5 0.0 reduce-scatter.2.cloned.1.call-start
  51.5 0.1 compare_and_fusion
  51.7 3.7 %all-gather.4.cloned.1.call-done = bf16[4096,128]{1,0:T(8,128)(2,1)} async-done(((bf16[1024,128]{1,0:T(8,128)(2,1)}), bf16[4096,128]{1,0:T(8,128)(2,1)}) %all-gather.4.cloned.1.call-update) | async-done | bytes 1048592 | tf_op jit(solution)/shard_map/all_gather | solution.py:73
  55.3 1.9 collective-permute-start.1
  57.3 2.3 constant_dynamic-update-slice_fusion.1
  59.5 27.6 %all-gather.6.cloned.1.call-done = bf16[4096,128]{1,0:T(8,128)(2,1)} async-done(((bf16[1024,128]{1,0:T(8,128)(2,1)}), bf16[4096,128]{1,0:T(8,128)(2,1)}) %all-gather.6.cloned.1.call-update) | async-done | bytes 1048592 | tf_op jit(solution)/shard_map/all_gather | solution.py:73
  87.1 1.9 collective-permute-start.3
  89.1 2.3 constant_dynamic-update-slice_fusion.3
  91.3 27.6 %all-gather.8.cloned.1.call-done = bf16[4096,128]{1,0:T(8,128)(2,1)} async-done(((bf16[1024,128]{1,0:T(8,128)(2,1)}), bf16[4096,128]{1,0:T(8,128)(2,1)}) %all-gather.8.cloned.1.call-update) | async-done | bytes 1048592 | tf_op jit(solution)/shard_map/all_gather | solution.py:73
  119.0 1.9 collective-permute-start.5
  120.9 1.3 constant_dynamic-update-slice_fusion.5
  122.2 0.0 collective-permute-done.1
  122.2 1.1 constant_dynamic-update-slice_fusion
  123.2 12.9 %gather_fusion = bf16[4096,128]{1,0:T(8,128)(2,1)S(1)} fusion(bf16[8192,128]{1,0:T(8,128)(2,1)} %constant_dynamic-update-slice_fusion, s32[4096]{0:T(1024)S(1)} %broadcast_clamp_fusion.1), kind=kCustom, calls=%fused_computation.clone | custom fusion | bytes 2113536 | tf_op jit(solution)/shard_map/jit(_take)/gather | solution.py:77
  136.1 16.1 %gather_fusion.1 = bf16[4096,128]{1,0:T(8,128)(2,1)} fusion(bf16[8192,128]{1,0:T(8,128)(2,1)} %constant_dynamic-update-slice_fusion, s32[4096]{0:T(1024)S(1)} %broadcast_clamp_fusion), kind=kCustom, calls=%fused_computation.1.clone | custom fusion | bytes 2113536 | tf_op jit(solution)/shard_map/jit(_take)/gather | solution.py:78
  152.2 0.0 collective-permute-done.3
  152.2 2.3 constant_dynamic-update-slice_fusion.2
  154.5 16.1 %gather_fusion.2 = bf16[4096,128]{1,0:T(8,128)(2,1)} fusion(bf16[8192,128]{1,0:T(8,128)(2,1)} %constant_dynamic-update-slice_fusion.2, s32[4096]{0:T(1024)S(1)} %broadcast_clamp_fusion.1), kind=kCustom, calls=%fused_computation.2.clone | custom fusion | bytes 2113536 | tf_op jit(solution)/shard_map/jit(_take)/gather | solution.py:77
  170.6 16.1 %gather_fusion.3 = bf16[4096,128]{1,0:T(8,128)(2,1)} fusion(bf16[8192,128]{1,0:T(8,128)(2,1)} %constant_dynamic-update-slice_fusion.2, s32[4096]{0:T(1024)S(1)} %broadcast_clamp_fusion), kind=kCustom, calls=%fused_computation.3.clone | custom fusion | bytes 2113536 | tf_op jit(solution)/shard_map/jit(_take)/gather | solution.py:78
  186.7 0.0 collective-permute-done.5
  186.7 1.4 constant_dynamic-update-slice_fusion.4
  188.1 14.9 %gather_fusion.4 = bf16[4096,128]{1,0:T(8,128)(2,1)} fusion(bf16[8192,128]{1,0:T(8,128)(2,1)S(1)} %constant_dynamic-update-slice_fusion.4, s32[4096]{0:T(1024)S(1)} %broadcast_clamp_fusion.1), kind=kCustom, calls=%fused_computation.4.clone | custom fusion | bytes 2113536 | tf_op jit(solution)/shard_map/jit(_take)/gather | solution.py:77
  203.0 14.9 %gather_fusion.5 = bf16[4096,128]{1,0:T(8,128)(2,1)} fusion(bf16[8192,128]{1,0:T(8,128)(2,1)S(1)} %constant_dynamic-update-slice_fusion.4, s32[4096]{0:T(1024)S(1)} %broadcast_clamp_fusion), kind=kCustom, calls=%fused_computation.5.clone | custom fusion | bytes 2113536 | tf_op jit(solution)/shard_map/jit(_take)/gather | solution.py:78
  217.9 10.6 %fusion.2 = (f32[4096]{0:T(1024)S(1)}, f32[4096]{0:T(1024)S(1)}, bf16[4096,128]{1,0:T(8,128)(2,1)S(1)}, f32[4096]{0:T(1024)S(1)}, f32[4096]{0:T(1024)S(1)}, /*in...) fusion(pred[4096]{0:T(1024)(128)(4,1)S(1)} %get-tuple-element.14, ...), kind=kLoop, calls=%fused_computation.31 | loop fusion | flops 28286976 | bytes 9555968 | tf_op jit(solution)/shard_map/reduce_sum | solution.py:84
  228.5 0.4 fusion.22
  228.9 0.4 convolution_add_fusion.1
  229.3 0.4 convolution_add_fusion
  229.8 3.8 %concatenate.27 = f32[32,136,128]{2,1,0:T(8,128)} concatenate(f32[32,128,128]{2,1,0:T(8,128)S(1)} %bitcast.22, f32[32,1,128]{2,1,0:T(1,128)S(1)} %broadcast_in_dim.59, f32[32,1,128]{2,1,0:T(1,128)S(1)} %bitcast.24, f32[32,1,128]{2,1,0:T(1,128)S(1)} %bitcast.23, f32[32,5,128]{2,1,0:T(8,128)S(1)} %broadcast_in_dim.60), dimensions={1} | concatenate | bytes 4456448 | tf_op jit(solution)/shard_map/concatenate | solution.py:95
  233.6 0.0 reduce-scatter.2.cloned.1.call-update
  233.7 46.5 %reduce-scatter.2.cloned.1.call-done = f32[544,128]{1,0:T(8,128)} async-done(((f32[4352,128]{1,0:T(8,128)}), f32[544,128]{1,0:T(8,128)}) %reduce-scatter.2.cloned.1.call-update) | async-done | bytes 278544 | tf_op jit(solution)/shard_map/reduce_scatter | solution.py:105
  280.2 1.0 constant_dynamic-slice_fusion.2
  281.2 3.5 %collective-permute-start.6 = (f32[136,128]{1,0:T(8,128)S(1)}, f32[136,128]{1,0:T(8,128)S(1)}, u32[]{:S(2)}, u32[]{:S(2)}) collective-permute-start(f32[136,128]{1,0:T(8,128)S(1)} %get-tuple-element.25), channel_id=1, source_target_pairs={{0,1},{1,2},{2,3},{3,0},{4,5},{5,6},{6,7},{7,4},{8,9},{9,10},{10,1... | collective-permute-start | bytes 208904 | tf_op jit(solution)/shard_map/ppermute | solution.py:111
  284.7 4.6 %collective-permute-start.7 = (f32[136,128]{1,0:T(8,128)S(1)}, f32[136,128]{1,0:T(8,128)S(1)}, u32[]{:S(2)}, u32[]{:S(2)}) collective-permute-start(f32[136,128]{1,0:T(8,128)S(1)} %get-tuple-element.27), channel_id=1, source_target_pairs={{0,2},{1,3},{2,0},{3,1},{4,6},{5,7},{6,4},{7,5},{8,10},{9,11},{10,... | collective-permute-start | bytes 208904 | tf_op jit(solution)/shard_map/ppermute | solution.py:111
  289.3 3.3 %collective-permute-start.8 = (f32[136,128]{1,0:T(8,128)S(1)}, f32[136,128]{1,0:T(8,128)S(1)}, u32[]{:S(2)}, u32[]{:S(2)}) collective-permute-start(f32[136,128]{1,0:T(8,128)S(1)} %get-tuple-element.26), channel_id=1, source_target_pairs={{0,3},{1,0},{2,1},{3,2},{4,7},{5,4},{6,5},{7,6},{8,11},{9,8},{10,9... | collective-permute-start | bytes 208904 | tf_op jit(solution)/shard_map/ppermute | solution.py:111
  292.6 0.0 collective-permute-done.6
  292.6 0.0 collective-permute-done.7
  292.6 2.8 collective-permute-done.8
  295.5 0.9 add_add_fusion
  296.4 0.7 fusion.19
  (9 shorter events, 0.1 us)
Async XLA Ops:
  6.5 40.3 %copy-start.1 = (s32[3,4096]{1,0:T(4,128)S(1)}, s32[3,4096]{1,0:T(4,128)}, u32[]{:S(2)}) copy-start(s32[3,4096]{1,0:T(4,128)} %param.7) | copy-start | bytes 147460
  6.5 40.4 %copy-start = (bf16[384,128]{1,0:T(8,128)(2,1)S(1)}, bf16[384,128]{1,0:T(8,128)(2,1)}, u32[]{:S(2)}) copy-start(bf16[384,128]{1,0:T(8,128)(2,1)} %param.6) | copy-start | bytes 294916
  6.5 48.8 %all-gather.4.cloned.1.call-start = ((), (), s32[]{:S(2)}) async-start(), calls=%async_computation.1 | async-start | bytes 1310720 | tf_op jit(solution)/shard_map/all_gather | solution.py:73
  7.6 14.5 %collective-permute-start = (bf16[512,128]{1,0:T(8,128)(2,1)S(1)}, bf16[512,128]{1,0:T(8,128)(2,1)S(1)}, u32[]{:S(2)}, u32[]{:S(2)}) collective-permute-start(bf16[512,128]{1,0:T(8,128)(2,1)S(1)} %get-tuple-element.23), channel_id=1, source_target_pairs={{0,64},{64,0},{1,65},{65,1},{2,66},{66,2},{3,67},{67,3},{4,68},{68... | collective-permute-start | bytes 393224 | tf_op jit(solution)/shard_map/ppermute | solution.py:71
  22.9 64.2 %all-gather.6.cloned.1.call-start = ((), (), s32[]{:S(2)}) async-start(), calls=%async_computation.2 | async-start | bytes 1310720 | tf_op jit(solution)/shard_map/all_gather | solution.py:73
  22.9 14.8 %collective-permute-start.2 = (bf16[512,128]{1,0:T(8,128)(2,1)S(1)}, bf16[512,128]{1,0:T(8,128)(2,1)S(1)}, u32[]{:S(2)}, u32[]{:S(2)}) collective-permute-start(bf16[512,128]{1,0:T(8,128)(2,1)S(1)} %get-tuple-element.24), channel_id=1, source_target_pairs={{0,64},{64,0},{1,65},{65,1},{2,66},{66,2},{3,67},{67,3},{4,68},{68... | collective-permute-start | bytes 393224 | tf_op jit(solution)/shard_map/ppermute | solution.py:71
  38.5 80.4 %all-gather.8.cloned.1.call-start = ((), (), s32[]{:S(2)}) async-start(), calls=%async_computation.3 | async-start | bytes 1310720 | tf_op jit(solution)/shard_map/all_gather | solution.py:73
  38.6 12.2 %collective-permute-start.4 = (bf16[512,128]{1,0:T(8,128)(2,1)S(1)}, bf16[512,128]{1,0:T(8,128)(2,1)S(1)}, u32[]{:S(2)}, u32[]{:S(2)}) collective-permute-start(bf16[512,128]{1,0:T(8,128)(2,1)S(1)} %get-tuple-element.22), channel_id=1, source_target_pairs={{0,64},{64,0},{1,65},{65,1},{2,66},{66,2},{3,67},{67,3},{4,68},{68... | collective-permute-start | bytes 393224 | tf_op jit(solution)/shard_map/ppermute | solution.py:71
  51.5 228.7 %reduce-scatter.2.cloned.1.call-start = ((), (), s32[]{:S(2)}) async-start(), calls=%async_computation.4 | async-start | bytes 2506752 | tf_op jit(solution)/shard_map/reduce_scatter | solution.py:105
  55.3 66.8 %collective-permute-start.1 = (bf16[4096,128]{1,0:T(8,128)(2,1)}, bf16[4096,128]{1,0:T(8,128)(2,1)S(1)}, u32[]{:S(2)}, u32[]{:S(2)}) collective-permute-start(bf16[4096,128]{1,0:T(8,128)(2,1)} %all-gather.4.cloned.1.call-done), channel_id=1, source_target_pairs={{0,32},{32,0},{1,33},{33,1},{2,34},{34,2},{3,35},{35,3},{4,36},{36... | collective-permute-start | bytes 3145736 | tf_op jit(solution)/shard_map/ppermute | solution.py:75
  87.1 65.1 %collective-permute-start.3 = (bf16[4096,128]{1,0:T(8,128)(2,1)}, bf16[4096,128]{1,0:T(8,128)(2,1)}, u32[]{:S(2)}, u32[]{:S(2)}) collective-permute-start(bf16[4096,128]{1,0:T(8,128)(2,1)} %all-gather.6.cloned.1.call-done), channel_id=1, source_target_pairs={{0,32},{32,0},{1,33},{33,1},{2,34},{34,2},{3,35},{35,3},{4,36},{36... | collective-permute-start | bytes 3145736 | tf_op jit(solution)/shard_map/ppermute | solution.py:75
  119.0 67.8 %collective-permute-start.5 = (bf16[4096,128]{1,0:T(8,128)(2,1)}, bf16[4096,128]{1,0:T(8,128)(2,1)}, u32[]{:S(2)}, u32[]{:S(2)}) collective-permute-start(bf16[4096,128]{1,0:T(8,128)(2,1)} %all-gather.8.cloned.1.call-done), channel_id=1, source_target_pairs={{0,32},{32,0},{1,33},{33,1},{2,34},{34,2},{3,35},{35,3},{4,36},{36... | collective-permute-start | bytes 3145736 | tf_op jit(solution)/shard_map/ppermute | solution.py:75
  281.2 11.4 %collective-permute-start.6 = (f32[136,128]{1,0:T(8,128)S(1)}, f32[136,128]{1,0:T(8,128)S(1)}, u32[]{:S(2)}, u32[]{:S(2)}) collective-permute-start(f32[136,128]{1,0:T(8,128)S(1)} %get-tuple-element.25), channel_id=1, source_target_pairs={{0,1},{1,2},{2,3},{3,0},{4,5},{5,6},{6,7},{7,4},{8,9},{9,10},{10,1... | collective-permute-start | bytes 208904 | tf_op jit(solution)/shard_map/ppermute | solution.py:111
  284.7 7.9 %collective-permute-start.7 = (f32[136,128]{1,0:T(8,128)S(1)}, f32[136,128]{1,0:T(8,128)S(1)}, u32[]{:S(2)}, u32[]{:S(2)}) collective-permute-start(f32[136,128]{1,0:T(8,128)S(1)} %get-tuple-element.27), channel_id=1, source_target_pairs={{0,2},{1,3},{2,0},{3,1},{4,6},{5,7},{6,4},{7,5},{8,10},{9,11},{10,... | collective-permute-start | bytes 208904 | tf_op jit(solution)/shard_map/ppermute | solution.py:111
  289.3 6.2 %collective-permute-start.8 = (f32[136,128]{1,0:T(8,128)S(1)}, f32[136,128]{1,0:T(8,128)S(1)}, u32[]{:S(2)}, u32[]{:S(2)}) collective-permute-start(f32[136,128]{1,0:T(8,128)S(1)} %get-tuple-element.26), channel_id=1, source_target_pairs={{0,3},{1,0},{2,1},{3,2},{4,7},{5,4},{6,5},{7,6},{8,11},{9,8},{10,9... | collective-permute-start | bytes 208904 | tf_op jit(solution)/shard_map/ppermute | solution.py:111
Sparse Core Ops, SparseCore 0:
  23.0 32.2 all-gather.3
  57.4 29.6 all-gather.5
  89.3 29.6 all-gather.7
  233.8 46.3 reduce-scatter.1

commit v4 on v2

--- a/solution.py
+++ b/solution.py
@@ -30,6 +30,18 @@
     return built.astype(jnp.bfloat16)
 
 
+def ring_gather(block, axis, n):
+    assert n == 4
+    fwd = [(i, (i + 1) % n) for i in range(n)]
+    bwd = [(i, (i - 1) % n) for i in range(n)]
+    from_left = lax.ppermute(block, axis, perm=fwd)
+    from_right = lax.ppermute(block, axis, perm=bwd)
+    half = block.shape[0] // 2
+    far_a = lax.ppermute(from_left[:half], axis, perm=fwd)
+    far_b = lax.ppermute(from_right[half:], axis, perm=bwd)
+    return jnp.concatenate([block, from_right, far_a, far_b, from_left], axis=0)
+
+
 def finish(product, first_sums, square_sums, col_totals, sample_count):
     means = first_sums / sample_count
     variance = square_sums / sample_count - means * means
@@ -49,16 +61,18 @@
     sample_count = residuals.shape[0] * n_samp
 
     rows = lax.all_gather(tier_one, "zh", axis=0, tiled=True)
-    rows = lax.all_gather(rows, "x", axis=0, tiled=True)
+    rows = ring_gather(rows, "x", n_x)
     other = lax.ppermute(rows, "c", perm=[(0, 1), (1, 0)])
     rows = jnp.concatenate([rows, other], axis=0)
     my_c = lax.axis_index("c")
+    my_x = lax.axis_index("x")
 
     def position(g):
         f, r = g // local_rows, g % local_rows
         x, zh, c = f // (2 * n_zh), (f // 2) % n_zh, f % 2
         half = (c != my_c).astype(jnp.int32)
-        return ((half * n_x + x) * n_zh + zh) * local_rows + r
+        x_slot = (x - my_x + n_x) % n_x
+        return ((half * n_x + x_slot) * n_zh + zh) * local_rows + r
 
     first = jnp.take(rows, position(pair_list[0]), axis=0)
     second = jnp.take(rows, position(pair_list[1]), axis=0)

time: 214 us -> 206 us (0.963)
  waiting for transfers between devices: 103 us -> 85.2 us
  starting transfers between devices: 12.6 us -> 24.8 us
    all_gather x1 -> x0, waiting for transfers between devices: 50.9 us -> none  [per_device(): rows = lax.all_gather(rows, 'x', axis=0, tiled=True)]
    ppermute x0 -> x4, waiting for transfers between devices: none -> 20.7 us  [the longest x1 14.7 us: ring_gather(): from_left = lax.ppermute(block, axis, perm=fwd)]
    ppermute x0 -> x4, starting transfers between devices: none -> 11.7 us  [the longest x1 3.46 us: ring_gather(): from_right = lax.ppermute(block, axis, perm=bwd)]
    reduce_scatter x1, waiting for transfers between devices: 47.1 us -> 56.1 us  [per_device(): owned = lax.psum_scatter(packed, 'y', scatter_dimension=0, tiled=True)]
    ppermute x1, waiting for transfers between devices: 0.01 us -> 5.4 us  [per_device(): other = lax.ppermute(rows, 'c', perm=[(0, 1), (1, 0)])]
    gather x1, local copies, waits for them, and re-layouts: 20.3 us -> 17.6 us  [per_device(): first = jnp.take(rows, position(pair_list[0]), axis=0)]
    gather x1, local copies, waits for them, and re-layouts: 17.6 us -> 20.3 us  [per_device(): second = jnp.take(rows, position(pair_list[1]), axis=0)]
    unnamed x3 -> x8, local copies, waits for them, and re-layouts: 3.87 us -> 4.59 us
  transfers between devices with their start and end apart: 6 -> 9, of which waited for: 4 -> 6; matrix products, arithmetic and copies ran while one was open for 3% -> 2% of each run, Pallas kernels for 0% -> 0%
where the time goes in v4:
time: 206 us; the launch traced here: 205 us
  waiting for transfers between devices  85.2 us (41%)
  local copies, waits for them, and re-layouts  50.8 us (25%)
  starting transfers between devices  24.8 us (12%)
  blocking collectives  19.2 us (9%)
  between operations  13.6 us (7%)
  other arithmetic  10.6 us (5%)
    reduce_scatter x1, waiting for transfers between devices, per_device(): owned = lax.psum_scatter(packed, 'y', scatter_dimension=0, tiled=True)  56.1 us
    gather x1, local copies, waits for them, and re-layouts, per_device(): second = jnp.take(rows, position(pair_list[1]), axis=0)  20.3 us
    all_gather x1, blocking collectives, per_device(): rows = lax.all_gather(tier_one, 'zh', axis=0, tiled=True)  19.2 us
    gather x1, local copies, waits for them, and re-layouts, per_device(): first = jnp.take(rows, position(pair_list[0]), axis=0)  17.6 us
    ppermute x1, waiting for transfers between devices, ring_gather(): from_left = lax.ppermute(block, axis, perm=fwd)  14.7 us
    ppermute x3, starting transfers between devices, per_device(): lax.ppermute(piece, 'zl', perm=[(i, (i + shift) % n_zl) for i in range(n_...  11.2 us
    reduce_sum x1, other arithmetic, per_device(): square_sums = jnp.sum(widened * widened, axis=1)  8.61 us
    ppermute x1, waiting for transfers between devices, per_device(): other = lax.ppermute(rows, 'c', perm=[(0, 1), (1, 0)])  5.4 us
  transfers between devices with their start and end apart: 9, of which 6 were waited for; matrix products, arithmetic and copies ran while one was open for 2% of the time, Pallas kernels for 0%

profile of v4, /device:TPU:6, one launch (start us, length us, event | category | flops | bytes accessed | tf_op | source)
XLA Modules:
  0.0 205.2 jit_solution(9899649223715799506)
XLA Ops:
  6.5 0.0 reduce-scatter.2.cloned.1.call-start
  6.5 19.2 %all_gather.3 = bf16[1024,384]{1,0:T(8,128)(2,1)S(1)} all-gather(bf16[512,384]{1,0:T(8,128)(2,1)} %param.5), channel_id=1, replica_groups=mesh['x'=4,'zh'=2,'c'=2,'y'=8,'zl'=4] {'zh'}, dimensions={0}, use_global_device_ids=true | all-gather | bytes 1179648 | tf_op jit(solution)/shard_map/all_gather | solution.py:63
  25.7 2.4 %collective-permute-start.1 = (bf16[1024,384]{1,0:T(8,128)(2,1)S(1)}, bf16[1024,384]{1,0:T(8,128)(2,1)S(1)}, u32[]{:S(2)}, u32[]{:S(2)}) collective-permute-start(bf16[1024,384]{1,0:T(8,128)(2,1)S(1)} %all_gather.3), channel_id=1, source_target_pairs={{0,128},{128,256},{256,384},{384,0},{1,129},{129,257},{257,385},{3... | collective-permute-start | bytes 2359304 | tf_op jit(solution)/shard_map/ppermute | solution.py:37
  28.1 3.5 %collective-permute-start = (bf16[1024,384]{1,0:T(8,128)(2,1)S(1)}, bf16[1024,384]{1,0:T(8,128)(2,1)S(1)}, u32[]{:S(2)}, u32[]{:S(2)}) collective-permute-start(bf16[1024,384]{1,0:T(8,128)(2,1)S(1)} %all_gather.3), channel_id=1, source_target_pairs={{0,384},{128,0},{256,128},{384,256},{1,385},{129,1},{257,129},{385... | collective-permute-start | bytes 2359304 | tf_op jit(solution)/shard_map/ppermute | solution.py:38
  31.6 14.7 %collective-permute-done.1 = bf16[1024,384]{1,0:T(8,128)(2,1)S(1)} collective-permute-done((bf16[1024,384]{1,0:T(8,128)(2,1)S(1)}, bf16[1024,384]{1,0:T(8,128)(2,1)S(1)}, u32[]{:S(2)}, u32[]{:S(2)}) %collective-permute-start.1) | collective-permute-done | bytes 786464 | tf_op jit(solution)/shard_map/ppermute | solution.py:37
  46.3 3.4 %collective-permute-start.2 = (bf16[512,384]{1,0:T(8,128)(2,1)S(1)}, bf16[512,384]{1,0:T(8,128)(2,1)S(1)}, u32[]{:S(2)}, u32[]{:S(2)}) collective-permute-start(bf16[512,384]{1,0:T(8,128)(2,1)S(1)} %slice.40), channel_id=1, source_target_pairs={{0,128},{128,256},{256,384},{384,0},{1,129},{129,257},{257,385},{3... | collective-permute-start | bytes 1179656 | tf_op jit(solution)/shard_map/ppermute | solution.py:40
  49.7 0.0 collective-permute-done
  49.8 2.4 %collective-permute-start.3 = (bf16[512,384]{1,0:T(8,128)(2,1)S(1)}, bf16[512,384]{1,0:T(8,128)(2,1)S(1)}, u32[]{:S(2)}, u32[]{:S(2)}) collective-permute-start(bf16[512,384]{1,0:T(8,128)(2,1)S(1)} %slice.41), channel_id=1, source_target_pairs={{0,384},{128,0},{256,128},{384,256},{1,385},{129,1},{257,129},{385... | collective-permute-start | bytes 1179656 | tf_op jit(solution)/shard_map/ppermute | solution.py:41
  52.2 1.3 constant_dynamic-update-slice_fusion.4
  53.5 0.0 copy-start
  53.5 0.0 copy-start.1
  53.5 1.3 constant_dynamic-update-slice_fusion.3
  54.9 2.7 %collective-permute-done.2 = bf16[512,384]{1,0:T(8,128)(2,1)S(1)} collective-permute-done((bf16[512,384]{1,0:T(8,128)(2,1)S(1)}, bf16[512,384]{1,0:T(8,128)(2,1)S(1)}, u32[]{:S(2)}, u32[]{:S(2)}) %collective-permute-start.2) | collective-permute-done | bytes 393248 | tf_op jit(solution)/shard_map/ppermute | solution.py:40
  57.6 1.0 constant_dynamic-update-slice_fusion.2
  58.5 3.2 %collective-permute-done.3 = bf16[512,384]{1,0:T(8,128)(2,1)S(1)} collective-permute-done((bf16[512,384]{1,0:T(8,128)(2,1)S(1)}, bf16[512,384]{1,0:T(8,128)(2,1)S(1)}, u32[]{:S(2)}, u32[]{:S(2)}) %collective-permute-start.3) | collective-permute-done | bytes 393248 | tf_op jit(solution)/shard_map/ppermute | solution.py:41
  61.8 1.0 constant_dynamic-update-slice_fusion.1
  62.8 1.4 constant_dynamic-update-slice_fusion
  64.1 1.9 collective-permute-start.4
  66.1 0.0 copy-done
  66.1 0.1 convert_reduce_fusion.1
  66.1 0.0 copy-done.1
  66.1 0.2 compare_reduce_fusion.2
  66.3 0.1 compare_and_fusion
  66.5 5.4 %collective-permute-done.4 = bf16[4096,384]{1,0:T(8,128)(2,1)S(1)} collective-permute-done((bf16[4096,384]{1,0:T(8,128)(2,1)}, bf16[4096,384]{1,0:T(8,128)(2,1)S(1)}, u32[]{:S(2)}, u32[]{:S(2)}) %collective-permute-start.4) | collective-permute-done | bytes 3145760 | tf_op jit(solution)/shard_map/ppermute | solution.py:65
  71.9 2.0 constant_dynamic-update-slice_fusion.5
  73.9 17.6 %gather_fusion = bf16[4096,384]{1,0:T(8,128)(2,1)S(1)} fusion(bf16[8192,384]{1,0:T(8,128)(2,1)} %constant_dynamic-update-slice_fusion.5, s32[4096]{0:T(1024)S(1)} %broadcast_clamp_fusion.1), kind=kCustom, calls=%fused_computation.clone | custom fusion | bytes 6307840 | tf_op jit(solution)/shard_map/jit(_take)/gather | solution.py:77
  91.5 20.3 %gather_fusion.1 = bf16[4096,384]{1,0:T(8,128)(2,1)} fusion(bf16[8192,384]{1,0:T(8,128)(2,1)} %constant_dynamic-update-slice_fusion.5, s32[4096]{0:T(1024)S(1)} %broadcast_clamp_fusion), kind=kCustom, calls=%fused_computation.1.clone | custom fusion | bytes 6307840 | tf_op jit(solution)/shard_map/jit(_take)/gather | solution.py:78
  111.8 8.6 %fusion = (f32[4096]{0:T(1024)S(1)}, f32[4096]{0:T(1024)S(1)}, bf16[4096,384]{1,0:T(8,128)(2,1)S(1)}) fusion(pred[4096]{0:T(1024)(128)(4,1)S(1)} %get-tuple-element.10, pred[4096]{0:T(1024)(128)(4,1)S(1)} %get-tuple-element.9, bf16[4096,384]{1,0:T(8,128)(2,1)} %gather_fusion.1, pred[4096]{0:T(1024)(128)(4,1)S(1)} %get-tuple-element.14, ...), kind=kLoop, calls=%fused_computation.9 | loop fusion | flops 28303360 | bytes 9490432 | tf_op jit(solution)/shard_map/reduce_sum | solution.py:84
  120.4 1.0 fusion.41
  121.4 3.9 %concatenate.12 = f32[32,136,128]{2,1,0:T(8,128)} concatenate(f32[32,128,128]{2,1,0:T(8,128)S(1)} %bitcast.20, f32[32,1,128]{2,1,0:T(1,128)S(1)} %broadcast_in_dim.41, f32[32,1,128]{2,1,0:T(1,128)S(1)} %bitcast.23, f32[32,1,128]{2,1,0:T(1,128)S(1)} %bitcast.22, f32[32,5,128]{2,1,0:T(8,128)S(1)} %broadcast_in_dim.42), dimensions={1} | concatenate | bytes 4456448 | tf_op jit(solution)/shard_map/concatenate | solution.py:89
  125.3 0.0 reduce-scatter.2.cloned.1.call-update
  125.4 56.1 %reduce-scatter.2.cloned.1.call-done = f32[544,128]{1,0:T(8,128)} async-done(((f32[4352,128]{1,0:T(8,128)}), f32[544,128]{1,0:T(8,128)}) %reduce-scatter.2.cloned.1.call-update) | async-done | bytes 278544 | tf_op jit(solution)/shard_map/reduce_scatter | solution.py:99
  181.4 1.0 constant_dynamic-slice_fusion.2
  182.4 3.4 %collective-permute-start.5 = (f32[136,128]{1,0:T(8,128)S(1)}, f32[136,128]{1,0:T(8,128)S(1)}, u32[]{:S(2)}, u32[]{:S(2)}) collective-permute-start(f32[136,128]{1,0:T(8,128)S(1)} %get-tuple-element.26), channel_id=1, source_target_pairs={{0,1},{1,2},{2,3},{3,0},{4,5},{5,6},{6,7},{7,4},{8,9},{9,10},{10,1... | collective-permute-start | bytes 208904 | tf_op jit(solution)/shard_map/ppermute | solution.py:105
  185.8 4.7 %collective-permute-start.6 = (f32[136,128]{1,0:T(8,128)S(1)}, f32[136,128]{1,0:T(8,128)S(1)}, u32[]{:S(2)}, u32[]{:S(2)}) collective-permute-start(f32[136,128]{1,0:T(8,128)S(1)} %get-tuple-element.28), channel_id=1, source_target_pairs={{0,2},{1,3},{2,0},{3,1},{4,6},{5,7},{6,4},{7,5},{8,10},{9,11},{10,... | collective-permute-start | bytes 208904 | tf_op jit(solution)/shard_map/ppermute | solution.py:105
  190.5 3.1 %collective-permute-start.7 = (f32[136,128]{1,0:T(8,128)S(1)}, f32[136,128]{1,0:T(8,128)S(1)}, u32[]{:S(2)}, u32[]{:S(2)}) collective-permute-start(f32[136,128]{1,0:T(8,128)S(1)} %get-tuple-element.27), channel_id=1, source_target_pairs={{0,3},{1,0},{2,1},{3,2},{4,7},{5,4},{6,5},{7,6},{8,11},{9,8},{10,9... | collective-permute-start | bytes 208904 | tf_op jit(solution)/shard_map/ppermute | solution.py:105
  193.6 0.0 collective-permute-done.5
  193.6 0.0 collective-permute-done.6
  193.6 3.1 %collective-permute-done.7 = f32[136,128]{1,0:T(8,128)S(1)} collective-permute-done((f32[136,128]{1,0:T(8,128)S(1)}, f32[136,128]{1,0:T(8,128)S(1)}, u32[]{:S(2)}, u32[]{:S(2)}) %collective-permute-start.7) | collective-permute-done | bytes 69664 | tf_op jit(solution)/shard_map/ppermute | solution.py:105
  196.7 0.9 add_add_fusion
  197.6 0.7 fusion.7
  (9 shorter events, 0.2 us)
Async XLA Ops:
  6.5 174.9 %reduce-scatter.2.cloned.1.call-start = ((), (), s32[]{:S(2)}) async-start(), calls=%async_computation.1 | async-start | bytes 2506752 | tf_op jit(solution)/shard_map/reduce_scatter | solution.py:99
  25.7 20.6 %collective-permute-start.1 = (bf16[1024,384]{1,0:T(8,128)(2,1)S(1)}, bf16[1024,384]{1,0:T(8,128)(2,1)S(1)}, u32[]{:S(2)}, u32[]{:S(2)}) collective-permute-start(bf16[1024,384]{1,0:T(8,128)(2,1)S(1)} %all_gather.3), channel_id=1, source_target_pairs={{0,128},{128,256},{256,384},{384,0},{1,129},{129,257},{257,385},{3... | collective-permute-start | bytes 2359304 | tf_op jit(solution)/shard_map/ppermute | solution.py:37
  28.1 21.6 %collective-permute-start = (bf16[1024,384]{1,0:T(8,128)(2,1)S(1)}, bf16[1024,384]{1,0:T(8,128)(2,1)S(1)}, u32[]{:S(2)}, u32[]{:S(2)}) collective-permute-start(bf16[1024,384]{1,0:T(8,128)(2,1)S(1)} %all_gather.3), channel_id=1, source_target_pairs={{0,384},{128,0},{256,128},{384,256},{1,385},{129,1},{257,129},{385... | collective-permute-start | bytes 2359304 | tf_op jit(solution)/shard_map/ppermute | solution.py:38
  46.3 11.2 %collective-permute-start.2 = (bf16[512,384]{1,0:T(8,128)(2,1)S(1)}, bf16[512,384]{1,0:T(8,128)(2,1)S(1)}, u32[]{:S(2)}, u32[]{:S(2)}) collective-permute-start(bf16[512,384]{1,0:T(8,128)(2,1)S(1)} %slice.40), channel_id=1, source_target_pairs={{0,128},{128,256},{256,384},{384,0},{1,129},{129,257},{257,385},{3... | collective-permute-start | bytes 1179656 | tf_op jit(solution)/shard_map/ppermute | solution.py:40
  49.8 12.0 %collective-permute-start.3 = (bf16[512,384]{1,0:T(8,128)(2,1)S(1)}, bf16[512,384]{1,0:T(8,128)(2,1)S(1)}, u32[]{:S(2)}, u32[]{:S(2)}) collective-permute-start(bf16[512,384]{1,0:T(8,128)(2,1)S(1)} %slice.41), channel_id=1, source_target_pairs={{0,384},{128,0},{256,128},{384,256},{1,385},{129,1},{257,129},{385... | collective-permute-start | bytes 1179656 | tf_op jit(solution)/shard_map/ppermute | solution.py:41
  53.5 12.5 %copy-start = (bf16[384,128]{1,0:T(8,128)(2,1)S(1)}, bf16[384,128]{1,0:T(8,128)(2,1)}, u32[]{:S(2)}) copy-start(bf16[384,128]{1,0:T(8,128)(2,1)} %param.6) | copy-start | bytes 294916
  53.5 12.6 %copy-start.1 = (s32[3,4096]{1,0:T(4,128)S(1)}, s32[3,4096]{1,0:T(4,128)}, u32[]{:S(2)}) copy-start(s32[3,4096]{1,0:T(4,128)} %param.7) | copy-start | bytes 147460
  64.1 7.8 %collective-permute-start.4 = (bf16[4096,384]{1,0:T(8,128)(2,1)}, bf16[4096,384]{1,0:T(8,128)(2,1)S(1)}, u32[]{:S(2)}, u32[]{:S(2)}) collective-permute-start(bf16[4096,384]{1,0:T(8,128)(2,1)} %get-tuple-element.16), channel_id=1, source_target_pairs={{0,32},{32,0},{1,33},{33,1},{2,34},{34,2},{3,35},{35,3},{4,36},{36... | collective-permute-start | bytes 9437192 | tf_op jit(solution)/shard_map/ppermute | solution.py:65
  182.4 11.2 %collective-permute-start.5 = (f32[136,128]{1,0:T(8,128)S(1)}, f32[136,128]{1,0:T(8,128)S(1)}, u32[]{:S(2)}, u32[]{:S(2)}) collective-permute-start(f32[136,128]{1,0:T(8,128)S(1)} %get-tuple-element.26), channel_id=1, source_target_pairs={{0,1},{1,2},{2,3},{3,0},{4,5},{5,6},{6,7},{7,4},{8,9},{9,10},{10,1... | collective-permute-start | bytes 208904 | tf_op jit(solution)/shard_map/ppermute | solution.py:105
  185.8 7.9 %collective-permute-start.6 = (f32[136,128]{1,0:T(8,128)S(1)}, f32[136,128]{1,0:T(8,128)S(1)}, u32[]{:S(2)}, u32[]{:S(2)}) collective-permute-start(f32[136,128]{1,0:T(8,128)S(1)} %get-tuple-element.28), channel_id=1, source_target_pairs={{0,2},{1,3},{2,0},{3,1},{4,6},{5,7},{6,4},{7,5},{8,10},{9,11},{10,... | collective-permute-start | bytes 208904 | tf_op jit(solution)/shard_map/ppermute | solution.py:105
  190.5 6.2 %collective-permute-start.7 = (f32[136,128]{1,0:T(8,128)S(1)}, f32[136,128]{1,0:T(8,128)S(1)}, u32[]{:S(2)}, u32[]{:S(2)}) collective-permute-start(f32[136,128]{1,0:T(8,128)S(1)} %get-tuple-element.27), channel_id=1, source_target_pairs={{0,3},{1,0},{2,1},{3,2},{4,7},{5,4},{6,5},{7,6},{8,11},{9,8},{10,9... | collective-permute-start | bytes 208904 | tf_op jit(solution)/shard_map/ppermute | solution.py:105
Sparse Core Ops, SparseCore 0:
  125.4 55.9 reduce-scatter.1

commit v5 on v4

--- a/solution.py
+++ b/solution.py
@@ -74,29 +74,48 @@
         x_slot = (x - my_x + n_x) % n_x
         return ((half * n_x + x_slot) * n_zh + zh) * local_rows + r
 
-    first = jnp.take(rows, position(pair_list[0]), axis=0)
-    second = jnp.take(rows, position(pair_list[1]), axis=0)
-    built = combine_rows(first, second, pair_list[2][:, None])
-
-    product = jnp.dot(built, residuals, preferred_element_type=jnp.float32)
-    widened = built.astype(jnp.float32)
-    first_sums = jnp.sum(widened, axis=1)
-    square_sums = jnp.sum(widened * widened, axis=1)
+    first_pos = position(pair_list[0])
+    second_pos = position(pair_list[1])
+    operator_id = pair_list[2]
     col_part = jnp.sum(residuals.astype(jnp.float32), axis=0)
 
     blocks = local_pairs // width_k
     block_rows = width_k + EXTRA_ROWS
-    packed = jnp.concatenate(
-        [
-            product.reshape(blocks, width_k, width_k),
-            jnp.broadcast_to(col_part[None, None, :], (blocks, 1, width_k)),
-            first_sums.reshape(blocks, 1, width_k),
-            square_sums.reshape(blocks, 1, width_k),
-            jnp.zeros((blocks, EXTRA_ROWS - 3, width_k), jnp.float32),
-        ],
-        axis=1,
-    ).reshape(blocks * block_rows, width_k)
-    owned = lax.psum_scatter(packed, "y", scatter_dimension=0, tiled=True)
+    per_y = local_pairs // n_y
+    blocks_per_y = blocks // n_y
+
+    def y_block_terms(dest):
+        def pick(v):
+            return lax.dynamic_slice_in_dim(v, dest * per_y, per_y, 0)
+        first = jnp.take(rows, pick(first_pos), axis=0)
+        second = jnp.take(rows, pick(second_pos), axis=0)
+        built = combine_rows(first, second, pick(operator_id)[:, None])
+        product = jnp.dot(built, residuals, preferred_element_type=jnp.float32)
+        widened = built.astype(jnp.float32)
+        first_sums = jnp.sum(widened, axis=1)
+        square_sums = jnp.sum(widened * widened, axis=1)
+        return jnp.concatenate(
+            [
+                product.reshape(blocks_per_y, width_k, width_k),
+                jnp.broadcast_to(col_part[None, None, :], (blocks_per_y, 1, width_k)),
+                first_sums.reshape(blocks_per_y, 1, width_k),
+                square_sums.reshape(blocks_per_y, 1, width_k),
+                jnp.zeros((blocks_per_y, EXTRA_ROWS - 3, width_k), jnp.float32),
+            ],
+            axis=1,
+        ).reshape(blocks_per_y * block_rows, width_k)
+
+    my_y = lax.axis_index("y")
+    received = []
+    for shift in range(1, n_y):
+        dest = (my_y + shift) % n_y
+        received.append(lax.ppermute(
+            y_block_terms(dest), "y", perm=[(i, (i + shift) % n_y) for i in range(n_y)]
+        ))
+    owned = y_block_terms(my_y)
+    for piece in received:
+        owned = owned + piece
+
     my_zl = lax.axis_index("zl")
     total = lax.dynamic_slice_in_dim(owned, my_zl * block_rows, block_rows, 0)
     for shift in range(1, n_zl):

time: 206 us -> 240 us (1.17)
  local copies, waits for them, and re-layouts: 50.8 us -> 100 us
  waiting for transfers between devices: 85.2 us -> 43.7 us
  starting transfers between devices: 24.8 us -> 63.4 us
  between operations: 13.6 us -> 0.8 us
    reduce_scatter x1 -> x0, waiting for transfers between devices: 56.1 us -> none  [per_device(): owned = lax.psum_scatter(packed, 'y', scatter_dimension=0, tiled=True)]
    gather x2 -> x16, local copies, waits for them, and re-layouts: 37.9 us -> 86.4 us  [the longest x8 43.2 us: y_block_terms(): first = jnp.take(rows, pick(first_pos), axis=0)]
    ppermute x0 -> x7, starting transfers between devices: none -> 29.9 us  [per_device(): lax.ppermute(y_block_terms(dest), 'y', perm=[(i, (i + shift) % n_y) for i...]
    ppermute x0 -> x7, waiting for transfers between devices: none -> 13.5 us  [per_device(): lax.ppermute(y_block_terms(dest), 'y', perm=[(i, (i + shift) % n_y) for i...]
    ppermute x3, starting transfers between devices: 11.2 us -> 20 us  [per_device(): lax.ppermute(piece, 'zl', perm=[(i, (i + shift) % n_zl) for i in range(n_...]
    concatenate x1 -> x8, local copies, waits for them, and re-layouts: 3.86 us -> 6.92 us  [y_block_terms(): jnp.concatenate([product.reshape(blocks_per_y, width_k, width_k), jnp.bro...]
    reduce_sum x1 -> x8, other arithmetic: 8.61 us -> 7.54 us  [y_block_terms(): square_sums = jnp.sum(widened * widened, axis=1)]
  transfers between devices with their start and end apart: 9 -> 15, of which waited for: 6 -> 7; matrix products, arithmetic and copies ran while one was open for 2% -> 40% of each run, Pallas kernels for 0% -> 0%
where the time goes in v5:
time: 240 us; the launch traced here: 239 us
  local copies, waits for them, and re-layouts  100 us (42%)
  starting transfers between devices  63.4 us (26%)
  waiting for transfers between devices  43.7 us (18%)
  blocking collectives  19.3 us (8%)
  other arithmetic  9.03 us (4%)
    gather x8, local copies, waits for them, and re-layouts, y_block_terms(): first = jnp.take(rows, pick(first_pos), axis=0)  43.2 us
    gather x8, local copies, waits for them, and re-layouts, y_block_terms(): second = jnp.take(rows, pick(second_pos), axis=0)  43.2 us
    ppermute x7, starting transfers between devices, per_device(): lax.ppermute(y_block_terms(dest), 'y', perm=[(i, (i + shift) % n_y) for i...  29.9 us
    ppermute x3, starting transfers between devices, per_device(): lax.ppermute(piece, 'zl', perm=[(i, (i + shift) % n_zl) for i in range(n_...  20 us
    all_gather x1, blocking collectives, per_device(): rows = lax.all_gather(tier_one, 'zh', axis=0, tiled=True)  19.3 us
    ppermute x1, waiting for transfers between devices, ring_gather(): from_left = lax.ppermute(block, axis, perm=fwd)  14.7 us
    ppermute x7, waiting for transfers between devices, per_device(): lax.ppermute(y_block_terms(dest), 'y', perm=[(i, (i + shift) % n_y) for i...  13.5 us
    reduce_sum x8, other arithmetic, y_block_terms(): square_sums = jnp.sum(widened * widened, axis=1)  7.54 us
  transfers between devices with their start and end apart: 15, of which 7 were waited for; matrix products, arithmetic and copies ran while one was open for 40% of the time, Pallas kernels for 0%

profile of v5, /device:TPU:6, one launch (start us, length us, event | category | flops | bytes accessed | tf_op | source)
XLA Modules:
  0.0 238.7 jit_solution(10835804263231755834)
XLA Ops:
  0.0 19.3 %all_gather.3 = bf16[1024,384]{1,0:T(8,128)(2,1)S(1)} all-gather(bf16[512,384]{1,0:T(8,128)(2,1)} %param.5), channel_id=1, replica_groups=mesh['x'=4,'zh'=2,'c'=2,'y'=8,'zl'=4] {'zh'}, dimensions={0}, use_global_device_ids=true | all-gather | bytes 1179648 | tf_op jit(solution)/shard_map/all_gather | solution.py:63
  19.3 2.4 collective-permute-start.1
  21.7 3.5 %collective-permute-start = (bf16[1024,384]{1,0:T(8,128)(2,1)S(1)}, bf16[1024,384]{1,0:T(8,128)(2,1)S(1)}, u32[]{:S(2)}, u32[]{:S(2)}) collective-permute-start(bf16[1024,384]{1,0:T(8,128)(2,1)S(1)} %all_gather.3), channel_id=1, source_target_pairs={{0,384},{128,0},{256,128},{384,256},{1,385},{129,1},{257,129},{385... | collective-permute-start | bytes 2359304 | tf_op jit(solution)/shard_map/ppermute | solution.py:38
  25.2 14.7 %collective-permute-done.1 = bf16[1024,384]{1,0:T(8,128)(2,1)S(1)} collective-permute-done((bf16[1024,384]{1,0:T(8,128)(2,1)S(1)}, bf16[1024,384]{1,0:T(8,128)(2,1)S(1)}, u32[]{:S(2)}, u32[]{:S(2)}) %collective-permute-start.1) | collective-permute-done | bytes 786464 | tf_op jit(solution)/shard_map/ppermute | solution.py:37
  39.9 3.4 %collective-permute-start.2 = (bf16[512,384]{1,0:T(8,128)(2,1)S(1)}, bf16[512,384]{1,0:T(8,128)(2,1)S(1)}, u32[]{:S(2)}, u32[]{:S(2)}) collective-permute-start(bf16[512,384]{1,0:T(8,128)(2,1)S(1)} %slice.68), channel_id=1, source_target_pairs={{0,128},{128,256},{256,384},{384,0},{1,129},{129,257},{257,385},{3... | collective-permute-start | bytes 1179656 | tf_op jit(solution)/shard_map/ppermute | solution.py:40
  43.6 2.4 %collective-permute-start.3 = (bf16[512,384]{1,0:T(8,128)(2,1)S(1)}, bf16[512,384]{1,0:T(8,128)(2,1)S(1)}, u32[]{:S(2)}, u32[]{:S(2)}) collective-permute-start(bf16[512,384]{1,0:T(8,128)(2,1)S(1)} %slice.69), channel_id=1, source_target_pairs={{0,384},{128,0},{256,128},{384,256},{1,385},{129,1},{257,129},{385... | collective-permute-start | bytes 1179656 | tf_op jit(solution)/shard_map/ppermute | solution.py:41
  46.0 1.0 constant_dynamic-update-slice_fusion.4
  47.0 1.0 constant_dynamic-update-slice_fusion.3
  48.0 3.1 %collective-permute-done.2 = bf16[512,384]{1,0:T(8,128)(2,1)S(1)} collective-permute-done((bf16[512,384]{1,0:T(8,128)(2,1)S(1)}, bf16[512,384]{1,0:T(8,128)(2,1)S(1)}, u32[]{:S(2)}, u32[]{:S(2)}) %collective-permute-start.2) | collective-permute-done | bytes 393248 | tf_op jit(solution)/shard_map/ppermute | solution.py:40
  51.2 0.8 constant_dynamic-update-slice_fusion.2
  52.0 3.5 %collective-permute-done.3 = bf16[512,384]{1,0:T(8,128)(2,1)S(1)} collective-permute-done((bf16[512,384]{1,0:T(8,128)(2,1)S(1)}, bf16[512,384]{1,0:T(8,128)(2,1)S(1)}, u32[]{:S(2)}, u32[]{:S(2)}) %collective-permute-start.3) | collective-permute-done | bytes 393248 | tf_op jit(solution)/shard_map/ppermute | solution.py:41
  55.5 0.9 constant_dynamic-update-slice_fusion.1
  56.4 1.0 constant_dynamic-update-slice_fusion
  57.4 1.9 collective-permute-start.4
  60.2 4.8 %collective-permute-done.4 = bf16[4096,384]{1,0:T(8,128)(2,1)S(1)} collective-permute-done((bf16[4096,384]{1,0:T(8,128)(2,1)S(1)}, bf16[4096,384]{1,0:T(8,128)(2,1)S(1)}, u32[]{:S(2)}, u32[]{:S(2)}) %collective-permute-start.4) | collective-permute-done | bytes 3145760 | tf_op jit(solution)/shard_map/ppermute | solution.py:65
  65.0 2.0 constant_dynamic-update-slice_fusion.5
  67.0 5.4 %gather_fusion.15 = bf16[512,384]{1,0:T(8,128)(2,1)S(1)} fusion(bf16[8192,384]{1,0:T(8,128)(2,1)} %constant_dynamic-update-slice_fusion.5, s32[1024]{0:T(1024)S(1)} %pad_clamp_fusion), kind=kCustom, calls=%fused_computation.15.clone | custom fusion | bytes 788480 | tf_op jit(solution)/shard_map/jit(_take)/gather | solution.py:91
  72.4 5.4 %gather_fusion.14 = bf16[512,384]{1,0:T(8,128)(2,1)S(1)} fusion(bf16[8192,384]{1,0:T(8,128)(2,1)} %constant_dynamic-update-slice_fusion.5, s32[1024]{0:T(1024)S(1)} %pad_clamp_fusion.1), kind=kCustom, calls=%fused_computation.14.clone | custom fusion | bytes 788480 | tf_op jit(solution)/shard_map/jit(_take)/gather | solution.py:90
  77.8 0.9 fusion.7
  78.8 0.3 fusion.103
  79.1 5.7 %collective-permute-start.11 = (f32[544,128]{1,0:T(8,128)S(1)}, f32[544,128]{1,0:T(8,128)S(1)}, u32[]{:S(2)}, u32[]{:S(2)}) collective-permute-start(f32[544,128]{1,0:T(8,128)S(1)} %bitcast.83), channel_id=1, source_target_pairs={{0,28},{4,0},{8,4},{12,8},{16,12},{20,16},{24,20},{28,24},{1,29},{... | collective-permute-start | bytes 835592 | tf_op jit(solution)/shard_map/ppermute | solution.py:112
  84.8 5.4 %gather_fusion.13 = bf16[512,384]{1,0:T(8,128)(2,1)S(1)} fusion(bf16[8192,384]{1,0:T(8,128)(2,1)} %constant_dynamic-update-slice_fusion.5, s32[1024]{0:T(1024)S(1)} %pad_clamp_fusion.2), kind=kCustom, calls=%fused_computation.13.clone | custom fusion | bytes 788480 | tf_op jit(solution)/shard_map/jit(_take)/gather | solution.py:91
  90.3 5.4 %gather_fusion.12 = bf16[512,384]{1,0:T(8,128)(2,1)S(1)} fusion(bf16[8192,384]{1,0:T(8,128)(2,1)} %constant_dynamic-update-slice_fusion.5, s32[1024]{0:T(1024)S(1)} %pad_clamp_fusion.3), kind=kCustom, calls=%fused_computation.12.clone | custom fusion | bytes 788480 | tf_op jit(solution)/shard_map/jit(_take)/gather | solution.py:90
  95.7 0.9 fusion.6
  96.9 1.4 concatenate.39
  98.2 4.2 %collective-permute-start.10 = (f32[544,128]{1,0:T(8,128)}, f32[544,128]{1,0:T(8,128)S(1)}, u32[]{:S(2)}, u32[]{:S(2)}) collective-permute-start(f32[544,128]{1,0:T(8,128)} %bitcast.29), channel_id=1, source_target_pairs={{0,24},{4,28},{8,0},{12,4},{16,8},{20,12},{24,16},{28,20},{1,25},{... | collective-permute-start | bytes 835592 | tf_op jit(solution)/shard_map/ppermute | solution.py:112
  102.5 5.4 %gather_fusion.11 = bf16[512,384]{1,0:T(8,128)(2,1)S(1)} fusion(bf16[8192,384]{1,0:T(8,128)(2,1)} %constant_dynamic-update-slice_fusion.5, s32[1024]{0:T(1024)S(1)} %pad_clamp_fusion.4), kind=kCustom, calls=%fused_computation.11.clone | custom fusion | bytes 788480 | tf_op jit(solution)/shard_map/jit(_take)/gather | solution.py:91
  107.9 5.4 %gather_fusion.10 = bf16[512,384]{1,0:T(8,128)(2,1)S(1)} fusion(bf16[8192,384]{1,0:T(8,128)(2,1)} %constant_dynamic-update-slice_fusion.5, s32[1024]{0:T(1024)S(1)} %pad_clamp_fusion.5), kind=kCustom, calls=%fused_computation.10.clone | custom fusion | bytes 788480 | tf_op jit(solution)/shard_map/jit(_take)/gather | solution.py:90
  113.3 0.9 fusion.5
  114.5 1.3 concatenate.38
  115.9 3.0 %collective-permute-start.9 = (f32[544,128]{1,0:T(8,128)}, f32[544,128]{1,0:T(8,128)S(1)}, u32[]{:S(2)}, u32[]{:S(2)}) collective-permute-start(f32[544,128]{1,0:T(8,128)} %bitcast.25), channel_id=1, source_target_pairs={{0,20},{4,24},{8,28},{12,0},{16,4},{20,8},{24,12},{28,16},{1,21},{... | collective-permute-start | bytes 835592 | tf_op jit(solution)/shard_map/ppermute | solution.py:112
  118.9 5.4 %gather_fusion.9 = bf16[512,384]{1,0:T(8,128)(2,1)S(1)} fusion(bf16[8192,384]{1,0:T(8,128)(2,1)} %constant_dynamic-update-slice_fusion.5, s32[1024]{0:T(1024)S(1)} %pad_clamp_fusion.6), kind=kCustom, calls=%fused_computation.9.clone | custom fusion | bytes 788480 | tf_op jit(solution)/shard_map/jit(_take)/gather | solution.py:91
  124.3 5.4 %gather_fusion.8 = bf16[512,384]{1,0:T(8,128)(2,1)S(1)} fusion(bf16[8192,384]{1,0:T(8,128)(2,1)} %constant_dynamic-update-slice_fusion.5, s32[1024]{0:T(1024)S(1)} %pad_clamp_fusion.7), kind=kCustom, calls=%fused_computation.8.clone | custom fusion | bytes 788480 | tf_op jit(solution)/shard_map/jit(_take)/gather | solution.py:90
  129.7 0.9 fusion.4
  130.7 0.3 fusion.100
  130.9 1.4 concatenate.37
  132.3 5.9 %collective-permute-start.8 = (f32[544,128]{1,0:T(8,128)}, f32[544,128]{1,0:T(8,128)S(1)}, u32[]{:S(2)}, u32[]{:S(2)}) collective-permute-start(f32[544,128]{1,0:T(8,128)} %bitcast.21), channel_id=1, source_target_pairs={{0,16},{4,20},{8,24},{12,28},{16,0},{20,4},{24,8},{28,12},{1,17},{... | collective-permute-start | bytes 835592 | tf_op jit(solution)/shard_map/ppermute | solution.py:112
  138.2 5.4 %gather_fusion.7 = bf16[512,384]{1,0:T(8,128)(2,1)S(1)} fusion(bf16[8192,384]{1,0:T(8,128)(2,1)} %constant_dynamic-update-slice_fusion.5, s32[1024]{0:T(1024)S(1)} %pad_clamp_fusion.8), kind=kCustom, calls=%fused_computation.7.clone | custom fusion | bytes 788480 | tf_op jit(solution)/shard_map/jit(_take)/gather | solution.py:91
  143.6 5.4 %gather_fusion.6 = bf16[512,384]{1,0:T(8,128)(2,1)S(1)} fusion(bf16[8192,384]{1,0:T(8,128)(2,1)} %constant_dynamic-update-slice_fusion.5, s32[1024]{0:T(1024)S(1)} %pad_clamp_fusion.9), kind=kCustom, calls=%fused_computation.6.clone | custom fusion | bytes 788480 | tf_op jit(solution)/shard_map/jit(_take)/gather | solution.py:90
  149.0 0.9 fusion.3
  150.0 0.3 fusion.99
  150.3 1.4 concatenate.36
  151.6 2.1 collective-permute-start.7
  153.8 5.4 %gather_fusion.5 = bf16[512,384]{1,0:T(8,128)(2,1)S(1)} fusion(bf16[8192,384]{1,0:T(8,128)(2,1)} %constant_dynamic-update-slice_fusion.5, s32[1024]{0:T(1024)S(1)} %pad_clamp_fusion.10), kind=kCustom, calls=%fused_computation.5.clone | custom fusion | bytes 788480 | tf_op jit(solution)/shard_map/jit(_take)/gather | solution.py:91
  159.2 5.4 %gather_fusion.4 = bf16[512,384]{1,0:T(8,128)(2,1)S(1)} fusion(bf16[8192,384]{1,0:T(8,128)(2,1)} %constant_dynamic-update-slice_fusion.5, s32[1024]{0:T(1024)S(1)} %pad_clamp_fusion.11), kind=kCustom, calls=%fused_computation.4.clone | custom fusion | bytes 788480 | tf_op jit(solution)/shard_map/jit(_take)/gather | solution.py:90
  164.6 5.4 %gather_fusion.3 = bf16[512,384]{1,0:T(8,128)(2,1)S(1)} fusion(bf16[8192,384]{1,0:T(8,128)(2,1)} %constant_dynamic-update-slice_fusion.5, s32[1024]{0:T(1024)S(1)} %pad_clamp_fusion.12), kind=kCustom, calls=%fused_computation.3.clone | custom fusion | bytes 788480 | tf_op jit(solution)/shard_map/jit(_take)/gather | solution.py:91
  170.0 5.4 %gather_fusion.2 = bf16[512,384]{1,0:T(8,128)(2,1)S(1)} fusion(bf16[8192,384]{1,0:T(8,128)(2,1)} %constant_dynamic-update-slice_fusion.5, s32[1024]{0:T(1024)S(1)} %pad_clamp_fusion.13), kind=kCustom, calls=%fused_computation.2.clone | custom fusion | bytes 788480 | tf_op jit(solution)/shard_map/jit(_take)/gather | solution.py:90
  175.4 0.9 fusion.2
  176.4 0.9 fusion.1
  177.3 0.3 fusion.98
  177.6 5.4 %gather_fusion.1 = bf16[512,384]{1,0:T(8,128)(2,1)S(1)} fusion(bf16[8192,384]{1,0:T(8,128)(2,1)} %constant_dynamic-update-slice_fusion.5, s32[1024]{0:T(1024)S(1)} %pad_clamp_fusion.14), kind=kCustom, calls=%fused_computation.1.clone | custom fusion | bytes 788480 | tf_op jit(solution)/shard_map/jit(_take)/gather | solution.py:91
  183.0 5.4 %gather_fusion = bf16[512,384]{1,0:T(8,128)(2,1)S(1)} fusion(bf16[8192,384]{1,0:T(8,128)(2,1)} %constant_dynamic-update-slice_fusion.5, s32[1024]{0:T(1024)S(1)} %pad_clamp_fusion.15), kind=kCustom, calls=%fused_computation.clone | custom fusion | bytes 788480 | tf_op jit(solution)/shard_map/jit(_take)/gather | solution.py:90
  188.7 1.4 concatenate.34
  190.1 5.4 %collective-permute-start.6 = (f32[544,128]{1,0:T(8,128)S(1)}, f32[544,128]{1,0:T(8,128)S(1)}, u32[]{:S(2)}, u32[]{:S(2)}) collective-permute-start(f32[544,128]{1,0:T(8,128)S(1)} %bitcast.84), channel_id=1, source_target_pairs={{0,8},{4,12},{8,16},{12,20},{16,24},{20,28},{24,0},{28,4},{1,9},{5... | collective-permute-start | bytes 835592 | tf_op jit(solution)/shard_map/ppermute | solution.py:112
  195.5 3.5 %collective-permute-start.5 = (f32[544,128]{1,0:T(8,128)}, f32[544,128]{1,0:T(8,128)S(1)}, u32[]{:S(2)}, u32[]{:S(2)}) collective-permute-start(f32[544,128]{1,0:T(8,128)} %bitcast.85), channel_id=1, source_target_pairs={{0,4},{4,8},{8,12},{12,16},{16,20},{20,24},{24,28},{28,0},{1,5},{5... | collective-permute-start | bytes 835592 | tf_op jit(solution)/shard_map/ppermute | solution.py:112
  199.0 0.9 fusion
  199.9 0.3 fusion.96
  200.3 8.2 %collective-permute-done.6 = f32[544,128]{1,0:T(8,128)S(1)} collective-permute-done((f32[544,128]{1,0:T(8,128)S(1)}, f32[544,128]{1,0:T(8,128)S(1)}, u32[]{:S(2)}, u32[]{:S(2)}) %collective-permute-start.6) | collective-permute-done | bytes 278560 | tf_op jit(solution)/shard_map/ppermute | solution.py:112
  208.5 5.2 %collective-permute-done.5 = f32[544,128]{1,0:T(8,128)S(1)} collective-permute-done((f32[544,128]{1,0:T(8,128)}, f32[544,128]{1,0:T(8,128)S(1)}, u32[]{:S(2)}, u32[]{:S(2)}) %collective-permute-start.5) | collective-permute-done | bytes 278560 | tf_op jit(solution)/shard_map/ppermute | solution.py:112
  213.8 8.9 %collective-permute-start.14 = (f32[136,128]{1,0:T(8,128)S(1)}, f32[136,128]{1,0:T(8,128)S(1)}, u32[]{:S(2)}, u32[]{:S(2)}) collective-permute-start(f32[136,128]{1,0:T(8,128)S(1)} %get-tuple-element.97), channel_id=1, source_target_pairs={{0,3},{1,0},{2,1},{3,2},{4,7},{5,4},{6,5},{7,6},{8,11},{9,8},{10,9... | collective-permute-start | bytes 208904 | tf_op jit(solution)/shard_map/ppermute | solution.py:124
  222.8 7.1 %collective-permute-start.13 = (f32[136,128]{1,0:T(8,128)S(1)}, f32[136,128]{1,0:T(8,128)S(1)}, u32[]{:S(2)}, u32[]{:S(2)}) collective-permute-start(f32[136,128]{1,0:T(8,128)S(1)} %get-tuple-element.98), channel_id=1, source_target_pairs={{0,2},{1,3},{2,0},{3,1},{4,6},{5,7},{6,4},{7,5},{8,10},{9,11},{10,... | collective-permute-start | bytes 208904 | tf_op jit(solution)/shard_map/ppermute | solution.py:124
  229.9 3.9 %collective-permute-start.12 = (f32[136,128]{1,0:T(8,128)S(1)}, f32[136,128]{1,0:T(8,128)S(1)}, u32[]{:S(2)}, u32[]{:S(2)}) collective-permute-start(f32[136,128]{1,0:T(8,128)S(1)} %get-tuple-element.96), channel_id=1, source_target_pairs={{0,1},{1,2},{2,3},{3,0},{4,5},{5,6},{6,7},{7,4},{8,9},{9,10},{10,1... | collective-permute-start | bytes 208904 | tf_op jit(solution)/shard_map/ppermute | solution.py:124
  233.8 4.0 %collective-permute-done.12 = f32[136,128]{1,0:T(8,128)S(1)} collective-permute-done((f32[136,128]{1,0:T(8,128)S(1)}, f32[136,128]{1,0:T(8,128)S(1)}, u32[]{:S(2)}, u32[]{:S(2)}) %collective-permute-start.12) | collective-permute-done | bytes 69664 | tf_op jit(solution)/shard_map/ppermute | solution.py:124
  237.9 0.7 fusion.55
  (49 shorter events, 1.9 us)
Async XLA Ops:
  0.0 59.3 %copy-start.1 = (s32[3,4096]{1,0:T(4,128)S(1)}, s32[3,4096]{1,0:T(4,128)}, u32[]{:S(2)}) copy-start(s32[3,4096]{1,0:T(4,128)} %param.7) | copy-start | bytes 147460
  0.0 60.1 %copy-start = (bf16[384,128]{1,0:T(8,128)(2,1)S(1)}, bf16[384,128]{1,0:T(8,128)(2,1)}, u32[]{:S(2)}) copy-start(bf16[384,128]{1,0:T(8,128)(2,1)} %param.6) | copy-start | bytes 294916
  19.3 20.6 %collective-permute-start.1 = (bf16[1024,384]{1,0:T(8,128)(2,1)S(1)}, bf16[1024,384]{1,0:T(8,128)(2,1)S(1)}, u32[]{:S(2)}, u32[]{:S(2)}) collective-permute-start(bf16[1024,384]{1,0:T(8,128)(2,1)S(1)} %all_gather.3), channel_id=1, source_target_pairs={{0,128},{128,256},{256,384},{384,0},{1,129},{129,257},{257,385},{3... | collective-permute-start | bytes 2359304 | tf_op jit(solution)/shard_map/ppermute | solution.py:37
  21.7 21.8 %collective-permute-start = (bf16[1024,384]{1,0:T(8,128)(2,1)S(1)}, bf16[1024,384]{1,0:T(8,128)(2,1)S(1)}, u32[]{:S(2)}, u32[]{:S(2)}) collective-permute-start(bf16[1024,384]{1,0:T(8,128)(2,1)S(1)} %all_gather.3), channel_id=1, source_target_pairs={{0,384},{128,0},{256,128},{384,256},{1,385},{129,1},{257,129},{385... | collective-permute-start | bytes 2359304 | tf_op jit(solution)/shard_map/ppermute | solution.py:38
  39.9 11.2 %collective-permute-start.2 = (bf16[512,384]{1,0:T(8,128)(2,1)S(1)}, bf16[512,384]{1,0:T(8,128)(2,1)S(1)}, u32[]{:S(2)}, u32[]{:S(2)}) collective-permute-start(bf16[512,384]{1,0:T(8,128)(2,1)S(1)} %slice.68), channel_id=1, source_target_pairs={{0,128},{128,256},{256,384},{384,0},{1,129},{129,257},{257,385},{3... | collective-permute-start | bytes 1179656 | tf_op jit(solution)/shard_map/ppermute | solution.py:40
  43.6 12.0 %collective-permute-start.3 = (bf16[512,384]{1,0:T(8,128)(2,1)S(1)}, bf16[512,384]{1,0:T(8,128)(2,1)S(1)}, u32[]{:S(2)}, u32[]{:S(2)}) collective-permute-start(bf16[512,384]{1,0:T(8,128)(2,1)S(1)} %slice.69), channel_id=1, source_target_pairs={{0,384},{128,0},{256,128},{384,256},{1,385},{129,1},{257,129},{385... | collective-permute-start | bytes 1179656 | tf_op jit(solution)/shard_map/ppermute | solution.py:41
  57.4 7.5 %collective-permute-start.4 = (bf16[4096,384]{1,0:T(8,128)(2,1)S(1)}, bf16[4096,384]{1,0:T(8,128)(2,1)S(1)}, u32[]{:S(2)}, u32[]{:S(2)}) collective-permute-start(bf16[4096,384]{1,0:T(8,128)(2,1)S(1)} %get-tuple-element.86), channel_id=1, source_target_pairs={{0,32},{32,0},{1,33},{33,1},{2,34},{34,2},{3,35},{35,3},{4,36},{36... | collective-permute-start | bytes 9437192 | tf_op jit(solution)/shard_map/ppermute | solution.py:65
  79.1 111.0 %collective-permute-start.11 = (f32[544,128]{1,0:T(8,128)S(1)}, f32[544,128]{1,0:T(8,128)S(1)}, u32[]{:S(2)}, u32[]{:S(2)}) collective-permute-start(f32[544,128]{1,0:T(8,128)S(1)} %bitcast.83), channel_id=1, source_target_pairs={{0,28},{4,0},{8,4},{12,8},{16,12},{20,16},{24,20},{28,24},{1,29},{... | collective-permute-start | bytes 835592 | tf_op jit(solution)/shard_map/ppermute | solution.py:112
  98.2 97.2 %collective-permute-start.10 = (f32[544,128]{1,0:T(8,128)}, f32[544,128]{1,0:T(8,128)S(1)}, u32[]{:S(2)}, u32[]{:S(2)}) collective-permute-start(f32[544,128]{1,0:T(8,128)} %bitcast.29), channel_id=1, source_target_pairs={{0,24},{4,28},{8,0},{12,4},{16,8},{20,12},{24,16},{28,20},{1,25},{... | collective-permute-start | bytes 835592 | tf_op jit(solution)/shard_map/ppermute | solution.py:112
  115.9 84.4 %collective-permute-start.9 = (f32[544,128]{1,0:T(8,128)}, f32[544,128]{1,0:T(8,128)S(1)}, u32[]{:S(2)}, u32[]{:S(2)}) collective-permute-start(f32[544,128]{1,0:T(8,128)} %bitcast.25), channel_id=1, source_target_pairs={{0,20},{4,24},{8,28},{12,0},{16,4},{20,8},{24,12},{28,16},{1,21},{... | collective-permute-start | bytes 835592 | tf_op jit(solution)/shard_map/ppermute | solution.py:112
  132.3 68.0 %collective-permute-start.8 = (f32[544,128]{1,0:T(8,128)}, f32[544,128]{1,0:T(8,128)S(1)}, u32[]{:S(2)}, u32[]{:S(2)}) collective-permute-start(f32[544,128]{1,0:T(8,128)} %bitcast.21), channel_id=1, source_target_pairs={{0,16},{4,20},{8,24},{12,28},{16,0},{20,4},{24,8},{28,12},{1,17},{... | collective-permute-start | bytes 835592 | tf_op jit(solution)/shard_map/ppermute | solution.py:112
  151.6 48.6 %collective-permute-start.7 = (f32[544,128]{1,0:T(8,128)}, f32[544,128]{1,0:T(8,128)S(1)}, u32[]{:S(2)}, u32[]{:S(2)}) collective-permute-start(f32[544,128]{1,0:T(8,128)} %bitcast.17), channel_id=1, source_target_pairs={{0,12},{4,16},{8,20},{12,24},{16,28},{20,0},{24,4},{28,8},{1,13},{... | collective-permute-start | bytes 835592 | tf_op jit(solution)/shard_map/ppermute | solution.py:112
  190.1 18.4 %collective-permute-start.6 = (f32[544,128]{1,0:T(8,128)S(1)}, f32[544,128]{1,0:T(8,128)S(1)}, u32[]{:S(2)}, u32[]{:S(2)}) collective-permute-start(f32[544,128]{1,0:T(8,128)S(1)} %bitcast.84), channel_id=1, source_target_pairs={{0,8},{4,12},{8,16},{12,20},{16,24},{20,28},{24,0},{28,4},{1,9},{5... | collective-permute-start | bytes 835592 | tf_op jit(solution)/shard_map/ppermute | solution.py:112
  195.5 18.2 %collective-permute-start.5 = (f32[544,128]{1,0:T(8,128)}, f32[544,128]{1,0:T(8,128)S(1)}, u32[]{:S(2)}, u32[]{:S(2)}) collective-permute-start(f32[544,128]{1,0:T(8,128)} %bitcast.85), channel_id=1, source_target_pairs={{0,4},{4,8},{8,12},{12,16},{16,20},{20,24},{24,28},{28,0},{1,5},{5... | collective-permute-start | bytes 835592 | tf_op jit(solution)/shard_map/ppermute | solution.py:112
  213.8 20.0 %collective-permute-start.14 = (f32[136,128]{1,0:T(8,128)S(1)}, f32[136,128]{1,0:T(8,128)S(1)}, u32[]{:S(2)}, u32[]{:S(2)}) collective-permute-start(f32[136,128]{1,0:T(8,128)S(1)} %get-tuple-element.97), channel_id=1, source_target_pairs={{0,3},{1,0},{2,1},{3,2},{4,7},{5,4},{6,5},{7,6},{8,11},{9,8},{10,9... | collective-permute-start | bytes 208904 | tf_op jit(solution)/shard_map/ppermute | solution.py:124
  222.8 11.0 %collective-permute-start.13 = (f32[136,128]{1,0:T(8,128)S(1)}, f32[136,128]{1,0:T(8,128)S(1)}, u32[]{:S(2)}, u32[]{:S(2)}) collective-permute-start(f32[136,128]{1,0:T(8,128)S(1)} %get-tuple-element.98), channel_id=1, source_target_pairs={{0,2},{1,3},{2,0},{3,1},{4,6},{5,7},{6,4},{7,5},{8,10},{9,11},{10,... | collective-permute-start | bytes 208904 | tf_op jit(solution)/shard_map/ppermute | solution.py:124
  229.9 8.0 %collective-permute-start.12 = (f32[136,128]{1,0:T(8,128)S(1)}, f32[136,128]{1,0:T(8,128)S(1)}, u32[]{:S(2)}, u32[]{:S(2)}) collective-permute-start(f32[136,128]{1,0:T(8,128)S(1)} %get-tuple-element.96), channel_id=1, source_target_pairs={{0,1},{1,2},{2,3},{3,0},{4,5},{5,6},{6,7},{7,4},{8,9},{9,10},{10,1... | collective-permute-start | bytes 208904 | tf_op jit(solution)/shard_map/ppermute | solution.py:124

commit v6 on v4

--- a/solution.py
+++ b/solution.py
@@ -96,16 +96,10 @@
         ],
         axis=1,
     ).reshape(blocks * block_rows, width_k)
-    owned = lax.psum_scatter(packed, "y", scatter_dimension=0, tiled=True)
-    my_zl = lax.axis_index("zl")
-    total = lax.dynamic_slice_in_dim(owned, my_zl * block_rows, block_rows, 0)
-    for shift in range(1, n_zl):
-        dest = (my_zl + shift) % n_zl
-        piece = lax.dynamic_slice_in_dim(owned, dest * block_rows, block_rows, 0)
-        total = total + lax.ppermute(
-            piece, "zl", perm=[(i, (i + shift) % n_zl) for i in range(n_zl)]
-        )
-    owned = total
+    arrived = lax.all_to_all(
+        packed.reshape(blocks, block_rows, width_k), SAMP_AXES, 0, 0, tiled=False
+    )
+    owned = jnp.sum(arrived, axis=0)
 
     return finish(
         owned[:width_k], owned[width_k + 1], owned[width_k + 2], owned[width_k],

time: 206 us -> 196 us (0.951)
  blocking collectives: 19.2 us -> 95 us
  waiting for transfers between devices: 85.2 us -> 26.1 us
  between operations: 13.6 us -> 0.16 us
  starting transfers between devices: 24.8 us -> 13.6 us
    all_to_all x0 -> x1, blocking collectives: none -> 75.8 us  [per_device(): lax.all_to_all(packed.reshape(blocks, block_rows, width_k), SAMP_AXES, 0,...]
    reduce_scatter x1 -> x0, waiting for transfers between devices: 56.1 us -> none  [per_device(): owned = lax.psum_scatter(packed, 'y', scatter_dimension=0, tiled=True)]
    ppermute x3 -> x0, starting transfers between devices: 11.2 us -> none  [per_device(): lax.ppermute(piece, 'zl', perm=[(i, (i + shift) % n_zl) for i in range(n_...]
    ppermute x3 -> x0, waiting for transfers between devices: 3.07 us -> none  [per_device(): lax.ppermute(piece, 'zl', perm=[(i, (i + shift) % n_zl) for i in range(n_...]
  transfers between devices with their start and end apart: 9 -> 5, of which waited for: 6 -> 4; matrix products, arithmetic and copies ran while one was open for 2% -> 2% of each run, Pallas kernels for 0% -> 0%
where the time goes in v6:
time: 196 us; the launch traced here: 195 us
  blocking collectives  95 us (48%)
  local copies, waits for them, and re-layouts  49.8 us (25%)
  waiting for transfers between devices  26.1 us (13%)
  starting transfers between devices  13.6 us (7%)
  other arithmetic  9.84 us (5%)
    all_to_all x1, blocking collectives, per_device(): lax.all_to_all(packed.reshape(blocks, block_rows, width_k), SAMP_AXES, 0,...  75.8 us
    gather x1, local copies, waits for them, and re-layouts, per_device(): second = jnp.take(rows, position(pair_list[1]), axis=0)  20.3 us
    all_gather x1, blocking collectives, per_device(): rows = lax.all_gather(tier_one, 'zh', axis=0, tiled=True)  19.2 us
    gather x1, local copies, waits for them, and re-layouts, per_device(): first = jnp.take(rows, position(pair_list[0]), axis=0)  17.6 us
    ppermute x1, waiting for transfers between devices, ring_gather(): from_left = lax.ppermute(block, axis, perm=fwd)  14.7 us
    reduce_sum x1, other arithmetic, per_device(): square_sums = jnp.sum(widened * widened, axis=1)  8.61 us
    ppermute x1, waiting for transfers between devices, per_device(): other = lax.ppermute(rows, 'c', perm=[(0, 1), (1, 0)])  5.4 us
    unnamed x8, local copies, waits for them, and re-layouts  4.57 us
  transfers between devices with their start and end apart: 5, of which 4 were waited for; matrix products, arithmetic and copies ran while one was open for 2% of the time, Pallas kernels for 0%

profile of v6, /device:TPU:6, one launch (start us, length us, event | category | flops | bytes accessed | tf_op | source)
XLA Modules:
  0.0 195.5 jit_solution(10819614753384634786)
XLA Ops:
  0.0 19.2 %all_gather.3 = bf16[1024,384]{1,0:T(8,128)(2,1)S(1)} all-gather(bf16[512,384]{1,0:T(8,128)(2,1)} %param.5), channel_id=1, replica_groups=mesh['x'=4,'zh'=2,'c'=2,'y'=8,'zl'=4] {'zh'}, dimensions={0}, use_global_device_ids=true | all-gather | bytes 1179648 | tf_op jit(solution)/shard_map/all_gather | solution.py:63
  19.2 2.4 %collective-permute-start.1 = (bf16[1024,384]{1,0:T(8,128)(2,1)S(1)}, bf16[1024,384]{1,0:T(8,128)(2,1)S(1)}, u32[]{:S(2)}, u32[]{:S(2)}) collective-permute-start(bf16[1024,384]{1,0:T(8,128)(2,1)S(1)} %all_gather.3), channel_id=1, source_target_pairs={{0,128},{128,256},{256,384},{384,0},{1,129},{129,257},{257,385},{3... | collective-permute-start | bytes 2359304 | tf_op jit(solution)/shard_map/ppermute | solution.py:37
  21.6 3.5 %collective-permute-start = (bf16[1024,384]{1,0:T(8,128)(2,1)S(1)}, bf16[1024,384]{1,0:T(8,128)(2,1)S(1)}, u32[]{:S(2)}, u32[]{:S(2)}) collective-permute-start(bf16[1024,384]{1,0:T(8,128)(2,1)S(1)} %all_gather.3), channel_id=1, source_target_pairs={{0,384},{128,0},{256,128},{384,256},{1,385},{129,1},{257,129},{385... | collective-permute-start | bytes 2359304 | tf_op jit(solution)/shard_map/ppermute | solution.py:38
  25.0 14.7 %collective-permute-done.1 = bf16[1024,384]{1,0:T(8,128)(2,1)S(1)} collective-permute-done((bf16[1024,384]{1,0:T(8,128)(2,1)S(1)}, bf16[1024,384]{1,0:T(8,128)(2,1)S(1)}, u32[]{:S(2)}, u32[]{:S(2)}) %collective-permute-start.1) | collective-permute-done | bytes 786464 | tf_op jit(solution)/shard_map/ppermute | solution.py:37
  39.8 3.4 %collective-permute-start.2 = (bf16[512,384]{1,0:T(8,128)(2,1)S(1)}, bf16[512,384]{1,0:T(8,128)(2,1)S(1)}, u32[]{:S(2)}, u32[]{:S(2)}) collective-permute-start(bf16[512,384]{1,0:T(8,128)(2,1)S(1)} %slice.40), channel_id=1, source_target_pairs={{0,128},{128,256},{256,384},{384,0},{1,129},{129,257},{257,385},{3... | collective-permute-start | bytes 1179656 | tf_op jit(solution)/shard_map/ppermute | solution.py:40
  43.2 0.0 collective-permute-done
  43.3 2.4 %collective-permute-start.3 = (bf16[512,384]{1,0:T(8,128)(2,1)S(1)}, bf16[512,384]{1,0:T(8,128)(2,1)S(1)}, u32[]{:S(2)}, u32[]{:S(2)}) collective-permute-start(bf16[512,384]{1,0:T(8,128)(2,1)S(1)} %slice.41), channel_id=1, source_target_pairs={{0,384},{128,0},{256,128},{384,256},{1,385},{129,1},{257,129},{385... | collective-permute-start | bytes 1179656 | tf_op jit(solution)/shard_map/ppermute | solution.py:41
  45.7 1.3 constant_dynamic-update-slice_fusion.4
  47.0 0.0 copy-start
  47.0 0.0 copy-start.1
  47.0 1.3 constant_dynamic-update-slice_fusion.3
  48.3 2.7 %collective-permute-done.2 = bf16[512,384]{1,0:T(8,128)(2,1)S(1)} collective-permute-done((bf16[512,384]{1,0:T(8,128)(2,1)S(1)}, bf16[512,384]{1,0:T(8,128)(2,1)S(1)}, u32[]{:S(2)}, u32[]{:S(2)}) %collective-permute-start.2) | collective-permute-done | bytes 393248 | tf_op jit(solution)/shard_map/ppermute | solution.py:40
  51.0 1.0 constant_dynamic-update-slice_fusion.2
  52.0 3.2 %collective-permute-done.3 = bf16[512,384]{1,0:T(8,128)(2,1)S(1)} collective-permute-done((bf16[512,384]{1,0:T(8,128)(2,1)S(1)}, bf16[512,384]{1,0:T(8,128)(2,1)S(1)}, u32[]{:S(2)}, u32[]{:S(2)}) %collective-permute-start.3) | collective-permute-done | bytes 393248 | tf_op jit(solution)/shard_map/ppermute | solution.py:41
  55.2 1.0 constant_dynamic-update-slice_fusion.1
  56.3 1.3 constant_dynamic-update-slice_fusion
  57.6 1.9 collective-permute-start.4
  59.5 0.0 copy-done
  59.5 0.1 convert_reduce_fusion.1
  59.6 0.0 copy-done.1
  59.6 0.2 compare_reduce_fusion.2
  59.8 0.1 compare_and_fusion
  60.0 5.4 %collective-permute-done.4 = bf16[4096,384]{1,0:T(8,128)(2,1)S(1)} collective-permute-done((bf16[4096,384]{1,0:T(8,128)(2,1)}, bf16[4096,384]{1,0:T(8,128)(2,1)S(1)}, u32[]{:S(2)}, u32[]{:S(2)}) %collective-permute-start.4) | collective-permute-done | bytes 3145760 | tf_op jit(solution)/shard_map/ppermute | solution.py:65
  65.4 2.0 %constant_dynamic-update-slice_fusion.5 = bf16[8192,384]{1,0:T(8,128)(2,1)} fusion(bf16[8192,384]{1,0:T(8,128)(2,1)} %get-tuple-element.17, bf16[4096,384]{1,0:T(8,128)(2,1)S(1)} %collective-permute-done.4), kind=kLoop, calls=%fused_computation.67 | loop fusion | bytes 6291456 | tf_op jit(solution)/shard_map/concatenate | solution.py:66
  67.4 17.6 %gather_fusion = bf16[4096,384]{1,0:T(8,128)(2,1)S(1)} fusion(bf16[8192,384]{1,0:T(8,128)(2,1)} %constant_dynamic-update-slice_fusion.5, s32[4096]{0:T(1024)S(1)} %broadcast_clamp_fusion.1), kind=kCustom, calls=%fused_computation.clone | custom fusion | bytes 6307840 | tf_op jit(solution)/shard_map/jit(_take)/gather | solution.py:77
  85.0 20.3 %gather_fusion.1 = bf16[4096,384]{1,0:T(8,128)(2,1)} fusion(bf16[8192,384]{1,0:T(8,128)(2,1)} %constant_dynamic-update-slice_fusion.5, s32[4096]{0:T(1024)S(1)} %broadcast_clamp_fusion), kind=kCustom, calls=%fused_computation.1.clone | custom fusion | bytes 6307840 | tf_op jit(solution)/shard_map/jit(_take)/gather | solution.py:78
  105.3 8.6 %fusion = (f32[4096]{0:T(1024)S(1)}, f32[4096]{0:T(1024)S(1)}, bf16[4096,384]{1,0:T(8,128)(2,1)S(1)}) fusion(pred[4096]{0:T(1024)(128)(4,1)S(1)} %get-tuple-element.10, pred[4096]{0:T(1024)(128)(4,1)S(1)} %get-tuple-element.9, bf16[4096,384]{1,0:T(8,128)(2,1)} %gather_fusion.1, pred[4096]{0:T(1024)(128)(4,1)S(1)} %get-tuple-element.14, ...), kind=kLoop, calls=%fused_computation.9 | loop fusion | flops 28303360 | bytes 9490432 | tf_op jit(solution)/shard_map/reduce_sum | solution.py:84
  113.9 1.0 fusion.41
  114.9 3.8 %concatenate.12 = f32[32,136,128]{2,1,0:T(8,128)} concatenate(f32[32,128,128]{2,1,0:T(8,128)S(1)} %bitcast.19, f32[32,1,128]{2,1,0:T(1,128)S(1)} %broadcast_in_dim.41, f32[32,1,128]{2,1,0:T(1,128)S(1)} %bitcast.21, f32[32,1,128]{2,1,0:T(1,128)S(1)} %bitcast.20, f32[32,5,128]{2,1,0:T(8,128)S(1)} %broadcast_in_dim.42), dimensions={1} | concatenate | bytes 4456448 | tf_op jit(solution)/shard_map/concatenate | solution.py:89
  118.8 75.8 %all_to_all.5 = f32[32,136,128]{2,1,0:T(8,128)S(1)} all-to-all(f32[32,136,128]{2,1,0:T(8,128)} %concatenate.12), channel_id=1, replica_groups=mesh['x'=4,'zh'=2,'c'=2,'y'=8,'zl'=4] {'y','zl'}, dimensions={0} | all-to-all | bytes 4456448 | tf_op jit(solution)/shard_map/all_to_all | solution.py:99
  194.6 0.1 reduce_sum.39
  194.7 0.7 fusion.7
  (9 shorter events, 0.2 us)
Async XLA Ops:
  19.2 20.6 %collective-permute-start.1 = (bf16[1024,384]{1,0:T(8,128)(2,1)S(1)}, bf16[1024,384]{1,0:T(8,128)(2,1)S(1)}, u32[]{:S(2)}, u32[]{:S(2)}) collective-permute-start(bf16[1024,384]{1,0:T(8,128)(2,1)S(1)} %all_gather.3), channel_id=1, source_target_pairs={{0,128},{128,256},{256,384},{384,0},{1,129},{129,257},{257,385},{3... | collective-permute-start | bytes 2359304 | tf_op jit(solution)/shard_map/ppermute | solution.py:37
  21.6 21.6 %collective-permute-start = (bf16[1024,384]{1,0:T(8,128)(2,1)S(1)}, bf16[1024,384]{1,0:T(8,128)(2,1)S(1)}, u32[]{:S(2)}, u32[]{:S(2)}) collective-permute-start(bf16[1024,384]{1,0:T(8,128)(2,1)S(1)} %all_gather.3), channel_id=1, source_target_pairs={{0,384},{128,0},{256,128},{384,256},{1,385},{129,1},{257,129},{385... | collective-permute-start | bytes 2359304 | tf_op jit(solution)/shard_map/ppermute | solution.py:38
  39.8 11.2 %collective-permute-start.2 = (bf16[512,384]{1,0:T(8,128)(2,1)S(1)}, bf16[512,384]{1,0:T(8,128)(2,1)S(1)}, u32[]{:S(2)}, u32[]{:S(2)}) collective-permute-start(bf16[512,384]{1,0:T(8,128)(2,1)S(1)} %slice.40), channel_id=1, source_target_pairs={{0,128},{128,256},{256,384},{384,0},{1,129},{129,257},{257,385},{3... | collective-permute-start | bytes 1179656 | tf_op jit(solution)/shard_map/ppermute | solution.py:40
  43.3 12.0 %collective-permute-start.3 = (bf16[512,384]{1,0:T(8,128)(2,1)S(1)}, bf16[512,384]{1,0:T(8,128)(2,1)S(1)}, u32[]{:S(2)}, u32[]{:S(2)}) collective-permute-start(bf16[512,384]{1,0:T(8,128)(2,1)S(1)} %slice.41), channel_id=1, source_target_pairs={{0,384},{128,0},{256,128},{384,256},{1,385},{129,1},{257,129},{385... | collective-permute-start | bytes 1179656 | tf_op jit(solution)/shard_map/ppermute | solution.py:41
  47.0 12.5 %copy-start = (bf16[384,128]{1,0:T(8,128)(2,1)S(1)}, bf16[384,128]{1,0:T(8,128)(2,1)}, u32[]{:S(2)}) copy-start(bf16[384,128]{1,0:T(8,128)(2,1)} %param.6) | copy-start | bytes 294916
  47.0 12.6 %copy-start.1 = (s32[3,4096]{1,0:T(4,128)S(1)}, s32[3,4096]{1,0:T(4,128)}, u32[]{:S(2)}) copy-start(s32[3,4096]{1,0:T(4,128)} %param.7) | copy-start | bytes 147460
  57.6 7.8 %collective-permute-start.4 = (bf16[4096,384]{1,0:T(8,128)(2,1)}, bf16[4096,384]{1,0:T(8,128)(2,1)S(1)}, u32[]{:S(2)}, u32[]{:S(2)}) collective-permute-start(bf16[4096,384]{1,0:T(8,128)(2,1)} %get-tuple-element.16), channel_id=1, source_target_pairs={{0,32},{32,0},{1,33},{33,1},{2,34},{34,2},{3,35},{35,3},{4,36},{36... | collective-permute-start | bytes 9437192 | tf_op jit(solution)/shard_map/ppermute | solution.py:65

commit v7 on v6

--- a/solution.py
+++ b/solution.py
@@ -11,7 +11,7 @@
 
 FEAT_AXES = ("x", "zh", "c")
 SAMP_AXES = ("y", "zl")
-EXTRA_ROWS = 8
+EXTRA_ROWS = 16
 
 
 def combine_rows(first_rows, second_rows, operator_id):
@@ -40,6 +40,14 @@
     far_a = lax.ppermute(from_left[:half], axis, perm=fwd)
     far_b = lax.ppermute(from_right[half:], axis, perm=bwd)
     return jnp.concatenate([block, from_right, far_a, far_b, from_left], axis=0)
+
+
+def split3(v):
+    hi = lax.reduce_precision(v, exponent_bits=8, mantissa_bits=7)
+    rest = v - hi
+    mid = lax.reduce_precision(rest, exponent_bits=8, mantissa_bits=7)
+    lo = rest - mid
+    return jnp.stack([hi, mid, lo], axis=-2).astype(jnp.bfloat16)
 
 
 def finish(product, first_sums, square_sums, col_totals, sample_count):
@@ -83,26 +91,42 @@
     first_sums = jnp.sum(widened, axis=1)
     square_sums = jnp.sum(widened * widened, axis=1)
     col_part = jnp.sum(residuals.astype(jnp.float32), axis=0)
+    local_samples = residuals.shape[0]
+
+    local_means = first_sums / local_samples
+    centred = product - local_means[:, None] * col_part[None, :]
 
     blocks = local_pairs // width_k
     block_rows = width_k + EXTRA_ROWS
-    packed = jnp.concatenate(
+    extras = jnp.concatenate(
         [
-            product.reshape(blocks, width_k, width_k),
-            jnp.broadcast_to(col_part[None, None, :], (blocks, 1, width_k)),
-            first_sums.reshape(blocks, 1, width_k),
-            square_sums.reshape(blocks, 1, width_k),
-            jnp.zeros((blocks, EXTRA_ROWS - 3, width_k), jnp.float32),
+            split3(jnp.broadcast_to(col_part[None, :], (blocks, width_k))),
+            split3(first_sums.reshape(blocks, width_k)),
+            split3(square_sums.reshape(blocks, width_k)),
+            jnp.zeros((blocks, EXTRA_ROWS - 9, width_k), jnp.bfloat16),
         ],
         axis=1,
-    ).reshape(blocks * block_rows, width_k)
-    arrived = lax.all_to_all(
-        packed.reshape(blocks, block_rows, width_k), SAMP_AXES, 0, 0, tiled=False
     )
-    owned = jnp.sum(arrived, axis=0)
+    packed = jnp.concatenate(
+        [centred.astype(jnp.bfloat16).reshape(blocks, width_k, width_k), extras], axis=1
+    )
+    arrived = lax.all_to_all(packed, SAMP_AXES, 0, 0, tiled=False)
+    centred_sum = jnp.sum(arrived[:, :width_k].astype(jnp.float32), axis=0)
+    pieces = arrived[:, width_k:].astype(jnp.float32)
 
+    def joined(i):
+        return (pieces[:, i] + pieces[:, i + 1]) + pieces[:, i + 2]
+
+    col_parts, first_parts, square_parts = joined(0), joined(3), joined(6)
+    mean_share = jnp.einsum(
+        "dp,dk->pk", first_parts / local_samples, col_parts,
+        precision=lax.Precision.HIGHEST,
+    )
     return finish(
-        owned[:width_k], owned[width_k + 1], owned[width_k + 2], owned[width_k],
+        centred_sum + mean_share,
+        jnp.sum(first_parts, axis=0),
+        jnp.sum(square_parts, axis=0),
+        jnp.sum(col_parts, axis=0),
         sample_count,
     )
 

time: 196 us -> 171 us (0.87)
  blocking collectives: 95 us -> 72.3 us
  local copies, waits for them, and re-layouts: 49.8 us -> 46.7 us
    all_to_all x1, blocking collectives: 75.8 us -> 53.1 us  [per_device(): arrived = lax.all_to_all(packed, SAMP_AXES, 0, 0, tiled=False)]
    concatenate x1, local copies, waits for them, and re-layouts: 3.83 us -> 0.6 us  [per_device(): jnp.concatenate([centred.astype(jnp.bfloat16).reshape(blocks, width_k, wi...]
where the time goes in v7:
time: 171 us; the launch traced here: 170 us
  blocking collectives  72.3 us (42%)
  local copies, waits for them, and re-layouts  46.7 us (27%)
  waiting for transfers between devices  26.1 us (15%)
  starting transfers between devices  13.6 us (8%)
  other arithmetic  9.33 us (5%)
  matrix products  2.11 us (1%)
    all_to_all x1, blocking collectives, per_device(): arrived = lax.all_to_all(packed, SAMP_AXES, 0, 0, tiled=False)  53.1 us
    gather x1, local copies, waits for them, and re-layouts, per_device(): second = jnp.take(rows, position(pair_list[1]), axis=0)  20.3 us
    all_gather x1, blocking collectives, per_device(): rows = lax.all_gather(tier_one, 'zh', axis=0, tiled=True)  19.2 us
    gather x1, local copies, waits for them, and re-layouts, per_device(): first = jnp.take(rows, position(pair_list[0]), axis=0)  17.6 us
    ppermute x1, waiting for transfers between devices, ring_gather(): from_left = lax.ppermute(block, axis, perm=fwd)  14.7 us
    reduce_sum x1, other arithmetic, per_device(): square_sums = jnp.sum(widened * widened, axis=1)  8.61 us
    ppermute x1, waiting for transfers between devices, per_device(): other = lax.ppermute(rows, 'c', perm=[(0, 1), (1, 0)])  5.39 us
    unnamed x8, local copies, waits for them, and re-layouts  4.57 us
  transfers between devices with their start and end apart: 5, of which 4 were waited for; matrix products, arithmetic and copies ran while one was open for 2% of the time, Pallas kernels for 0%

profile of v7, /device:TPU:6, one launch (start us, length us, event | category | flops | bytes accessed | tf_op | source)
XLA Modules:
  0.0 170.4 jit_solution(11472657003874128858)
XLA Ops:
  0.0 19.2 %all_gather.3 = bf16[1024,384]{1,0:T(8,128)(2,1)S(1)} all-gather(bf16[512,384]{1,0:T(8,128)(2,1)} %param.5), channel_id=1, replica_groups=mesh['x'=4,'zh'=2,'c'=2,'y'=8,'zl'=4] {'zh'}, dimensions={0}, use_global_device_ids=true | all-gather | bytes 1179648 | tf_op jit(solution)/shard_map/all_gather | solution.py:71
  19.2 2.4 %collective-permute-start.1 = (bf16[1024,384]{1,0:T(8,128)(2,1)S(1)}, bf16[1024,384]{1,0:T(8,128)(2,1)S(1)}, u32[]{:S(2)}, u32[]{:S(2)}) collective-permute-start(bf16[1024,384]{1,0:T(8,128)(2,1)S(1)} %all_gather.3), channel_id=1, source_target_pairs={{0,128},{128,256},{256,384},{384,0},{1,129},{129,257},{257,385},{3... | collective-permute-start | bytes 2359304 | tf_op jit(solution)/shard_map/ppermute | solution.py:37
  21.6 3.5 %collective-permute-start = (bf16[1024,384]{1,0:T(8,128)(2,1)S(1)}, bf16[1024,384]{1,0:T(8,128)(2,1)S(1)}, u32[]{:S(2)}, u32[]{:S(2)}) collective-permute-start(bf16[1024,384]{1,0:T(8,128)(2,1)S(1)} %all_gather.3), channel_id=1, source_target_pairs={{0,384},{128,0},{256,128},{384,256},{1,385},{129,1},{257,129},{385... | collective-permute-start | bytes 2359304 | tf_op jit(solution)/shard_map/ppermute | solution.py:38
  25.0 14.7 %collective-permute-done.1 = bf16[1024,384]{1,0:T(8,128)(2,1)S(1)} collective-permute-done((bf16[1024,384]{1,0:T(8,128)(2,1)S(1)}, bf16[1024,384]{1,0:T(8,128)(2,1)S(1)}, u32[]{:S(2)}, u32[]{:S(2)}) %collective-permute-start.1) | collective-permute-done | bytes 786464 | tf_op jit(solution)/shard_map/ppermute | solution.py:37
  39.8 3.4 %collective-permute-start.2 = (bf16[512,384]{1,0:T(8,128)(2,1)S(1)}, bf16[512,384]{1,0:T(8,128)(2,1)S(1)}, u32[]{:S(2)}, u32[]{:S(2)}) collective-permute-start(bf16[512,384]{1,0:T(8,128)(2,1)S(1)} %slice.68), channel_id=1, source_target_pairs={{0,128},{128,256},{256,384},{384,0},{1,129},{129,257},{257,385},{3... | collective-permute-start | bytes 1179656 | tf_op jit(solution)/shard_map/ppermute | solution.py:40
  43.2 0.0 collective-permute-done
  43.3 2.4 %collective-permute-start.3 = (bf16[512,384]{1,0:T(8,128)(2,1)S(1)}, bf16[512,384]{1,0:T(8,128)(2,1)S(1)}, u32[]{:S(2)}, u32[]{:S(2)}) collective-permute-start(bf16[512,384]{1,0:T(8,128)(2,1)S(1)} %slice.69), channel_id=1, source_target_pairs={{0,384},{128,0},{256,128},{384,256},{1,385},{129,1},{257,129},{385... | collective-permute-start | bytes 1179656 | tf_op jit(solution)/shard_map/ppermute | solution.py:41
  45.7 1.3 constant_dynamic-update-slice_fusion.4
  47.0 0.0 copy-start
  47.0 0.0 copy-start.1
  47.0 1.3 constant_dynamic-update-slice_fusion.3
  48.3 2.7 %collective-permute-done.2 = bf16[512,384]{1,0:T(8,128)(2,1)S(1)} collective-permute-done((bf16[512,384]{1,0:T(8,128)(2,1)S(1)}, bf16[512,384]{1,0:T(8,128)(2,1)S(1)}, u32[]{:S(2)}, u32[]{:S(2)}) %collective-permute-start.2) | collective-permute-done | bytes 393248 | tf_op jit(solution)/shard_map/ppermute | solution.py:40
  51.0 1.0 constant_dynamic-update-slice_fusion.2
  52.0 3.2 %collective-permute-done.3 = bf16[512,384]{1,0:T(8,128)(2,1)S(1)} collective-permute-done((bf16[512,384]{1,0:T(8,128)(2,1)S(1)}, bf16[512,384]{1,0:T(8,128)(2,1)S(1)}, u32[]{:S(2)}, u32[]{:S(2)}) %collective-permute-start.3) | collective-permute-done | bytes 393248 | tf_op jit(solution)/shard_map/ppermute | solution.py:41
  55.2 1.0 constant_dynamic-update-slice_fusion.1
  56.3 1.3 constant_dynamic-update-slice_fusion
  57.6 1.9 %collective-permute-start.4 = (bf16[4096,384]{1,0:T(8,128)(2,1)}, bf16[4096,384]{1,0:T(8,128)(2,1)S(1)}, u32[]{:S(2)}, u32[]{:S(2)}) collective-permute-start(bf16[4096,384]{1,0:T(8,128)(2,1)} %get-tuple-element.20), channel_id=1, source_target_pairs={{0,32},{32,0},{1,33},{33,1},{2,34},{34,2},{3,35},{35,3},{4,36},{36... | collective-permute-start | bytes 9437192 | tf_op jit(solution)/shard_map/ppermute | solution.py:73
  59.5 0.0 copy-done
  59.5 0.1 convert_reduce_fusion.2
  59.6 0.0 copy-done.1
  59.6 0.2 compare_reduce_fusion.2
  59.8 0.1 compare_and_fusion
  60.0 5.4 %collective-permute-done.4 = bf16[4096,384]{1,0:T(8,128)(2,1)S(1)} collective-permute-done((bf16[4096,384]{1,0:T(8,128)(2,1)}, bf16[4096,384]{1,0:T(8,128)(2,1)S(1)}, u32[]{:S(2)}, u32[]{:S(2)}) %collective-permute-start.4) | collective-permute-done | bytes 3145760 | tf_op jit(solution)/shard_map/ppermute | solution.py:73
  65.4 2.0 %constant_dynamic-update-slice_fusion.5 = bf16[8192,384]{1,0:T(8,128)(2,1)} fusion(bf16[8192,384]{1,0:T(8,128)(2,1)} %get-tuple-element.21, bf16[4096,384]{1,0:T(8,128)(2,1)S(1)} %collective-permute-done.4), kind=kLoop, calls=%fused_computation.80 | loop fusion | bytes 6291456 | tf_op jit(solution)/shard_map/concatenate | solution.py:74
  67.4 17.6 %gather_fusion = bf16[4096,384]{1,0:T(8,128)(2,1)S(1)} fusion(bf16[8192,384]{1,0:T(8,128)(2,1)} %constant_dynamic-update-slice_fusion.5, s32[4096]{0:T(1024)S(1)} %broadcast_clamp_fusion.1), kind=kCustom, calls=%fused_computation.clone | custom fusion | bytes 6307840 | tf_op jit(solution)/shard_map/jit(_take)/gather | solution.py:85
  85.0 20.3 %gather_fusion.1 = bf16[4096,384]{1,0:T(8,128)(2,1)} fusion(bf16[8192,384]{1,0:T(8,128)(2,1)} %constant_dynamic-update-slice_fusion.5, s32[4096]{0:T(1024)S(1)} %broadcast_clamp_fusion), kind=kCustom, calls=%fused_computation.1.clone | custom fusion | bytes 6307840 | tf_op jit(solution)/shard_map/jit(_take)/gather | solution.py:86
  105.3 8.6 %fusion = (f32[4096]{0:T(1024)S(1)}, f32[4096]{0:T(1024)S(1)}, bf16[4096,384]{1,0:T(8,128)(2,1)S(1)}) fusion(pred[4096]{0:T(1024)(128)(4,1)S(1)} %get-tuple-element.10, pred[4096]{0:T(1024)(128)(4,1)S(1)} %get-tuple-element.9, bf16[4096,384]{1,0:T(8,128)(2,1)} %gather_fusion.1, pred[4096]{0:T(1024)(128)(4,1)S(1)} %get-tuple-element.18, ...), kind=kLoop, calls=%fused_computation.9 | loop fusion | flops 28303360 | bytes 9490432 | tf_op jit(solution)/shard_map/reduce_sum | solution.py:92
  114.1 1.2 fusion.6
  115.4 0.6 concatenate.13
  116.0 53.1 %all_to_all.5 = bf16[32,144,128]{2,1,0:T(8,128)(2,1)S(1)} all-to-all(bf16[32,144,128]{2,1,0:T(8,128)(2,1)S(1)} %concatenate.13), channel_id=1, replica_groups=mesh['x'=4,'zh'=2,'c'=2,'y'=8,'zl'=4] {'y','zl'}, dimensions={0} | all-to-all | bytes 2359296 | tf_op jit(solution)/shard_map/all_to_all | solution.py:113
  169.1 0.1 fusion.42
  169.3 0.2 convert_reduce_fusion.1
  169.5 0.9 fusion.9
  (22 shorter events, 0.3 us)
Async XLA Ops:
  19.2 20.6 %collective-permute-start.1 = (bf16[1024,384]{1,0:T(8,128)(2,1)S(1)}, bf16[1024,384]{1,0:T(8,128)(2,1)S(1)}, u32[]{:S(2)}, u32[]{:S(2)}) collective-permute-start(bf16[1024,384]{1,0:T(8,128)(2,1)S(1)} %all_gather.3), channel_id=1, source_target_pairs={{0,128},{128,256},{256,384},{384,0},{1,129},{129,257},{257,385},{3... | collective-permute-start | bytes 2359304 | tf_op jit(solution)/shard_map/ppermute | solution.py:37
  21.6 21.6 %collective-permute-start = (bf16[1024,384]{1,0:T(8,128)(2,1)S(1)}, bf16[1024,384]{1,0:T(8,128)(2,1)S(1)}, u32[]{:S(2)}, u32[]{:S(2)}) collective-permute-start(bf16[1024,384]{1,0:T(8,128)(2,1)S(1)} %all_gather.3), channel_id=1, source_target_pairs={{0,384},{128,0},{256,128},{384,256},{1,385},{129,1},{257,129},{385... | collective-permute-start | bytes 2359304 | tf_op jit(solution)/shard_map/ppermute | solution.py:38
  39.8 11.2 %collective-permute-start.2 = (bf16[512,384]{1,0:T(8,128)(2,1)S(1)}, bf16[512,384]{1,0:T(8,128)(2,1)S(1)}, u32[]{:S(2)}, u32[]{:S(2)}) collective-permute-start(bf16[512,384]{1,0:T(8,128)(2,1)S(1)} %slice.68), channel_id=1, source_target_pairs={{0,128},{128,256},{256,384},{384,0},{1,129},{129,257},{257,385},{3... | collective-permute-start | bytes 1179656 | tf_op jit(solution)/shard_map/ppermute | solution.py:40
  43.3 12.0 %collective-permute-start.3 = (bf16[512,384]{1,0:T(8,128)(2,1)S(1)}, bf16[512,384]{1,0:T(8,128)(2,1)S(1)}, u32[]{:S(2)}, u32[]{:S(2)}) collective-permute-start(bf16[512,384]{1,0:T(8,128)(2,1)S(1)} %slice.69), channel_id=1, source_target_pairs={{0,384},{128,0},{256,128},{384,256},{1,385},{129,1},{257,129},{385... | collective-permute-start | bytes 1179656 | tf_op jit(solution)/shard_map/ppermute | solution.py:41
  47.0 12.5 %copy-start = (bf16[384,128]{1,0:T(8,128)(2,1)S(1)}, bf16[384,128]{1,0:T(8,128)(2,1)}, u32[]{:S(2)}) copy-start(bf16[384,128]{1,0:T(8,128)(2,1)} %param.6) | copy-start | bytes 294916
  47.0 12.6 %copy-start.1 = (s32[3,4096]{1,0:T(4,128)S(1)}, s32[3,4096]{1,0:T(4,128)}, u32[]{:S(2)}) copy-start(s32[3,4096]{1,0:T(4,128)} %param.7) | copy-start | bytes 147460
  57.6 7.8 %collective-permute-start.4 = (bf16[4096,384]{1,0:T(8,128)(2,1)}, bf16[4096,384]{1,0:T(8,128)(2,1)S(1)}, u32[]{:S(2)}, u32[]{:S(2)}) collective-permute-start(bf16[4096,384]{1,0:T(8,128)(2,1)} %get-tuple-element.20), channel_id=1, source_target_pairs={{0,32},{32,0},{1,33},{33,1},{2,34},{34,2},{3,35},{35,3},{4,36},{36... | collective-permute-start | bytes 9437192 | tf_op jit(solution)/shard_map/ppermute | solution.py:73

commit v8 on v7

--- a/solution.py
+++ b/solution.py
@@ -68,19 +68,32 @@
     n_samp = n_y * n_zl
     sample_count = residuals.shape[0] * n_samp
 
-    rows = lax.all_gather(tier_one, "zh", axis=0, tiled=True)
-    rows = ring_gather(rows, "x", n_x)
-    other = lax.ppermute(rows, "c", perm=[(0, 1), (1, 0)])
-    rows = jnp.concatenate([rows, other], axis=0)
+    my_zh = lax.axis_index("zh")
     my_c = lax.axis_index("c")
     my_x = lax.axis_index("x")
+
+    own_ring = ring_gather(tier_one, "x", n_x)
+    pair_rows = lax.all_gather(tier_one, "zh", axis=0, tiled=True)
+    partner = lax.dynamic_slice_in_dim(pair_rows, (1 - my_zh) * local_rows, local_rows, 0)
+    partner_ring = ring_gather(partner, "x", n_x)
+    swap = [(0, 1), (1, 0)]
+    rows = jnp.concatenate(
+        [
+            own_ring,
+            partner_ring,
+            lax.ppermute(own_ring, "c", perm=swap),
+            lax.ppermute(partner_ring, "c", perm=swap),
+        ],
+        axis=0,
+    )
 
     def position(g):
         f, r = g // local_rows, g % local_rows
         x, zh, c = f // (2 * n_zh), (f // 2) % n_zh, f % 2
-        half = (c != my_c).astype(jnp.int32)
+        c_half = (c != my_c).astype(jnp.int32)
+        zh_half = (zh != my_zh).astype(jnp.int32)
         x_slot = (x - my_x + n_x) % n_x
-        return ((half * n_x + x_slot) * n_zh + zh) * local_rows + r
+        return ((c_half * n_zh + zh_half) * n_x + x_slot) * local_rows + r
 
     first = jnp.take(rows, position(pair_list[0]), axis=0)
     second = jnp.take(rows, position(pair_list[1]), axis=0)

time: 171 us -> 172 us (level); the launches traced: 170 us -> 169 us
  waiting for transfers between devices: 26.1 us -> 2.16 us
  starting transfers between devices: 13.6 us -> 34.6 us
  local copies, waits for them, and re-layouts: 46.7 us -> 51.8 us
  blocking collectives: 72.3 us -> 68.1 us
    ppermute x1 -> x2, waiting for transfers between devices: 14.7 us -> 0.65 us  [ring_gather(): from_left = lax.ppermute(block, axis, perm=fwd)]
    ppermute x1 -> x2, starting transfers between devices: 2.38 us -> 12.1 us  [ring_gather(): from_left = lax.ppermute(block, axis, perm=fwd)]
    unnamed x8 -> x16, local copies, waits for them, and re-layouts: 4.57 us -> 9.81 us
    ppermute x1 -> x2, starting transfers between devices: 3.41 us -> 7.65 us  [ring_gather(): far_a = lax.ppermute(from_left[:half], axis, perm=fwd)]
    ppermute x1 -> x2, waiting for transfers between devices: 5.39 us -> 1.5 us  [the longest x1 1.5 us: per_device(): lax.ppermute(partner_ring, 'c', perm=swap)]
    ppermute x1 -> x2, starting transfers between devices: 2.43 us -> 5.84 us  [ring_gather(): far_b = lax.ppermute(from_right[half:], axis, perm=bwd)]
    ppermute x1 -> x2, waiting for transfers between devices: 3.25 us -> 0.01 us  [ring_gather(): far_b = lax.ppermute(from_right[half:], axis, perm=bwd)]
    all_gather x1, blocking collectives: 19.2 us -> 16 us  [per_device(): pair_rows = lax.all_gather(tier_one, 'zh', axis=0, tiled=True)]
  transfers between devices with their start and end apart: 5 -> 10, of which waited for: 4 -> 2; matrix products, arithmetic and copies ran while one was open for 2% -> 7% of each run, Pallas kernels for 0% -> 0%
where the time goes in v8:
time: 172 us; the launch traced here: 169 us
  blocking collectives  68.1 us (40%)
  local copies, waits for them, and re-layouts  51.8 us (30%)
  starting transfers between devices  34.6 us (20%)
  other arithmetic  9.33 us (5%)
  waiting for transfers between devices  2.16 us (1%)
  matrix products  2.11 us (1%)
    all_to_all x1, blocking collectives, per_device(): arrived = lax.all_to_all(packed, SAMP_AXES, 0, 0, tiled=False)  52.1 us
    gather x1, local copies, waits for them, and re-layouts, per_device(): second = jnp.take(rows, position(pair_list[1]), axis=0)  20.3 us
    gather x1, local copies, waits for them, and re-layouts, per_device(): first = jnp.take(rows, position(pair_list[0]), axis=0)  17.6 us
    all_gather x1, blocking collectives, per_device(): pair_rows = lax.all_gather(tier_one, 'zh', axis=0, tiled=True)  16 us
    ppermute x2, starting transfers between devices, ring_gather(): from_left = lax.ppermute(block, axis, perm=fwd)  12.1 us
    unnamed x16, local copies, waits for them, and re-layouts  9.81 us
    reduce_sum x1, other arithmetic, per_device(): square_sums = jnp.sum(widened * widened, axis=1)  8.61 us
    ppermute x2, starting transfers between devices, ring_gather(): far_a = lax.ppermute(from_left[:half], axis, perm=fwd)  7.65 us
  transfers between devices with their start and end apart: 10, of which 2 were waited for; matrix products, arithmetic and copies ran while one was open for 7% of the time, Pallas kernels for 0%

profile of v8, /device:TPU:6, one launch (start us, length us, event | category | flops | bytes accessed | tf_op | source)
XLA Modules:
  0.0 168.5 jit_solution(8974886311788646372)
XLA Ops:
  0.0 0.0 copy-start
  0.0 0.0 copy-start.2
  0.0 2.9 %collective-permute-start = (bf16[512,384]{1,0:T(8,128)(2,1)}, bf16[512,384]{1,0:T(8,128)(2,1)S(1)}, u32[]{:S(2)}, u32[]{:S(2)}) collective-permute-start(bf16[512,384]{1,0:T(8,128)(2,1)} %param.5), channel_id=1, source_target_pairs={{0,384},{128,0},{256,128},{384,256},{1,385},{129,1},{257,129},{385... | collective-permute-start | bytes 1179656 | tf_op jit(solution)/shard_map/ppermute | solution.py:38
  2.9 6.9 %collective-permute-start.1 = (bf16[512,384]{1,0:T(8,128)(2,1)}, bf16[512,384]{1,0:T(8,128)(2,1)S(1)}, u32[]{:S(2)}, u32[]{:S(2)}) collective-permute-start(bf16[512,384]{1,0:T(8,128)(2,1)} %param.5), channel_id=1, source_target_pairs={{0,128},{128,256},{256,384},{384,0},{1,129},{129,257},{257,385},{3... | collective-permute-start | bytes 1179656 | tf_op jit(solution)/shard_map/ppermute | solution.py:37
  9.8 16.0 %all_gather.3 = bf16[1024,384]{1,0:T(8,128)(2,1)S(1)} all-gather(bf16[512,384]{1,0:T(8,128)(2,1)} %param.5), channel_id=1, replica_groups=mesh['x'=4,'zh'=2,'c'=2,'y'=8,'zl'=4] {'zh'}, dimensions={0}, use_global_device_ids=true | all-gather | bytes 1179648 | tf_op jit(solution)/shard_map/all_gather | solution.py:76
  25.8 0.8 constant_dynamic-update-slice_fusion.9
  26.7 1.9 %collective-permute-start.4 = (bf16[512,384]{1,0:T(8,128)(2,1)S(1)}, bf16[512,384]{1,0:T(8,128)(2,1)S(1)}, u32[]{:S(2)}, u32[]{:S(2)}) collective-permute-start(bf16[512,384]{1,0:T(8,128)(2,1)S(1)} %get-tuple-element.21), channel_id=1, source_target_pairs={{0,384},{128,0},{256,128},{384,256},{1,385},{129,1},{257,129},{385... | collective-permute-start | bytes 1179656 | tf_op jit(solution)/shard_map/ppermute | solution.py:38
  28.6 5.1 %collective-permute-start.5 = (bf16[512,384]{1,0:T(8,128)(2,1)S(1)}, bf16[512,384]{1,0:T(8,128)(2,1)S(1)}, u32[]{:S(2)}, u32[]{:S(2)}) collective-permute-start(bf16[512,384]{1,0:T(8,128)(2,1)S(1)} %get-tuple-element.21), channel_id=1, source_target_pairs={{0,128},{128,256},{256,384},{384,0},{1,129},{129,257},{257,385},{3... | collective-permute-start | bytes 1179656 | tf_op jit(solution)/shard_map/ppermute | solution.py:37
  33.7 2.0 %constant_dynamic-update-slice_fusion.4 = (bf16[2048,384]{1,0:T(8,128)(2,1)}, bf16[8192,384]{1,0:T(8,128)(2,1)}) fusion(bf16[512,384]{1,0:T(8,128)(2,1)} %param.5), kind=kLoop, calls=%fused_computation.33 | loop fusion | bytes 1179648
  35.7 0.0 copy-done
  35.7 0.1 convert_reduce_fusion.2
  35.8 0.0 copy-start.1
  35.8 0.0 collective-permute-done.1
  35.8 2.1 %collective-permute-start.2 = (bf16[256,384]{1,0:T(8,128)(2,1)S(1)}, bf16[256,384]{1,0:T(8,128)(2,1)S(1)}, u32[]{:S(2)}, u32[]{:S(2)}) collective-permute-start(bf16[256,384]{1,0:T(8,128)(2,1)S(1)} %slice.76), channel_id=1, source_target_pairs={{0,128},{128,256},{256,384},{384,0},{1,129},{129,257},{257,385},{3... | collective-permute-start | bytes 589832 | tf_op jit(solution)/shard_map/ppermute | solution.py:40
  37.9 0.0 copy-done.2
  37.9 0.2 compare_reduce_fusion.2
  38.0 0.0 collective-permute-done
  38.1 3.9 %collective-permute-start.3 = (bf16[256,384]{1,0:T(8,128)(2,1)S(1)}, bf16[256,384]{1,0:T(8,128)(2,1)S(1)}, u32[]{:S(2)}, u32[]{:S(2)}) collective-permute-start(bf16[256,384]{1,0:T(8,128)(2,1)S(1)} %slice.77), channel_id=1, source_target_pairs={{0,384},{128,0},{256,128},{384,256},{1,385},{129,1},{257,129},{385... | collective-permute-start | bytes 589832 | tf_op jit(solution)/shard_map/ppermute | solution.py:41
  42.0 0.6 collective-permute-done.5
  42.7 5.6 %collective-permute-start.6 = (bf16[256,384]{1,0:T(8,128)(2,1)S(1)}, bf16[256,384]{1,0:T(8,128)(2,1)S(1)}, u32[]{:S(2)}, u32[]{:S(2)}) collective-permute-start(bf16[256,384]{1,0:T(8,128)(2,1)S(1)} %slice.78), channel_id=1, source_target_pairs={{0,128},{128,256},{256,384},{384,0},{1,129},{129,257},{257,385},{3... | collective-permute-start | bytes 589832 | tf_op jit(solution)/shard_map/ppermute | solution.py:40
  48.3 0.0 collective-permute-done.4
  48.3 1.9 %collective-permute-start.7 = (bf16[256,384]{1,0:T(8,128)(2,1)S(1)}, bf16[256,384]{1,0:T(8,128)(2,1)S(1)}, u32[]{:S(2)}, u32[]{:S(2)}) collective-permute-start(bf16[256,384]{1,0:T(8,128)(2,1)S(1)} %slice.79), channel_id=1, source_target_pairs={{0,384},{128,0},{256,128},{384,256},{1,385},{129,1},{257,129},{385... | collective-permute-start | bytes 589832 | tf_op jit(solution)/shard_map/ppermute | solution.py:41
  50.3 1.0 constant_dynamic-update-slice_fusion.3
  51.2 0.0 collective-permute-done.2
  51.2 0.8 constant_dynamic-update-slice_fusion.2
  52.0 0.0 collective-permute-done.3
  52.0 0.8 constant_dynamic-update-slice_fusion.1
  52.8 1.0 constant_dynamic-update-slice_fusion
  53.8 1.9 %collective-permute-start.8 = (bf16[2048,384]{1,0:T(8,128)(2,1)}, bf16[2048,384]{1,0:T(8,128)(2,1)S(1)}, u32[]{:S(2)}, u32[]{:S(2)}) collective-permute-start(bf16[2048,384]{1,0:T(8,128)(2,1)} %get-tuple-element.26), channel_id=1, source_target_pairs={{0,32},{32,0},{1,33},{33,1},{2,34},{34,2},{3,35},{35,3},{4,36},{36... | collective-permute-start | bytes 4718600 | tf_op jit(solution)/shard_map/ppermute | solution.py:84
  55.7 0.8 constant_dynamic-update-slice_fusion.16
  56.5 0.0 copy-done.1
  56.5 0.9 constant_dynamic-update-slice_fusion.8
  57.4 0.0 collective-permute-done.6
  57.4 0.7 constant_dynamic-update-slice_fusion.7
  58.1 0.0 collective-permute-done.7
  58.1 0.7 constant_dynamic-update-slice_fusion.6
  58.9 0.9 constant_dynamic-update-slice_fusion.5
  59.7 2.4 %collective-permute-start.9 = (bf16[2048,384]{1,0:T(8,128)(2,1)S(1)}, bf16[2048,384]{1,0:T(8,128)(2,1)S(1)}, u32[]{:S(2)}, u32[]{:S(2)}) collective-permute-start(bf16[2048,384]{1,0:T(8,128)(2,1)S(1)} %get-tuple-element.22), channel_id=1, source_target_pairs={{0,32},{32,0},{1,33},{33,1},{2,34},{34,2},{3,35},{35,3},{4,36},{36... | collective-permute-start | bytes 4718600 | tf_op jit(solution)/shard_map/ppermute | solution.py:85
  62.1 0.1 compare_and_fusion
  62.3 0.0 collective-permute-done.8
  62.3 1.3 constant_dynamic-update-slice_fusion.11
  63.6 1.5 collective-permute-done.9
  65.1 1.3 constant_dynamic-update-slice_fusion.10
  66.4 17.6 %gather_fusion = bf16[4096,384]{1,0:T(8,128)(2,1)S(1)} fusion(bf16[8192,384]{1,0:T(8,128)(2,1)} %constant_dynamic-update-slice_fusion.10, s32[4096]{0:T(1024)S(1)} %broadcast_clamp_fusion.1), kind=kCustom, calls=%fused_computation.clone | custom fusion | bytes 6307840 | tf_op jit(solution)/shard_map/jit(_take)/gather | solution.py:98
  84.1 20.3 %gather_fusion.1 = bf16[4096,384]{1,0:T(8,128)(2,1)} fusion(bf16[8192,384]{1,0:T(8,128)(2,1)} %constant_dynamic-update-slice_fusion.10, s32[4096]{0:T(1024)S(1)} %broadcast_clamp_fusion), kind=kCustom, calls=%fused_computation.1.clone | custom fusion | bytes 6307840 | tf_op jit(solution)/shard_map/jit(_take)/gather | solution.py:99
  104.4 8.6 %fusion = (f32[4096]{0:T(1024)S(1)}, f32[4096]{0:T(1024)S(1)}, bf16[4096,384]{1,0:T(8,128)(2,1)S(1)}) fusion(pred[4096]{0:T(1024)(128)(4,1)S(1)} %get-tuple-element.10, pred[4096]{0:T(1024)(128)(4,1)S(1)} %get-tuple-element.9, bf16[4096,384]{1,0:T(8,128)(2,1)} %gather_fusion.1, pred[4096]{0:T(1024)(128)(4,1)S(1)} %get-tuple-element.18, ...), kind=kLoop, calls=%fused_computation.9 | loop fusion | flops 28303360 | bytes 9490432 | tf_op jit(solution)/shard_map/reduce_sum | solution.py:105
  113.2 1.2 fusion.6
  114.5 0.6 concatenate.17
  115.1 52.1 %all_to_all.5 = bf16[32,144,128]{2,1,0:T(8,128)(2,1)S(1)} all-to-all(bf16[32,144,128]{2,1,0:T(8,128)(2,1)S(1)} %concatenate.17), channel_id=1, replica_groups=mesh['x'=4,'zh'=2,'c'=2,'y'=8,'zl'=4] {'y','zl'}, dimensions={0} | all-to-all | bytes 2359296 | tf_op jit(solution)/shard_map/all_to_all | solution.py:126
  167.3 0.1 fusion.40
  167.4 0.2 convert_reduce_fusion.1
  167.6 0.9 fusion.9
  (24 shorter events, 0.3 us)
Async XLA Ops:
  0.0 35.7 %copy-start = (bf16[384,128]{1,0:T(8,128)(2,1)S(1)}, bf16[384,128]{1,0:T(8,128)(2,1)}, u32[]{:S(2)}) copy-start(bf16[384,128]{1,0:T(8,128)(2,1)} %param.6) | copy-start | bytes 294916
  0.0 37.9 %copy-start.2 = (s32[3,4096]{1,0:T(4,128)S(1)}, s32[3,4096]{1,0:T(4,128)}, u32[]{:S(2)}) copy-start(s32[3,4096]{1,0:T(4,128)} %param.7) | copy-start | bytes 147460
  0.0 38.0 %collective-permute-start = (bf16[512,384]{1,0:T(8,128)(2,1)}, bf16[512,384]{1,0:T(8,128)(2,1)S(1)}, u32[]{:S(2)}, u32[]{:S(2)}) collective-permute-start(bf16[512,384]{1,0:T(8,128)(2,1)} %param.5), channel_id=1, source_target_pairs={{0,384},{128,0},{256,128},{384,256},{1,385},{129,1},{257,129},{385... | collective-permute-start | bytes 1179656 | tf_op jit(solution)/shard_map/ppermute | solution.py:38
  2.9 32.9 %collective-permute-start.1 = (bf16[512,384]{1,0:T(8,128)(2,1)}, bf16[512,384]{1,0:T(8,128)(2,1)S(1)}, u32[]{:S(2)}, u32[]{:S(2)}) collective-permute-start(bf16[512,384]{1,0:T(8,128)(2,1)} %param.5), channel_id=1, source_target_pairs={{0,128},{128,256},{256,384},{384,0},{1,129},{129,257},{257,385},{3... | collective-permute-start | bytes 1179656 | tf_op jit(solution)/shard_map/ppermute | solution.py:37
  26.7 21.6 %collective-permute-start.4 = (bf16[512,384]{1,0:T(8,128)(2,1)S(1)}, bf16[512,384]{1,0:T(8,128)(2,1)S(1)}, u32[]{:S(2)}, u32[]{:S(2)}) collective-permute-start(bf16[512,384]{1,0:T(8,128)(2,1)S(1)} %get-tuple-element.21), channel_id=1, source_target_pairs={{0,384},{128,0},{256,128},{384,256},{1,385},{129,1},{257,129},{385... | collective-permute-start | bytes 1179656 | tf_op jit(solution)/shard_map/ppermute | solution.py:38
  28.6 14.1 %collective-permute-start.5 = (bf16[512,384]{1,0:T(8,128)(2,1)S(1)}, bf16[512,384]{1,0:T(8,128)(2,1)S(1)}, u32[]{:S(2)}, u32[]{:S(2)}) collective-permute-start(bf16[512,384]{1,0:T(8,128)(2,1)S(1)} %get-tuple-element.21), channel_id=1, source_target_pairs={{0,128},{128,256},{256,384},{384,0},{1,129},{129,257},{257,385},{3... | collective-permute-start | bytes 1179656 | tf_op jit(solution)/shard_map/ppermute | solution.py:37
  35.8 20.8 %copy-start.1 = (bf16[2048,384]{1,0:T(8,128)(2,1)S(1)}, bf16[2048,384]{1,0:T(8,128)(2,1)}, u32[]{:S(2)}) copy-start(bf16[2048,384]{1,0:T(8,128)(2,1)} %get-tuple-element.20) | copy-start | bytes 4718596
  35.8 15.4 %collective-permute-start.2 = (bf16[256,384]{1,0:T(8,128)(2,1)S(1)}, bf16[256,384]{1,0:T(8,128)(2,1)S(1)}, u32[]{:S(2)}, u32[]{:S(2)}) collective-permute-start(bf16[256,384]{1,0:T(8,128)(2,1)S(1)} %slice.76), channel_id=1, source_target_pairs={{0,128},{128,256},{256,384},{384,0},{1,129},{129,257},{257,385},{3... | collective-permute-start | bytes 589832 | tf_op jit(solution)/shard_map/ppermute | solution.py:40
  38.1 14.0 %collective-permute-start.3 = (bf16[256,384]{1,0:T(8,128)(2,1)S(1)}, bf16[256,384]{1,0:T(8,128)(2,1)S(1)}, u32[]{:S(2)}, u32[]{:S(2)}) collective-permute-start(bf16[256,384]{1,0:T(8,128)(2,1)S(1)} %slice.77), channel_id=1, source_target_pairs={{0,384},{128,0},{256,128},{384,256},{1,385},{129,1},{257,129},{385... | collective-permute-start | bytes 589832 | tf_op jit(solution)/shard_map/ppermute | solution.py:41
  42.7 14.7 %collective-permute-start.6 = (bf16[256,384]{1,0:T(8,128)(2,1)S(1)}, bf16[256,384]{1,0:T(8,128)(2,1)S(1)}, u32[]{:S(2)}, u32[]{:S(2)}) collective-permute-start(bf16[256,384]{1,0:T(8,128)(2,1)S(1)} %slice.78), channel_id=1, source_target_pairs={{0,128},{128,256},{256,384},{384,0},{1,129},{129,257},{257,385},{3... | collective-permute-start | bytes 589832 | tf_op jit(solution)/shard_map/ppermute | solution.py:40
  48.3 9.8 %collective-permute-start.7 = (bf16[256,384]{1,0:T(8,128)(2,1)S(1)}, bf16[256,384]{1,0:T(8,128)(2,1)S(1)}, u32[]{:S(2)}, u32[]{:S(2)}) collective-permute-start(bf16[256,384]{1,0:T(8,128)(2,1)S(1)} %slice.79), channel_id=1, source_target_pairs={{0,384},{128,0},{256,128},{384,256},{1,385},{129,1},{257,129},{385... | collective-permute-start | bytes 589832 | tf_op jit(solution)/shard_map/ppermute | solution.py:41
  53.8 8.5 %collective-permute-start.8 = (bf16[2048,384]{1,0:T(8,128)(2,1)}, bf16[2048,384]{1,0:T(8,128)(2,1)S(1)}, u32[]{:S(2)}, u32[]{:S(2)}) collective-permute-start(bf16[2048,384]{1,0:T(8,128)(2,1)} %get-tuple-element.26), channel_id=1, source_target_pairs={{0,32},{32,0},{1,33},{33,1},{2,34},{34,2},{3,35},{35,3},{4,36},{36... | collective-permute-start | bytes 4718600 | tf_op jit(solution)/shard_map/ppermute | solution.py:84
  59.7 5.4 %collective-permute-start.9 = (bf16[2048,384]{1,0:T(8,128)(2,1)S(1)}, bf16[2048,384]{1,0:T(8,128)(2,1)S(1)}, u32[]{:S(2)}, u32[]{:S(2)}) collective-permute-start(bf16[2048,384]{1,0:T(8,128)(2,1)S(1)} %get-tuple-element.22), channel_id=1, source_target_pairs={{0,32},{32,0},{1,33},{33,1},{2,34},{34,2},{3,35},{35,3},{4,36},{36... | collective-permute-start | bytes 4718600 | tf_op jit(solution)/shard_map/ppermute | solution.py:85

commit v9 on v7

--- a/solution.py
+++ b/solution.py
@@ -69,7 +69,9 @@
     sample_count = residuals.shape[0] * n_samp
 
     rows = lax.all_gather(tier_one, "zh", axis=0, tiled=True)
-    rows = ring_gather(rows, "x", n_x)
+    rows = lax.all_to_all(
+        jnp.broadcast_to(rows[None], (n_x,) + rows.shape), "x", 0, 0, tiled=False
+    ).reshape(n_x * rows.shape[0], rows.shape[1])
     other = lax.ppermute(rows, "c", perm=[(0, 1), (1, 0)])
     rows = jnp.concatenate([rows, other], axis=0)
     my_c = lax.axis_index("c")
@@ -79,8 +81,7 @@
         f, r = g // local_rows, g % local_rows
         x, zh, c = f // (2 * n_zh), (f // 2) % n_zh, f % 2
         half = (c != my_c).astype(jnp.int32)
-        x_slot = (x - my_x + n_x) % n_x
-        return ((half * n_x + x_slot) * n_zh + zh) * local_rows + r
+        return ((half * n_x + x) * n_zh + zh) * local_rows + r
 
     first = jnp.take(rows, position(pair_list[0]), axis=0)
     second = jnp.take(rows, position(pair_list[1]), axis=0)

time: 171 us -> 175 us (1.023)
  blocking collectives: 72.3 us -> 111 us
  waiting for transfers between devices: 26.1 us -> 5.32 us
  starting transfers between devices: 13.6 us -> 1.91 us
  local copies, waits for them, and re-layouts: 46.7 us -> 39 us
  other arithmetic: 9.33 us -> 14.5 us
    all_to_all x0 -> x1, blocking collectives: none -> 39.6 us  [per_device(): lax.all_to_all(jnp.broadcast_to(rows[None], (n_x,) + rows.shape), 'x', 0,...]
    ppermute x4 -> x0, waiting for transfers between devices: 20.7 us -> none  [the longest x1 14.7 us: ring_gather(): from_left = lax.ppermute(block, axis, perm=fwd)]
    ppermute x4 -> x0, starting transfers between devices: 11.7 us -> none  [the longest x1 3.46 us: ring_gather(): from_right = lax.ppermute(block, axis, perm=bwd)]
    concatenate x0 -> x1, other arithmetic: none -> 5.18 us  [per_device(): rows = jnp.concatenate([rows, other], axis=0)]
    unnamed x8 -> x4, local copies, waits for them, and re-layouts: 4.57 us -> 0.01 us
    concatenate x2 -> x0, local copies, waits for them, and re-layouts: 3.36 us -> none  [the longest x1 2.02 us: per_device(): rows = jnp.concatenate([rows, other], axis=0)]
    gather x1, local copies, waits for them, and re-layouts: 17.6 us -> 20.3 us  [per_device(): first = jnp.take(rows, position(pair_list[0]), axis=0)]
    gather x1, local copies, waits for them, and re-layouts: 20.3 us -> 17.6 us  [per_device(): second = jnp.take(rows, position(pair_list[1]), axis=0)]
  transfers between devices with their start and end apart: 5 -> 1, of which waited for: 4 -> 1; matrix products, arithmetic and copies ran while one was open for 2% -> 0% of each run, Pallas kernels for 0% -> 0%
where the time goes in v9:
time: 175 us; the launch traced here: 174 us
  blocking collectives  111 us (63%)
  local copies, waits for them, and re-layouts  39 us (22%)
  other arithmetic  14.5 us (8%)
  waiting for transfers between devices  5.32 us (3%)
  matrix products  2.12 us (1%)
  starting transfers between devices  1.91 us (1%)
    all_to_all x1, blocking collectives, per_device(): arrived = lax.all_to_all(packed, SAMP_AXES, 0, 0, tiled=False)  52 us
    all_to_all x1, blocking collectives, per_device(): lax.all_to_all(jnp.broadcast_to(rows[None], (n_x,) + rows.shape), 'x', 0,...  39.6 us
    gather x1, local copies, waits for them, and re-layouts, per_device(): first = jnp.take(rows, position(pair_list[0]), axis=0)  20.3 us
    all_gather x1, blocking collectives, per_device(): rows = lax.all_gather(tier_one, 'zh', axis=0, tiled=True)  19.2 us
    gather x1, local copies, waits for them, and re-layouts, per_device(): second = jnp.take(rows, position(pair_list[1]), axis=0)  17.6 us
    reduce_sum x1, other arithmetic, per_device(): square_sums = jnp.sum(widened * widened, axis=1)  8.6 us
    ppermute x1, waiting for transfers between devices, per_device(): other = lax.ppermute(rows, 'c', perm=[(0, 1), (1, 0)])  5.32 us
    concatenate x1, other arithmetic, per_device(): rows = jnp.concatenate([rows, other], axis=0)  5.18 us
  transfers between devices with their start and end apart: 1, of which 1 were waited for; matrix products, arithmetic and copies ran while one was open for 0% of the time, Pallas kernels for 0%

profile of v9, /device:TPU:6, one launch (start us, length us, event | category | flops | bytes accessed | tf_op | source)
XLA Modules:
  0.0 173.8 jit_solution(7513708258728204088)
XLA Ops:
  0.0 19.2 %all_gather.3 = bf16[1024,384]{1,0:T(8,128)(2,1)S(1)} all-gather(bf16[512,384]{1,0:T(8,128)(2,1)} %param.5), channel_id=1, replica_groups=mesh['x'=4,'zh'=2,'c'=2,'y'=8,'zl'=4] {'zh'}, dimensions={0}, use_global_device_ids=true | all-gather | bytes 1179648 | tf_op jit(solution)/shard_map/all_gather | solution.py:71
  19.2 0.3 broadcast_in_dim.46
  19.5 0.0 copy-start
  19.5 0.0 copy-start.1
  19.5 39.6 %all_to_all.10 = bf16[4,1024,384]{2,1,0:T(8,128)(2,1)S(1)} all-to-all(bf16[4,1024,384]{2,1,0:T(8,128)(2,1)S(1)} %broadcast_in_dim.46), channel_id=1, replica_groups=mesh['x'=4,'zh'=2,'c'=2,'y'=8,'zl'=4] {'x'}, dimensions={0} | all-to-all | bytes 6291456 | tf_op jit(solution)/shard_map/all_to_all | solution.py:72
  59.1 1.9 %collective-permute-start = (bf16[4096,384]{1,0:T(8,128)(2,1)S(1)}, bf16[4096,384]{1,0:T(8,128)(2,1)}, u32[]{:S(2)}, u32[]{:S(2)}) collective-permute-start(bf16[4096,384]{1,0:T(8,128)(2,1)S(1)} %bitcast.24), channel_id=1, source_target_pairs={{0,32},{32,0},{1,33},{33,1},{2,34},{34,2},{3,35},{35,3},{4,36},{36... | collective-permute-start | bytes 9437192 | tf_op jit(solution)/shard_map/ppermute | solution.py:75
  61.0 0.0 copy-done
  61.0 0.1 convert_reduce_fusion.2
  61.1 0.0 copy-done.1
  61.1 0.2 compare_reduce_fusion.2
  61.3 0.1 compare_and_fusion
  61.4 5.3 %collective-permute-done = bf16[4096,384]{1,0:T(8,128)(2,1)} collective-permute-done((bf16[4096,384]{1,0:T(8,128)(2,1)S(1)}, bf16[4096,384]{1,0:T(8,128)(2,1)}, u32[]{:S(2)}, u32[]{:S(2)}) %collective-permute-start) | collective-permute-done | bytes 3145760 | tf_op jit(solution)/shard_map/ppermute | solution.py:75
  66.8 5.2 %pad_maximum_fusion = bf16[8192,384]{1,0:T(8,128)(2,1)} fusion(bf16[4096,384]{1,0:T(8,128)(2,1)} %collective-permute-done, bf16[4096,384]{1,0:T(8,128)(2,1)S(1)} %bitcast.25), kind=kLoop, calls=%fused_computation.14 | loop fusion | flops 12582912 | bytes 12582912 | tf_op jit(solution)/shard_map/concatenate | solution.py:76
  71.9 17.6 %gather_fusion.1 = bf16[4096,384]{1,0:T(8,128)(2,1)S(1)} fusion(bf16[8192,384]{1,0:T(8,128)(2,1)} %pad_maximum_fusion, s32[4096]{0:T(1024)S(1)} %broadcast_clamp_fusion), kind=kCustom, calls=%fused_computation.1.clone | custom fusion | bytes 6307840 | tf_op jit(solution)/shard_map/jit(_take)/gather | solution.py:87
  89.6 20.3 %gather_fusion = bf16[4096,384]{1,0:T(8,128)(2,1)} fusion(bf16[8192,384]{1,0:T(8,128)(2,1)} %pad_maximum_fusion, s32[4096]{0:T(1024)S(1)} %broadcast_clamp_fusion.1), kind=kCustom, calls=%fused_computation.clone | custom fusion | bytes 6307840 | tf_op jit(solution)/shard_map/jit(_take)/gather | solution.py:86
  109.9 8.6 %fusion = (f32[4096]{0:T(1024)S(1)}, f32[4096]{0:T(1024)S(1)}, bf16[4096,384]{1,0:T(8,128)(2,1)S(1)}) fusion(pred[4096]{0:T(1024)(128)(4,1)S(1)} %get-tuple-element.10, pred[4096]{0:T(1024)(128)(4,1)S(1)} %get-tuple-element.9, bf16[4096,384]{1,0:T(8,128)(2,1)S(1)} %gather_fusion.1, pred[4096]{0:T(1024)(128)(4,1)S(1)} %get-tuple-element.18, ...), kind=kLoop, calls=%fused_computation.9 | loop fusion | flops 28303360 | bytes 9490432 | tf_op jit(solution)/shard_map/reduce_sum | solution.py:93
  118.6 1.2 fusion.6
  119.9 0.6 concatenate.8
  120.5 52.0 %all_to_all.11 = bf16[32,144,128]{2,1,0:T(8,128)(2,1)S(1)} all-to-all(bf16[32,144,128]{2,1,0:T(8,128)(2,1)S(1)} %concatenate.8), channel_id=1, replica_groups=mesh['x'=4,'zh'=2,'c'=2,'y'=8,'zl'=4] {'y','zl'}, dimensions={0} | all-to-all | bytes 2359296 | tf_op jit(solution)/shard_map/all_to_all | solution.py:114
  172.6 0.1 fusion.36
  172.7 0.2 convert_reduce_fusion.1
  172.9 0.9 fusion.9
  (20 shorter events, 0.2 us)
Async XLA Ops:
  19.5 41.6 %copy-start = (bf16[384,128]{1,0:T(8,128)(2,1)S(1)}, bf16[384,128]{1,0:T(8,128)(2,1)}, u32[]{:S(2)}) copy-start(bf16[384,128]{1,0:T(8,128)(2,1)} %param.6) | copy-start | bytes 294916
  19.5 41.6 %copy-start.1 = (s32[3,4096]{1,0:T(4,128)S(1)}, s32[3,4096]{1,0:T(4,128)}, u32[]{:S(2)}) copy-start(s32[3,4096]{1,0:T(4,128)} %param.7) | copy-start | bytes 147460
  59.1 7.7 %collective-permute-start = (bf16[4096,384]{1,0:T(8,128)(2,1)S(1)}, bf16[4096,384]{1,0:T(8,128)(2,1)}, u32[]{:S(2)}, u32[]{:S(2)}) collective-permute-start(bf16[4096,384]{1,0:T(8,128)(2,1)S(1)} %bitcast.24), channel_id=1, source_target_pairs={{0,32},{32,0},{1,33},{33,1},{2,34},{34,2},{3,35},{35,3},{4,36},{36... | collective-permute-start | bytes 9437192 | tf_op jit(solution)/shard_map/ppermute | solution.py:75

commit v10 on v7

--- a/solution.py
+++ b/solution.py
@@ -2,6 +2,8 @@
 
 import jax
 import jax.numpy as jnp
+from jax.experimental import pallas as pl
+from jax.experimental.pallas import tpu as pltpu
 import numpy as np
 from jax import lax
 from jax.sharding import Mesh
@@ -12,6 +14,7 @@
 FEAT_AXES = ("x", "zh", "c")
 SAMP_AXES = ("y", "zl")
 EXTRA_ROWS = 16
+GATHER_TILE = 512
 
 
 def combine_rows(first_rows, second_rows, operator_id):
@@ -28,6 +31,43 @@
         ),
     )
     return built.astype(jnp.bfloat16)
+
+
+def gather_kernel(first_ref, second_ref, table_ref, op_ref, out_ref, first_buf, second_buf):
+    tile = first_buf.shape[0]
+    base = pl.program_id(0) * tile
+    def body(j, carry):
+        a = first_ref[base + j]
+        b = second_ref[base + j]
+        first_buf[pl.ds(j, 1), :] = table_ref[pl.ds(a, 1), :]
+        second_buf[pl.ds(j, 1), :] = table_ref[pl.ds(b, 1), :]
+        return carry
+    lax.fori_loop(0, tile, body, 0, unroll=8)
+    out_ref[...] = combine_rows(first_buf[...], second_buf[...], op_ref[...])
+
+def build_descriptors(table, first_pos, second_pos, operator_id):
+    n_rows, width = table.shape
+    pairs = first_pos.shape[0]
+    tile = min(GATHER_TILE, pairs)
+    grid_spec = pltpu.PrefetchScalarGridSpec(
+        num_scalar_prefetch=2,
+        grid=(pairs // tile,),
+        in_specs=[
+            pl.BlockSpec((n_rows, width), lambda i, p1, p2: (0, 0)),
+            pl.BlockSpec((tile, 1), lambda i, p1, p2: (i, 0)),
+        ],
+        out_specs=pl.BlockSpec((tile, width), lambda i, p1, p2: (i, 0)),
+        scratch_shapes=[pltpu.VMEM((tile, width), jnp.float32)] * 2,
+    )
+    return pl.pallas_call(
+        gather_kernel,
+        grid_spec=grid_spec,
+        out_shape=jax.ShapeDtypeStruct((pairs, width), jnp.bfloat16),
+        compiler_params=pltpu.CompilerParams(vmem_limit_bytes=60 * 1024 * 1024),
+        cost_estimate=pl.CostEstimate(
+            flops=10 * pairs * width, transcendentals=0,
+            bytes_accessed=n_rows * width * 4 + pairs * width * 2),
+    )(first_pos, second_pos, table.astype(jnp.float32), operator_id[:, None])
 
 
 def ring_gather(block, axis, n):
@@ -82,9 +122,9 @@
         x_slot = (x - my_x + n_x) % n_x
         return ((half * n_x + x_slot) * n_zh + zh) * local_rows + r
 
-    first = jnp.take(rows, position(pair_list[0]), axis=0)
-    second = jnp.take(rows, position(pair_list[1]), axis=0)
-    built = combine_rows(first, second, pair_list[2][:, None])
+    built = build_descriptors(
+        rows, position(pair_list[0]), position(pair_list[1]), pair_list[2]
+    )
 
     product = jnp.dot(built, residuals, preferred_element_type=jnp.float32)
     widened = built.astype(jnp.float32)

time: 171 us -> 170 us (level)
  local copies, waits for them, and re-layouts: 46.7 us -> 10.7 us
  Pallas kernels: 0 us -> 34.8 us
  other arithmetic: 9.33 us -> 12.6 us
  waiting for transfers between devices: 26.1 us -> 23.6 us
    gather x2 -> x0, local copies, waits for them, and re-layouts: 37.9 us -> none  [the longest x1 20.3 us: per_device(): second = jnp.take(rows, position(pair_list[1]), axis=0)]
    pallas_call x0 -> x1, Pallas kernels: none -> 34.8 us  [build_descriptors(): pl.pallas_call(gather_kernel, grid_spec=grid_spec, out_shape=jax.ShapeDty...]
    convert_element_type x0 -> x1, other arithmetic: none -> 8.16 us  [build_descriptors(): table.astype(jnp.float32)]
    reduce_sum x1, other arithmetic: 8.61 us -> 3.29 us  [per_device(): square_sums = jnp.sum(widened * widened, axis=1)]
    ppermute x1, waiting for transfers between devices: 5.39 us -> 3.03 us  [per_device(): other = lax.ppermute(rows, 'c', perm=[(0, 1), (1, 0)])]
    another operation x6 -> x8, local copies, waits for them, and re-layouts: 0.09 us -> 2.08 us  [the longest x2 1.99 us: build_descriptors(): operator_id[:, None]]
    unnamed x8 -> x10, local copies, waits for them, and re-layouts: 4.57 us -> 4.65 us
  transfers between devices with their start and end apart: 5 -> 5, of which waited for: 4 -> 4; matrix products, arithmetic and copies ran while one was open for 2% -> 4% of each run, Pallas kernels for 0% -> 0%
where the time goes in v10:
time: 170 us
  blocking collectives  72.3 us (43%)
  Pallas kernels  34.8 us (20%)
  waiting for transfers between devices  23.6 us (14%)
  starting transfers between devices  13.6 us (8%)
  other arithmetic  12.6 us (7%)
  local copies, waits for them, and re-layouts  10.7 us (6%)
  matrix products  2.12 us (1%)
    all_to_all x1, blocking collectives, per_device(): arrived = lax.all_to_all(packed, SAMP_AXES, 0, 0, tiled=False)  53.1 us
    pallas_call x1, Pallas kernels, build_descriptors(): pl.pallas_call(gather_kernel, grid_spec=grid_spec, out_shape=jax.ShapeDty...  34.8 us
    all_gather x1, blocking collectives, per_device(): rows = lax.all_gather(tier_one, 'zh', axis=0, tiled=True)  19.2 us
    ppermute x1, waiting for transfers between devices, ring_gather(): from_left = lax.ppermute(block, axis, perm=fwd)  14.7 us
    convert_element_type x1, other arithmetic, build_descriptors(): table.astype(jnp.float32)  8.16 us
    unnamed x10, local copies, waits for them, and re-layouts  4.65 us
    ppermute x1, starting transfers between devices, ring_gather(): from_right = lax.ppermute(block, axis, perm=bwd)  3.46 us
    ppermute x1, starting transfers between devices, ring_gather(): far_a = lax.ppermute(from_left[:half], axis, perm=fwd)  3.41 us
  transfers between devices with their start and end apart: 5, of which 4 were waited for; matrix products, arithmetic and copies ran while one was open for 4% of the time, Pallas kernels for 0%

profile of v10, /device:TPU:6, one launch (start us, length us, event | category | flops | bytes accessed | tf_op | source)
XLA Modules:
  0.0 170.0 jit_solution(14591525258476179108)
XLA Ops:
  0.0 19.2 %all_gather.3 = bf16[1024,384]{1,0:T(8,128)(2,1)S(1)} all-gather(bf16[512,384]{1,0:T(8,128)(2,1)} %param.3), channel_id=1, replica_groups=mesh['x'=4,'zh'=2,'c'=2,'y'=8,'zl'=4] {'zh'}, dimensions={0}, use_global_device_ids=true | all-gather | bytes 1179648 | tf_op jit(solution)/shard_map/all_gather | solution.py:111
  19.2 2.4 %collective-permute-start.1 = (bf16[1024,384]{1,0:T(8,128)(2,1)S(1)}, bf16[1024,384]{1,0:T(8,128)(2,1)S(1)}, u32[]{:S(2)}, u32[]{:S(2)}) collective-permute-start(bf16[1024,384]{1,0:T(8,128)(2,1)S(1)} %all_gather.3), channel_id=1, source_target_pairs={{0,128},{128,256},{256,384},{384,0},{1,129},{129,257},{257,385},{3... | collective-permute-start | bytes 2359304 | tf_op jit(solution)/shard_map/ppermute | solution.py:77
  21.6 3.5 %collective-permute-start = (bf16[1024,384]{1,0:T(8,128)(2,1)S(1)}, bf16[1024,384]{1,0:T(8,128)(2,1)S(1)}, u32[]{:S(2)}, u32[]{:S(2)}) collective-permute-start(bf16[1024,384]{1,0:T(8,128)(2,1)S(1)} %all_gather.3), channel_id=1, source_target_pairs={{0,384},{128,0},{256,128},{384,256},{1,385},{129,1},{257,129},{385... | collective-permute-start | bytes 2359304 | tf_op jit(solution)/shard_map/ppermute | solution.py:78
  25.0 14.7 %collective-permute-done.1 = bf16[1024,384]{1,0:T(8,128)(2,1)S(1)} collective-permute-done((bf16[1024,384]{1,0:T(8,128)(2,1)S(1)}, bf16[1024,384]{1,0:T(8,128)(2,1)S(1)}, u32[]{:S(2)}, u32[]{:S(2)}) %collective-permute-start.1) | collective-permute-done | bytes 786464 | tf_op jit(solution)/shard_map/ppermute | solution.py:77
  39.8 3.4 %collective-permute-start.2 = (bf16[512,384]{1,0:T(8,128)(2,1)S(1)}, bf16[512,384]{1,0:T(8,128)(2,1)S(1)}, u32[]{:S(2)}, u32[]{:S(2)}) collective-permute-start(bf16[512,384]{1,0:T(8,128)(2,1)S(1)} %slice.64), channel_id=1, source_target_pairs={{0,128},{128,256},{256,384},{384,0},{1,129},{129,257},{257,385},{3... | collective-permute-start | bytes 1179656 | tf_op jit(solution)/shard_map/ppermute | solution.py:80
  43.2 0.0 collective-permute-done
  43.3 2.4 %collective-permute-start.3 = (bf16[512,384]{1,0:T(8,128)(2,1)S(1)}, bf16[512,384]{1,0:T(8,128)(2,1)S(1)}, u32[]{:S(2)}, u32[]{:S(2)}) collective-permute-start(bf16[512,384]{1,0:T(8,128)(2,1)S(1)} %slice.65), channel_id=1, source_target_pairs={{0,384},{128,0},{256,128},{384,256},{1,385},{129,1},{257,129},{385... | collective-permute-start | bytes 1179656 | tf_op jit(solution)/shard_map/ppermute | solution.py:81
  45.7 1.4 constant_dynamic-update-slice_fusion.4
  47.1 0.0 copy-start.2
  47.1 1.3 constant_dynamic-update-slice_fusion.3
  48.4 2.6 %collective-permute-done.2 = bf16[512,384]{1,0:T(8,128)(2,1)S(1)} collective-permute-done((bf16[512,384]{1,0:T(8,128)(2,1)S(1)}, bf16[512,384]{1,0:T(8,128)(2,1)S(1)}, u32[]{:S(2)}, u32[]{:S(2)}) %collective-permute-start.2) | collective-permute-done | bytes 393248 | tf_op jit(solution)/shard_map/ppermute | solution.py:80
  51.0 1.0 constant_dynamic-update-slice_fusion.2
  52.0 0.0 copy-start.1
  52.0 3.3 %collective-permute-done.3 = bf16[512,384]{1,0:T(8,128)(2,1)S(1)} collective-permute-done((bf16[512,384]{1,0:T(8,128)(2,1)S(1)}, bf16[512,384]{1,0:T(8,128)(2,1)S(1)}, u32[]{:S(2)}, u32[]{:S(2)}) %collective-permute-start.3) | collective-permute-done | bytes 393248 | tf_op jit(solution)/shard_map/ppermute | solution.py:81
  55.2 1.0 constant_dynamic-update-slice_fusion.1
  56.2 1.3 constant_dynamic-update-slice_fusion
  57.5 1.9 %collective-permute-start.4 = (bf16[4096,384]{1,0:T(8,128)(2,1)}, bf16[4096,384]{1,0:T(8,128)(2,1)S(1)}, u32[]{:S(2)}, u32[]{:S(2)}) collective-permute-start(bf16[4096,384]{1,0:T(8,128)(2,1)} %get-tuple-element.11), channel_id=1, source_target_pairs={{0,32},{32,0},{1,33},{33,1},{2,34},{34,2},{3,35},{35,3},{4,36},{36... | collective-permute-start | bytes 9437192 | tf_op jit(solution)/shard_map/ppermute | solution.py:113
  59.5 0.0 copy-done.2
  59.5 2.0 %copy.5.op_ref = s32[4096,1]{1,0:T(8,128)} copy(s32[4096,1]{0,1:T(1,128)S(1)} %get-tuple-element.25) | data formatting | bytes 32768 | tf_op jit(solution)/shard_map/broadcast_in_dim;squeeze | solution.py:70
  61.5 0.0 copy-done.1
  61.5 0.1 convert_reduce_fusion.2
  61.5 0.7 fusion.16
  62.2 3.0 %collective-permute-done.4 = bf16[4096,384]{1,0:T(8,128)(2,1)S(1)} collective-permute-done((bf16[4096,384]{1,0:T(8,128)(2,1)}, bf16[4096,384]{1,0:T(8,128)(2,1)S(1)}, u32[]{:S(2)}, u32[]{:S(2)}) %collective-permute-start.4) | collective-permute-done | bytes 3145760 | tf_op jit(solution)/shard_map/ppermute | solution.py:113
  65.3 2.0 %constant_dynamic-update-slice_fusion.5 = bf16[8192,384]{1,0:T(8,128)(2,1)} fusion(bf16[8192,384]{1,0:T(8,128)(2,1)} %get-tuple-element.12, bf16[4096,384]{1,0:T(8,128)(2,1)S(1)} %collective-permute-done.4), kind=kLoop, calls=%fused_computation.55 | loop fusion | bytes 6291456 | tf_op jit(solution)/shard_map/concatenate | solution.py:114
  67.3 8.2 %convert_element_type.23.table_ref = f32[8192,384]{1,0:T(8,128)} convert(bf16[8192,384]{1,0:T(8,128)(2,1)} %constant_dynamic-update-slice_fusion.5) | non-fusion elementwise | flops 3145728 | bytes 18874368 | tf_op jit(solution)/shard_map/convert_element_type | solution.py:70
  75.4 34.8 %shard_map.37 = bf16[4096,384]{1,0:T(8,128)(2,1)} custom-call(s32[4096]{0:T(1024)} %get-tuple-element.39.first_ref, s32[4096]{0:T(1024)} %get-tuple-element.40.second_ref, f32[8192,384]{1,0:T(8,128)} %convert_element_type.23.table_ref, s32[4096,1]{1,0:T(8,128)} %copy.5.op_ref), custom_call_target="tpu_custom_call" | custom-call | flops 15728640 | bytes 15728640 | tf_op jit(solution)/shard_map/pallas_call | solution.py:62
  110.2 0.0 copy-start
  110.2 3.3 %fusion = (f32[4096]{0:T(1024)S(1)}, f32[4096]{0:T(1024)S(1)}) fusion(bf16[4096,384]{1,0:T(8,128)(2,1)} %shard_map.37), kind=kLoop, calls=%fused_computation.2 | loop fusion | flops 6283264 | bytes 3178496 | tf_op jit(solution)/shard_map/reduce_sum | solution.py:132
  113.5 0.0 copy-done
  113.5 1.2 fusion.1
  115.0 0.6 concatenate.13
  115.6 53.1 %all_to_all.5 = bf16[32,144,128]{2,1,0:T(8,128)(2,1)S(1)} all-to-all(bf16[32,144,128]{2,1,0:T(8,128)(2,1)S(1)} %concatenate.13), channel_id=1, replica_groups=mesh['x'=4,'zh'=2,'c'=2,'y'=8,'zl'=4] {'y','zl'}, dimensions={0} | all-to-all | bytes 2359296 | tf_op jit(solution)/shard_map/all_to_all | solution.py:153
  168.7 0.1 fusion.37
  168.9 0.2 convert_reduce_fusion.1
  169.1 0.9 fusion.4
  (20 shorter events, 0.3 us)
Async XLA Ops:
  19.2 20.6 %collective-permute-start.1 = (bf16[1024,384]{1,0:T(8,128)(2,1)S(1)}, bf16[1024,384]{1,0:T(8,128)(2,1)S(1)}, u32[]{:S(2)}, u32[]{:S(2)}) collective-permute-start(bf16[1024,384]{1,0:T(8,128)(2,1)S(1)} %all_gather.3), channel_id=1, source_target_pairs={{0,128},{128,256},{256,384},{384,0},{1,129},{129,257},{257,385},{3... | collective-permute-start | bytes 2359304 | tf_op jit(solution)/shard_map/ppermute | solution.py:77
  21.6 21.6 %collective-permute-start = (bf16[1024,384]{1,0:T(8,128)(2,1)S(1)}, bf16[1024,384]{1,0:T(8,128)(2,1)S(1)}, u32[]{:S(2)}, u32[]{:S(2)}) collective-permute-start(bf16[1024,384]{1,0:T(8,128)(2,1)S(1)} %all_gather.3), channel_id=1, source_target_pairs={{0,384},{128,0},{256,128},{384,256},{1,385},{129,1},{257,129},{385... | collective-permute-start | bytes 2359304 | tf_op jit(solution)/shard_map/ppermute | solution.py:78
  39.8 11.2 %collective-permute-start.2 = (bf16[512,384]{1,0:T(8,128)(2,1)S(1)}, bf16[512,384]{1,0:T(8,128)(2,1)S(1)}, u32[]{:S(2)}, u32[]{:S(2)}) collective-permute-start(bf16[512,384]{1,0:T(8,128)(2,1)S(1)} %slice.64), channel_id=1, source_target_pairs={{0,128},{128,256},{256,384},{384,0},{1,129},{129,257},{257,385},{3... | collective-permute-start | bytes 1179656 | tf_op jit(solution)/shard_map/ppermute | solution.py:80
  43.3 12.0 %collective-permute-start.3 = (bf16[512,384]{1,0:T(8,128)(2,1)S(1)}, bf16[512,384]{1,0:T(8,128)(2,1)S(1)}, u32[]{:S(2)}, u32[]{:S(2)}) collective-permute-start(bf16[512,384]{1,0:T(8,128)(2,1)S(1)} %slice.65), channel_id=1, source_target_pairs={{0,384},{128,0},{256,128},{384,256},{1,385},{129,1},{257,129},{385... | collective-permute-start | bytes 1179656 | tf_op jit(solution)/shard_map/ppermute | solution.py:81
  47.1 12.4 %copy-start.2 = (s32[3,4096]{1,0:T(4,128)S(1)}, s32[3,4096]{1,0:T(4,128)}, u32[]{:S(2)}) copy-start(s32[3,4096]{1,0:T(4,128)} %param.5) | copy-start | bytes 147460
  52.0 9.5 %copy-start.1 = (bf16[384,128]{1,0:T(8,128)(2,1)S(1)}, bf16[384,128]{1,0:T(8,128)(2,1)}, u32[]{:S(2)}) copy-start(bf16[384,128]{1,0:T(8,128)(2,1)} %param.4) | copy-start | bytes 294916
  57.5 7.8 %collective-permute-start.4 = (bf16[4096,384]{1,0:T(8,128)(2,1)}, bf16[4096,384]{1,0:T(8,128)(2,1)S(1)}, u32[]{:S(2)}, u32[]{:S(2)}) collective-permute-start(bf16[4096,384]{1,0:T(8,128)(2,1)} %get-tuple-element.11), channel_id=1, source_target_pairs={{0,32},{32,0},{1,33},{33,1},{2,34},{34,2},{3,35},{35,3},{4,36},{36... | collective-permute-start | bytes 9437192 | tf_op jit(solution)/shard_map/ppermute | solution.py:113
  110.2 3.3 %copy-start = (bf16[4096,384]{1,0:T(8,128)(2,1)S(1)}, bf16[4096,384]{1,0:T(8,128)(2,1)}, u32[]{:S(2)}) copy-start(bf16[4096,384]{1,0:T(8,128)(2,1)} %shard_map.37) | copy-start | bytes 9437188

commit v11 on v10

--- a/solution.py
+++ b/solution.py
@@ -33,17 +33,30 @@
     return built.astype(jnp.bfloat16)
 
 
-def gather_kernel(first_ref, second_ref, table_ref, op_ref, out_ref, first_buf, second_buf):
+def gather_kernel(first_ref, second_ref, table_ref, op_ref, out_ref, table, first_buf, second_buf):
     tile = first_buf.shape[0]
+    step = 256
+
+    @pl.when(pl.program_id(0) == 0)
+    def _():
+        def widen(i, carry):
+            rows = pl.ds(pl.multiple_of(i * step, step), step)
+            table[rows, :] = table_ref[rows, :].astype(jnp.float32)
+            return carry
+        lax.fori_loop(0, table.shape[0] // step, widen, 0)
+
     base = pl.program_id(0) * tile
+
     def body(j, carry):
         a = first_ref[base + j]
         b = second_ref[base + j]
-        first_buf[pl.ds(j, 1), :] = table_ref[pl.ds(a, 1), :]
-        second_buf[pl.ds(j, 1), :] = table_ref[pl.ds(b, 1), :]
+        first_buf[pl.ds(j, 1), :] = table[pl.ds(a, 1), :]
+        second_buf[pl.ds(j, 1), :] = table[pl.ds(b, 1), :]
         return carry
+
     lax.fori_loop(0, tile, body, 0, unroll=8)
     out_ref[...] = combine_rows(first_buf[...], second_buf[...], op_ref[...])
+
 
 def build_descriptors(table, first_pos, second_pos, operator_id):
     n_rows, width = table.shape
@@ -57,17 +70,20 @@
             pl.BlockSpec((tile, 1), lambda i, p1, p2: (i, 0)),
         ],
         out_specs=pl.BlockSpec((tile, width), lambda i, p1, p2: (i, 0)),
-        scratch_shapes=[pltpu.VMEM((tile, width), jnp.float32)] * 2,
+        scratch_shapes=[pltpu.VMEM((n_rows, width), jnp.float32)]
+        + [pltpu.VMEM((tile, width), jnp.float32)] * 2,
     )
     return pl.pallas_call(
         gather_kernel,
         grid_spec=grid_spec,
         out_shape=jax.ShapeDtypeStruct((pairs, width), jnp.bfloat16),
-        compiler_params=pltpu.CompilerParams(vmem_limit_bytes=60 * 1024 * 1024),
+        compiler_params=pltpu.CompilerParams(
+            dimension_semantics=("arbitrary",), vmem_limit_bytes=60 * 1024 * 1024
+        ),
         cost_estimate=pl.CostEstimate(
             flops=10 * pairs * width, transcendentals=0,
-            bytes_accessed=n_rows * width * 4 + pairs * width * 2),
-    )(first_pos, second_pos, table.astype(jnp.float32), operator_id[:, None])
+            bytes_accessed=n_rows * width * 2 + pairs * width * 2),
+    )(first_pos, second_pos, table, operator_id[:, None])
 
 
 def ring_gather(block, axis, n):

time: 170 us -> 162 us (0.953)
  other arithmetic: 12.6 us -> 4.42 us
    convert_element_type x1 -> x0, other arithmetic: 8.16 us -> none  [build_descriptors(): table.astype(jnp.float32)]
where the time goes in v11:
time: 162 us; the launch traced here: 161 us
  blocking collectives  72.3 us (45%)
  Pallas kernels  34 us (21%)
  waiting for transfers between devices  23.7 us (15%)
  starting transfers between devices  13.6 us (8%)
  local copies, waits for them, and re-layouts  10.8 us (7%)
  other arithmetic  4.42 us (3%)
  matrix products  2.11 us (1%)
    all_to_all x1, blocking collectives, per_device(): arrived = lax.all_to_all(packed, SAMP_AXES, 0, 0, tiled=False)  53.1 us
    pallas_call x1, Pallas kernels, build_descriptors(): pl.pallas_call(gather_kernel, grid_spec=grid_spec, out_shape=jax.ShapeDty...  34 us
    all_gather x1, blocking collectives, per_device(): rows = lax.all_gather(tier_one, 'zh', axis=0, tiled=True)  19.2 us
    ppermute x1, waiting for transfers between devices, ring_gather(): from_left = lax.ppermute(block, axis, perm=fwd)  14.7 us
    unnamed x10, local copies, waits for them, and re-layouts  4.57 us
    ppermute x1, starting transfers between devices, ring_gather(): from_right = lax.ppermute(block, axis, perm=bwd)  3.46 us
    ppermute x1, starting transfers between devices, ring_gather(): far_a = lax.ppermute(from_left[:half], axis, perm=fwd)  3.41 us
    reduce_sum x1, other arithmetic, per_device(): square_sums = jnp.sum(widened * widened, axis=1)  3.29 us
  transfers between devices with their start and end apart: 5, of which 4 were waited for; matrix products, arithmetic and copies ran while one was open for 4% of the time, Pallas kernels for 0%

profile of v11, /device:TPU:6, one launch (start us, length us, event | category | flops | bytes accessed | tf_op | source)
XLA Modules:
  0.0 161.2 jit_solution(6427573732778729924)
XLA Ops:
  0.0 19.2 %all_gather.3 = bf16[1024,384]{1,0:T(8,128)(2,1)S(1)} all-gather(bf16[512,384]{1,0:T(8,128)(2,1)} %param.3), channel_id=1, replica_groups=mesh['x'=4,'zh'=2,'c'=2,'y'=8,'zl'=4] {'zh'}, dimensions={0}, use_global_device_ids=true | all-gather | bytes 1179648 | tf_op jit(solution)/shard_map/all_gather | solution.py:127
  19.2 2.4 %collective-permute-start.1 = (bf16[1024,384]{1,0:T(8,128)(2,1)S(1)}, bf16[1024,384]{1,0:T(8,128)(2,1)S(1)}, u32[]{:S(2)}, u32[]{:S(2)}) collective-permute-start(bf16[1024,384]{1,0:T(8,128)(2,1)S(1)} %all_gather.3), channel_id=1, source_target_pairs={{0,128},{128,256},{256,384},{384,0},{1,129},{129,257},{257,385},{3... | collective-permute-start | bytes 2359304 | tf_op jit(solution)/shard_map/ppermute | solution.py:93
  21.6 3.5 %collective-permute-start = (bf16[1024,384]{1,0:T(8,128)(2,1)S(1)}, bf16[1024,384]{1,0:T(8,128)(2,1)S(1)}, u32[]{:S(2)}, u32[]{:S(2)}) collective-permute-start(bf16[1024,384]{1,0:T(8,128)(2,1)S(1)} %all_gather.3), channel_id=1, source_target_pairs={{0,384},{128,0},{256,128},{384,256},{1,385},{129,1},{257,129},{385... | collective-permute-start | bytes 2359304 | tf_op jit(solution)/shard_map/ppermute | solution.py:94
  25.0 14.7 %collective-permute-done.1 = bf16[1024,384]{1,0:T(8,128)(2,1)S(1)} collective-permute-done((bf16[1024,384]{1,0:T(8,128)(2,1)S(1)}, bf16[1024,384]{1,0:T(8,128)(2,1)S(1)}, u32[]{:S(2)}, u32[]{:S(2)}) %collective-permute-start.1) | collective-permute-done | bytes 786464 | tf_op jit(solution)/shard_map/ppermute | solution.py:93
  39.8 3.4 %collective-permute-start.2 = (bf16[512,384]{1,0:T(8,128)(2,1)S(1)}, bf16[512,384]{1,0:T(8,128)(2,1)S(1)}, u32[]{:S(2)}, u32[]{:S(2)}) collective-permute-start(bf16[512,384]{1,0:T(8,128)(2,1)S(1)} %slice.64), channel_id=1, source_target_pairs={{0,128},{128,256},{256,384},{384,0},{1,129},{129,257},{257,385},{3... | collective-permute-start | bytes 1179656 | tf_op jit(solution)/shard_map/ppermute | solution.py:96
  43.2 0.0 collective-permute-done
  43.3 2.4 %collective-permute-start.3 = (bf16[512,384]{1,0:T(8,128)(2,1)S(1)}, bf16[512,384]{1,0:T(8,128)(2,1)S(1)}, u32[]{:S(2)}, u32[]{:S(2)}) collective-permute-start(bf16[512,384]{1,0:T(8,128)(2,1)S(1)} %slice.65), channel_id=1, source_target_pairs={{0,384},{128,0},{256,128},{384,256},{1,385},{129,1},{257,129},{385... | collective-permute-start | bytes 1179656 | tf_op jit(solution)/shard_map/ppermute | solution.py:97
  45.7 1.3 constant_dynamic-update-slice_fusion.4
  47.0 0.0 copy-start.2
  47.0 1.3 constant_dynamic-update-slice_fusion.3
  48.3 2.7 %collective-permute-done.2 = bf16[512,384]{1,0:T(8,128)(2,1)S(1)} collective-permute-done((bf16[512,384]{1,0:T(8,128)(2,1)S(1)}, bf16[512,384]{1,0:T(8,128)(2,1)S(1)}, u32[]{:S(2)}, u32[]{:S(2)}) %collective-permute-start.2) | collective-permute-done | bytes 393248 | tf_op jit(solution)/shard_map/ppermute | solution.py:96
  51.0 1.0 constant_dynamic-update-slice_fusion.2
  52.0 0.0 copy-start.1
  52.0 3.2 %collective-permute-done.3 = bf16[512,384]{1,0:T(8,128)(2,1)S(1)} collective-permute-done((bf16[512,384]{1,0:T(8,128)(2,1)S(1)}, bf16[512,384]{1,0:T(8,128)(2,1)S(1)}, u32[]{:S(2)}, u32[]{:S(2)}) %collective-permute-start.3) | collective-permute-done | bytes 393248 | tf_op jit(solution)/shard_map/ppermute | solution.py:97
  55.2 1.0 constant_dynamic-update-slice_fusion.1
  56.3 1.3 constant_dynamic-update-slice_fusion
  57.6 1.9 %collective-permute-start.4 = (bf16[4096,384]{1,0:T(8,128)(2,1)}, bf16[4096,384]{1,0:T(8,128)(2,1)S(1)}, u32[]{:S(2)}, u32[]{:S(2)}) collective-permute-start(bf16[4096,384]{1,0:T(8,128)(2,1)} %get-tuple-element.11), channel_id=1, source_target_pairs={{0,32},{32,0},{1,33},{33,1},{2,34},{34,2},{3,35},{35,3},{4,36},{36... | collective-permute-start | bytes 9437192 | tf_op jit(solution)/shard_map/ppermute | solution.py:129
  59.5 0.0 copy-done.2
  59.6 2.0 %copy.5.op_ref = s32[4096,1]{1,0:T(8,128)} copy(s32[4096,1]{0,1:T(1,128)S(1)} %get-tuple-element.25) | data formatting | bytes 32768 | tf_op jit(solution)/shard_map/broadcast_in_dim;squeeze | solution.py:86
  61.6 0.0 copy-done.1
  61.6 0.1 convert_reduce_fusion.2
  61.6 0.7 fusion.16
  62.3 3.0 %collective-permute-done.4 = bf16[4096,384]{1,0:T(8,128)(2,1)S(1)} collective-permute-done((bf16[4096,384]{1,0:T(8,128)(2,1)}, bf16[4096,384]{1,0:T(8,128)(2,1)S(1)}, u32[]{:S(2)}, u32[]{:S(2)}) %collective-permute-start.4) | collective-permute-done | bytes 3145760 | tf_op jit(solution)/shard_map/ppermute | solution.py:129
  65.4 2.0 %constant_dynamic-update-slice_fusion.5.table_ref = bf16[8192,384]{1,0:T(8,128)(2,1)} fusion(bf16[8192,384]{1,0:T(8,128)(2,1)} %get-tuple-element.12, bf16[4096,384]{1,0:T(8,128)(2,1)S(1)} %collective-permute-done.4), kind=kLoop, calls=%fused_computation.55 | loop fusion | bytes 6291456 | tf_op jit(solution)/shard_map/concatenate | solution.py:130
  67.4 34.0 %shard_map.37 = bf16[4096,384]{1,0:T(8,128)(2,1)} custom-call(s32[4096]{0:T(1024)} %get-tuple-element.39.first_ref, s32[4096]{0:T(1024)} %get-tuple-element.40.second_ref, bf16[8192,384]{1,0:T(8,128)(2,1)} %constant_dynamic-update-slice_fusion.5.table_ref, s32[4096,1]{1,0:T(8,128)} %copy.5.op_ref), custom_call_target="tpu_custom_call" | custom-call | flops 15728640 | bytes 9437184 | tf_op jit(solution)/shard_map/pallas_call | solution.py:76
  101.4 0.0 copy-start
  101.4 3.3 %fusion = (f32[4096]{0:T(1024)S(1)}, f32[4096]{0:T(1024)S(1)}) fusion(bf16[4096,384]{1,0:T(8,128)(2,1)} %shard_map.37), kind=kLoop, calls=%fused_computation.2 | loop fusion | flops 6283264 | bytes 3178496 | tf_op jit(solution)/shard_map/reduce_sum | solution.py:148
  104.7 0.0 copy-done
  104.7 1.2 fusion.1
  106.1 0.6 concatenate.13
  106.7 53.1 %all_to_all.5 = bf16[32,144,128]{2,1,0:T(8,128)(2,1)S(1)} all-to-all(bf16[32,144,128]{2,1,0:T(8,128)(2,1)S(1)} %concatenate.13), channel_id=1, replica_groups=mesh['x'=4,'zh'=2,'c'=2,'y'=8,'zl'=4] {'y','zl'}, dimensions={0} | all-to-all | bytes 2359296 | tf_op jit(solution)/shard_map/all_to_all | solution.py:169
  159.9 0.1 fusion.37
  160.1 0.2 convert_reduce_fusion.1
  160.2 0.9 fusion.4
  (20 shorter events, 0.3 us)
Async XLA Ops:
  19.2 20.6 %collective-permute-start.1 = (bf16[1024,384]{1,0:T(8,128)(2,1)S(1)}, bf16[1024,384]{1,0:T(8,128)(2,1)S(1)}, u32[]{:S(2)}, u32[]{:S(2)}) collective-permute-start(bf16[1024,384]{1,0:T(8,128)(2,1)S(1)} %all_gather.3), channel_id=1, source_target_pairs={{0,128},{128,256},{256,384},{384,0},{1,129},{129,257},{257,385},{3... | collective-permute-start | bytes 2359304 | tf_op jit(solution)/shard_map/ppermute | solution.py:93
  21.6 21.6 %collective-permute-start = (bf16[1024,384]{1,0:T(8,128)(2,1)S(1)}, bf16[1024,384]{1,0:T(8,128)(2,1)S(1)}, u32[]{:S(2)}, u32[]{:S(2)}) collective-permute-start(bf16[1024,384]{1,0:T(8,128)(2,1)S(1)} %all_gather.3), channel_id=1, source_target_pairs={{0,384},{128,0},{256,128},{384,256},{1,385},{129,1},{257,129},{385... | collective-permute-start | bytes 2359304 | tf_op jit(solution)/shard_map/ppermute | solution.py:94
  39.8 11.2 %collective-permute-start.2 = (bf16[512,384]{1,0:T(8,128)(2,1)S(1)}, bf16[512,384]{1,0:T(8,128)(2,1)S(1)}, u32[]{:S(2)}, u32[]{:S(2)}) collective-permute-start(bf16[512,384]{1,0:T(8,128)(2,1)S(1)} %slice.64), channel_id=1, source_target_pairs={{0,128},{128,256},{256,384},{384,0},{1,129},{129,257},{257,385},{3... | collective-permute-start | bytes 1179656 | tf_op jit(solution)/shard_map/ppermute | solution.py:96
  43.3 12.0 %collective-permute-start.3 = (bf16[512,384]{1,0:T(8,128)(2,1)S(1)}, bf16[512,384]{1,0:T(8,128)(2,1)S(1)}, u32[]{:S(2)}, u32[]{:S(2)}) collective-permute-start(bf16[512,384]{1,0:T(8,128)(2,1)S(1)} %slice.65), channel_id=1, source_target_pairs={{0,384},{128,0},{256,128},{384,256},{1,385},{129,1},{257,129},{385... | collective-permute-start | bytes 1179656 | tf_op jit(solution)/shard_map/ppermute | solution.py:97
  47.0 12.5 %copy-start.2 = (s32[3,4096]{1,0:T(4,128)S(1)}, s32[3,4096]{1,0:T(4,128)}, u32[]{:S(2)}) copy-start(s32[3,4096]{1,0:T(4,128)} %param.5) | copy-start | bytes 147460
  52.0 9.6 %copy-start.1 = (bf16[384,128]{1,0:T(8,128)(2,1)S(1)}, bf16[384,128]{1,0:T(8,128)(2,1)}, u32[]{:S(2)}) copy-start(bf16[384,128]{1,0:T(8,128)(2,1)} %param.4) | copy-start | bytes 294916
  57.6 7.8 %collective-permute-start.4 = (bf16[4096,384]{1,0:T(8,128)(2,1)}, bf16[4096,384]{1,0:T(8,128)(2,1)S(1)}, u32[]{:S(2)}, u32[]{:S(2)}) collective-permute-start(bf16[4096,384]{1,0:T(8,128)(2,1)} %get-tuple-element.11), channel_id=1, source_target_pairs={{0,32},{32,0},{1,33},{33,1},{2,34},{34,2},{3,35},{35,3},{4,36},{36... | collective-permute-start | bytes 9437192 | tf_op jit(solution)/shard_map/ppermute | solution.py:129
  101.4 3.3 %copy-start = (bf16[4096,384]{1,0:T(8,128)(2,1)S(1)}, bf16[4096,384]{1,0:T(8,128)(2,1)}, u32[]{:S(2)}) copy-start(bf16[4096,384]{1,0:T(8,128)(2,1)} %shard_map.37) | copy-start | bytes 9437188

commit v12 on v11

--- a/solution.py
+++ b/solution.py
@@ -47,14 +47,17 @@
 
     base = pl.program_id(0) * tile
 
-    def body(j, carry):
-        a = first_ref[base + j]
-        b = second_ref[base + j]
-        first_buf[pl.ds(j, 1), :] = table[pl.ds(a, 1), :]
-        second_buf[pl.ds(j, 1), :] = table[pl.ds(b, 1), :]
+    def body(g, carry):
+        j0 = pl.multiple_of(g * 8, 8)
+        firsts, seconds = [], []
+        for t in range(8):
+            firsts.append(table[pl.ds(first_ref[base + j0 + t], 1), :])
+            seconds.append(table[pl.ds(second_ref[base + j0 + t], 1), :])
+        first_buf[pl.ds(j0, 8), :] = jnp.concatenate(firsts, axis=0)
+        second_buf[pl.ds(j0, 8), :] = jnp.concatenate(seconds, axis=0)
         return carry
 
-    lax.fori_loop(0, tile, body, 0, unroll=8)
+    lax.fori_loop(0, tile // 8, body, 0)
     out_ref[...] = combine_rows(first_buf[...], second_buf[...], op_ref[...])
 
 

time: 162 us -> 156 us (0.963)
  Pallas kernels: 34 us -> 28.1 us
    pallas_call x1, Pallas kernels: 34 us -> 28.1 us  [build_descriptors(): pl.pallas_call(gather_kernel, grid_spec=grid_spec, out_shape=jax.ShapeDty...]
where the time goes in v12:
time: 156 us; the launch traced here: 155 us
  blocking collectives  72.3 us (46%)
  Pallas kernels  28.1 us (18%)
  waiting for transfers between devices  23.7 us (15%)
  starting transfers between devices  13.6 us (9%)
  local copies, waits for them, and re-layouts  10.8 us (7%)
  other arithmetic  4.42 us (3%)
  matrix products  2.11 us (1%)
    all_to_all x1, blocking collectives, per_device(): arrived = lax.all_to_all(packed, SAMP_AXES, 0, 0, tiled=False)  53.1 us
    pallas_call x1, Pallas kernels, build_descriptors(): pl.pallas_call(gather_kernel, grid_spec=grid_spec, out_shape=jax.ShapeDty...  28.1 us
    all_gather x1, blocking collectives, per_device(): rows = lax.all_gather(tier_one, 'zh', axis=0, tiled=True)  19.2 us
    ppermute x1, waiting for transfers between devices, ring_gather(): from_left = lax.ppermute(block, axis, perm=fwd)  14.7 us
    unnamed x10, local copies, waits for them, and re-layouts  4.57 us
    ppermute x1, starting transfers between devices, ring_gather(): from_right = lax.ppermute(block, axis, perm=bwd)  3.46 us
    ppermute x1, starting transfers between devices, ring_gather(): far_a = lax.ppermute(from_left[:half], axis, perm=fwd)  3.41 us
    reduce_sum x1, other arithmetic, per_device(): square_sums = jnp.sum(widened * widened, axis=1)  3.29 us
  transfers between devices with their start and end apart: 5, of which 4 were waited for; matrix products, arithmetic and copies ran while one was open for 4% of the time, Pallas kernels for 0%

profile of v12, /device:TPU:6, one launch (start us, length us, event | category | flops | bytes accessed | tf_op | source)
XLA Modules:
  0.0 155.2 jit_solution(686303047553981768)
XLA Ops:
  0.0 19.2 %all_gather.3 = bf16[1024,384]{1,0:T(8,128)(2,1)S(1)} all-gather(bf16[512,384]{1,0:T(8,128)(2,1)} %param.3), channel_id=1, replica_groups=mesh['x'=4,'zh'=2,'c'=2,'y'=8,'zl'=4] {'zh'}, dimensions={0}, use_global_device_ids=true | all-gather | bytes 1179648 | tf_op jit(solution)/shard_map/all_gather | solution.py:130
  19.2 2.4 %collective-permute-start.1 = (bf16[1024,384]{1,0:T(8,128)(2,1)S(1)}, bf16[1024,384]{1,0:T(8,128)(2,1)S(1)}, u32[]{:S(2)}, u32[]{:S(2)}) collective-permute-start(bf16[1024,384]{1,0:T(8,128)(2,1)S(1)} %all_gather.3), channel_id=1, source_target_pairs={{0,128},{128,256},{256,384},{384,0},{1,129},{129,257},{257,385},{3... | collective-permute-start | bytes 2359304 | tf_op jit(solution)/shard_map/ppermute | solution.py:96
  21.6 3.5 %collective-permute-start = (bf16[1024,384]{1,0:T(8,128)(2,1)S(1)}, bf16[1024,384]{1,0:T(8,128)(2,1)S(1)}, u32[]{:S(2)}, u32[]{:S(2)}) collective-permute-start(bf16[1024,384]{1,0:T(8,128)(2,1)S(1)} %all_gather.3), channel_id=1, source_target_pairs={{0,384},{128,0},{256,128},{384,256},{1,385},{129,1},{257,129},{385... | collective-permute-start | bytes 2359304 | tf_op jit(solution)/shard_map/ppermute | solution.py:97
  25.0 14.7 %collective-permute-done.1 = bf16[1024,384]{1,0:T(8,128)(2,1)S(1)} collective-permute-done((bf16[1024,384]{1,0:T(8,128)(2,1)S(1)}, bf16[1024,384]{1,0:T(8,128)(2,1)S(1)}, u32[]{:S(2)}, u32[]{:S(2)}) %collective-permute-start.1) | collective-permute-done | bytes 786464 | tf_op jit(solution)/shard_map/ppermute | solution.py:96
  39.8 3.4 %collective-permute-start.2 = (bf16[512,384]{1,0:T(8,128)(2,1)S(1)}, bf16[512,384]{1,0:T(8,128)(2,1)S(1)}, u32[]{:S(2)}, u32[]{:S(2)}) collective-permute-start(bf16[512,384]{1,0:T(8,128)(2,1)S(1)} %slice.64), channel_id=1, source_target_pairs={{0,128},{128,256},{256,384},{384,0},{1,129},{129,257},{257,385},{3... | collective-permute-start | bytes 1179656 | tf_op jit(solution)/shard_map/ppermute | solution.py:99
  43.2 0.0 collective-permute-done
  43.3 2.4 %collective-permute-start.3 = (bf16[512,384]{1,0:T(8,128)(2,1)S(1)}, bf16[512,384]{1,0:T(8,128)(2,1)S(1)}, u32[]{:S(2)}, u32[]{:S(2)}) collective-permute-start(bf16[512,384]{1,0:T(8,128)(2,1)S(1)} %slice.65), channel_id=1, source_target_pairs={{0,384},{128,0},{256,128},{384,256},{1,385},{129,1},{257,129},{385... | collective-permute-start | bytes 1179656 | tf_op jit(solution)/shard_map/ppermute | solution.py:100
  45.7 1.3 constant_dynamic-update-slice_fusion.4
  47.0 0.0 copy-start.2
  47.0 1.3 constant_dynamic-update-slice_fusion.3
  48.3 2.7 %collective-permute-done.2 = bf16[512,384]{1,0:T(8,128)(2,1)S(1)} collective-permute-done((bf16[512,384]{1,0:T(8,128)(2,1)S(1)}, bf16[512,384]{1,0:T(8,128)(2,1)S(1)}, u32[]{:S(2)}, u32[]{:S(2)}) %collective-permute-start.2) | collective-permute-done | bytes 393248 | tf_op jit(solution)/shard_map/ppermute | solution.py:99
  51.0 1.0 constant_dynamic-update-slice_fusion.2
  52.0 0.0 copy-start.1
  52.0 3.2 %collective-permute-done.3 = bf16[512,384]{1,0:T(8,128)(2,1)S(1)} collective-permute-done((bf16[512,384]{1,0:T(8,128)(2,1)S(1)}, bf16[512,384]{1,0:T(8,128)(2,1)S(1)}, u32[]{:S(2)}, u32[]{:S(2)}) %collective-permute-start.3) | collective-permute-done | bytes 393248 | tf_op jit(solution)/shard_map/ppermute | solution.py:100
  55.2 1.0 constant_dynamic-update-slice_fusion.1
  56.3 1.3 constant_dynamic-update-slice_fusion
  57.6 1.9 %collective-permute-start.4 = (bf16[4096,384]{1,0:T(8,128)(2,1)}, bf16[4096,384]{1,0:T(8,128)(2,1)S(1)}, u32[]{:S(2)}, u32[]{:S(2)}) collective-permute-start(bf16[4096,384]{1,0:T(8,128)(2,1)} %get-tuple-element.11), channel_id=1, source_target_pairs={{0,32},{32,0},{1,33},{33,1},{2,34},{34,2},{3,35},{35,3},{4,36},{36... | collective-permute-start | bytes 9437192 | tf_op jit(solution)/shard_map/ppermute | solution.py:132
  59.5 0.0 copy-done.2
  59.6 2.0 %copy.5.op_ref = s32[4096,1]{1,0:T(8,128)} copy(s32[4096,1]{0,1:T(1,128)S(1)} %get-tuple-element.25) | data formatting | bytes 32768 | tf_op jit(solution)/shard_map/broadcast_in_dim;squeeze | solution.py:89
  61.6 0.0 copy-done.1
  61.6 0.1 convert_reduce_fusion.2
  61.6 0.7 fusion.16
  62.3 3.0 %collective-permute-done.4 = bf16[4096,384]{1,0:T(8,128)(2,1)S(1)} collective-permute-done((bf16[4096,384]{1,0:T(8,128)(2,1)}, bf16[4096,384]{1,0:T(8,128)(2,1)S(1)}, u32[]{:S(2)}, u32[]{:S(2)}) %collective-permute-start.4) | collective-permute-done | bytes 3145760 | tf_op jit(solution)/shard_map/ppermute | solution.py:132
  65.4 2.0 %constant_dynamic-update-slice_fusion.5.table_ref = bf16[8192,384]{1,0:T(8,128)(2,1)} fusion(bf16[8192,384]{1,0:T(8,128)(2,1)} %get-tuple-element.12, bf16[4096,384]{1,0:T(8,128)(2,1)S(1)} %collective-permute-done.4), kind=kLoop, calls=%fused_computation.55 | loop fusion | bytes 6291456 | tf_op jit(solution)/shard_map/concatenate | solution.py:133
  67.4 28.1 %shard_map.37 = bf16[4096,384]{1,0:T(8,128)(2,1)} custom-call(s32[4096]{0:T(1024)} %get-tuple-element.39.first_ref, s32[4096]{0:T(1024)} %get-tuple-element.40.second_ref, bf16[8192,384]{1,0:T(8,128)(2,1)} %constant_dynamic-update-slice_fusion.5.table_ref, s32[4096,1]{1,0:T(8,128)} %copy.5.op_ref), custom_call_target="tpu_custom_call" | custom-call | flops 15728640 | bytes 9437184 | tf_op jit(solution)/shard_map/pallas_call | solution.py:79
  95.4 0.0 copy-start
  95.4 3.3 %fusion = (f32[4096]{0:T(1024)S(1)}, f32[4096]{0:T(1024)S(1)}) fusion(bf16[4096,384]{1,0:T(8,128)(2,1)} %shard_map.37), kind=kLoop, calls=%fused_computation.2 | loop fusion | flops 6283264 | bytes 3178496 | tf_op jit(solution)/shard_map/reduce_sum | solution.py:151
  98.7 0.0 copy-done
  98.8 1.2 fusion.1
  100.2 0.6 concatenate.13
  100.8 53.1 %all_to_all.5 = bf16[32,144,128]{2,1,0:T(8,128)(2,1)S(1)} all-to-all(bf16[32,144,128]{2,1,0:T(8,128)(2,1)S(1)} %concatenate.13), channel_id=1, replica_groups=mesh['x'=4,'zh'=2,'c'=2,'y'=8,'zl'=4] {'y','zl'}, dimensions={0} | all-to-all | bytes 2359296 | tf_op jit(solution)/shard_map/all_to_all | solution.py:172
  153.9 0.1 fusion.37
  154.1 0.2 convert_reduce_fusion.1
  154.3 0.9 fusion.4
  (20 shorter events, 0.3 us)
Async XLA Ops:
  19.2 20.6 %collective-permute-start.1 = (bf16[1024,384]{1,0:T(8,128)(2,1)S(1)}, bf16[1024,384]{1,0:T(8,128)(2,1)S(1)}, u32[]{:S(2)}, u32[]{:S(2)}) collective-permute-start(bf16[1024,384]{1,0:T(8,128)(2,1)S(1)} %all_gather.3), channel_id=1, source_target_pairs={{0,128},{128,256},{256,384},{384,0},{1,129},{129,257},{257,385},{3... | collective-permute-start | bytes 2359304 | tf_op jit(solution)/shard_map/ppermute | solution.py:96
  21.6 21.6 %collective-permute-start = (bf16[1024,384]{1,0:T(8,128)(2,1)S(1)}, bf16[1024,384]{1,0:T(8,128)(2,1)S(1)}, u32[]{:S(2)}, u32[]{:S(2)}) collective-permute-start(bf16[1024,384]{1,0:T(8,128)(2,1)S(1)} %all_gather.3), channel_id=1, source_target_pairs={{0,384},{128,0},{256,128},{384,256},{1,385},{129,1},{257,129},{385... | collective-permute-start | bytes 2359304 | tf_op jit(solution)/shard_map/ppermute | solution.py:97
  39.8 11.2 %collective-permute-start.2 = (bf16[512,384]{1,0:T(8,128)(2,1)S(1)}, bf16[512,384]{1,0:T(8,128)(2,1)S(1)}, u32[]{:S(2)}, u32[]{:S(2)}) collective-permute-start(bf16[512,384]{1,0:T(8,128)(2,1)S(1)} %slice.64), channel_id=1, source_target_pairs={{0,128},{128,256},{256,384},{384,0},{1,129},{129,257},{257,385},{3... | collective-permute-start | bytes 1179656 | tf_op jit(solution)/shard_map/ppermute | solution.py:99
  43.3 12.0 %collective-permute-start.3 = (bf16[512,384]{1,0:T(8,128)(2,1)S(1)}, bf16[512,384]{1,0:T(8,128)(2,1)S(1)}, u32[]{:S(2)}, u32[]{:S(2)}) collective-permute-start(bf16[512,384]{1,0:T(8,128)(2,1)S(1)} %slice.65), channel_id=1, source_target_pairs={{0,384},{128,0},{256,128},{384,256},{1,385},{129,1},{257,129},{385... | collective-permute-start | bytes 1179656 | tf_op jit(solution)/shard_map/ppermute | solution.py:100
  47.0 12.5 %copy-start.2 = (s32[3,4096]{1,0:T(4,128)S(1)}, s32[3,4096]{1,0:T(4,128)}, u32[]{:S(2)}) copy-start(s32[3,4096]{1,0:T(4,128)} %param.5) | copy-start | bytes 147460
  52.0 9.6 %copy-start.1 = (bf16[384,128]{1,0:T(8,128)(2,1)S(1)}, bf16[384,128]{1,0:T(8,128)(2,1)}, u32[]{:S(2)}) copy-start(bf16[384,128]{1,0:T(8,128)(2,1)} %param.4) | copy-start | bytes 294916
  57.6 7.8 %collective-permute-start.4 = (bf16[4096,384]{1,0:T(8,128)(2,1)}, bf16[4096,384]{1,0:T(8,128)(2,1)S(1)}, u32[]{:S(2)}, u32[]{:S(2)}) collective-permute-start(bf16[4096,384]{1,0:T(8,128)(2,1)} %get-tuple-element.11), channel_id=1, source_target_pairs={{0,32},{32,0},{1,33},{33,1},{2,34},{34,2},{3,35},{35,3},{4,36},{36... | collective-permute-start | bytes 9437192 | tf_op jit(solution)/shard_map/ppermute | solution.py:132
  95.4 3.3 %copy-start = (bf16[4096,384]{1,0:T(8,128)(2,1)S(1)}, bf16[4096,384]{1,0:T(8,128)(2,1)}, u32[]{:S(2)}) copy-start(bf16[4096,384]{1,0:T(8,128)(2,1)} %shard_map.37) | copy-start | bytes 9437188

commit v13 on v12

--- a/solution.py
+++ b/solution.py
@@ -57,7 +57,7 @@
         second_buf[pl.ds(j0, 8), :] = jnp.concatenate(seconds, axis=0)
         return carry
 
-    lax.fori_loop(0, tile // 8, body, 0)
+    lax.fori_loop(0, tile // 8, body, 0, unroll=2)
     out_ref[...] = combine_rows(first_buf[...], second_buf[...], op_ref[...])
 
 

time: 156 us -> 156 us (level)
  no operation moved by 1% of the time
where the time goes in v13:
time: 156 us; the launch traced here: 155 us
  blocking collectives  72.3 us (46%)
  Pallas kernels  28.1 us (18%)
  waiting for transfers between devices  23.7 us (15%)
  starting transfers between devices  13.6 us (9%)
  local copies, waits for them, and re-layouts  10.8 us (7%)
  other arithmetic  4.42 us (3%)
  matrix products  2.11 us (1%)
    all_to_all x1, blocking collectives, per_device(): arrived = lax.all_to_all(packed, SAMP_AXES, 0, 0, tiled=False)  53.1 us
    pallas_call x1, Pallas kernels, build_descriptors(): pl.pallas_call(gather_kernel, grid_spec=grid_spec, out_shape=jax.ShapeDty...  28.1 us
    all_gather x1, blocking collectives, per_device(): rows = lax.all_gather(tier_one, 'zh', axis=0, tiled=True)  19.2 us
    ppermute x1, waiting for transfers between devices, ring_gather(): from_left = lax.ppermute(block, axis, perm=fwd)  14.7 us
    unnamed x10, local copies, waits for them, and re-layouts  4.57 us
    ppermute x1, starting transfers between devices, ring_gather(): from_right = lax.ppermute(block, axis, perm=bwd)  3.46 us
    ppermute x1, starting transfers between devices, ring_gather(): far_a = lax.ppermute(from_left[:half], axis, perm=fwd)  3.41 us
    reduce_sum x1, other arithmetic, per_device(): square_sums = jnp.sum(widened * widened, axis=1)  3.29 us
  transfers between devices with their start and end apart: 5, of which 4 were waited for; matrix products, arithmetic and copies ran while one was open for 4% of the time, Pallas kernels for 0%

profile of v13, /device:TPU:6, one launch (start us, length us, event | category | flops | bytes accessed | tf_op | source)
XLA Modules:
  0.0 155.3 jit_solution(165893839347006239)
XLA Ops:
  0.0 19.2 %all_gather.3 = bf16[1024,384]{1,0:T(8,128)(2,1)S(1)} all-gather(bf16[512,384]{1,0:T(8,128)(2,1)} %param.3), channel_id=1, replica_groups=mesh['x'=4,'zh'=2,'c'=2,'y'=8,'zl'=4] {'zh'}, dimensions={0}, use_global_device_ids=true | all-gather | bytes 1179648 | tf_op jit(solution)/shard_map/all_gather | solution.py:130
  19.2 2.4 %collective-permute-start.1 = (bf16[1024,384]{1,0:T(8,128)(2,1)S(1)}, bf16[1024,384]{1,0:T(8,128)(2,1)S(1)}, u32[]{:S(2)}, u32[]{:S(2)}) collective-permute-start(bf16[1024,384]{1,0:T(8,128)(2,1)S(1)} %all_gather.3), channel_id=1, source_target_pairs={{0,128},{128,256},{256,384},{384,0},{1,129},{129,257},{257,385},{3... | collective-permute-start | bytes 2359304 | tf_op jit(solution)/shard_map/ppermute | solution.py:96
  21.6 3.5 %collective-permute-start = (bf16[1024,384]{1,0:T(8,128)(2,1)S(1)}, bf16[1024,384]{1,0:T(8,128)(2,1)S(1)}, u32[]{:S(2)}, u32[]{:S(2)}) collective-permute-start(bf16[1024,384]{1,0:T(8,128)(2,1)S(1)} %all_gather.3), channel_id=1, source_target_pairs={{0,384},{128,0},{256,128},{384,256},{1,385},{129,1},{257,129},{385... | collective-permute-start | bytes 2359304 | tf_op jit(solution)/shard_map/ppermute | solution.py:97
  25.0 14.7 %collective-permute-done.1 = bf16[1024,384]{1,0:T(8,128)(2,1)S(1)} collective-permute-done((bf16[1024,384]{1,0:T(8,128)(2,1)S(1)}, bf16[1024,384]{1,0:T(8,128)(2,1)S(1)}, u32[]{:S(2)}, u32[]{:S(2)}) %collective-permute-start.1) | collective-permute-done | bytes 786464 | tf_op jit(solution)/shard_map/ppermute | solution.py:96
  39.8 3.4 %collective-permute-start.2 = (bf16[512,384]{1,0:T(8,128)(2,1)S(1)}, bf16[512,384]{1,0:T(8,128)(2,1)S(1)}, u32[]{:S(2)}, u32[]{:S(2)}) collective-permute-start(bf16[512,384]{1,0:T(8,128)(2,1)S(1)} %slice.64), channel_id=1, source_target_pairs={{0,128},{128,256},{256,384},{384,0},{1,129},{129,257},{257,385},{3... | collective-permute-start | bytes 1179656 | tf_op jit(solution)/shard_map/ppermute | solution.py:99
  43.2 0.0 collective-permute-done
  43.3 2.4 %collective-permute-start.3 = (bf16[512,384]{1,0:T(8,128)(2,1)S(1)}, bf16[512,384]{1,0:T(8,128)(2,1)S(1)}, u32[]{:S(2)}, u32[]{:S(2)}) collective-permute-start(bf16[512,384]{1,0:T(8,128)(2,1)S(1)} %slice.65), channel_id=1, source_target_pairs={{0,384},{128,0},{256,128},{384,256},{1,385},{129,1},{257,129},{385... | collective-permute-start | bytes 1179656 | tf_op jit(solution)/shard_map/ppermute | solution.py:100
  45.7 1.3 constant_dynamic-update-slice_fusion.4
  47.0 0.0 copy-start.2
  47.0 1.3 constant_dynamic-update-slice_fusion.3
  48.3 2.7 %collective-permute-done.2 = bf16[512,384]{1,0:T(8,128)(2,1)S(1)} collective-permute-done((bf16[512,384]{1,0:T(8,128)(2,1)S(1)}, bf16[512,384]{1,0:T(8,128)(2,1)S(1)}, u32[]{:S(2)}, u32[]{:S(2)}) %collective-permute-start.2) | collective-permute-done | bytes 393248 | tf_op jit(solution)/shard_map/ppermute | solution.py:99
  51.0 1.0 constant_dynamic-update-slice_fusion.2
  52.0 0.0 copy-start.1
  52.0 3.2 %collective-permute-done.3 = bf16[512,384]{1,0:T(8,128)(2,1)S(1)} collective-permute-done((bf16[512,384]{1,0:T(8,128)(2,1)S(1)}, bf16[512,384]{1,0:T(8,128)(2,1)S(1)}, u32[]{:S(2)}, u32[]{:S(2)}) %collective-permute-start.3) | collective-permute-done | bytes 393248 | tf_op jit(solution)/shard_map/ppermute | solution.py:100
  55.2 1.0 constant_dynamic-update-slice_fusion.1
  56.3 1.3 constant_dynamic-update-slice_fusion
  57.6 1.9 %collective-permute-start.4 = (bf16[4096,384]{1,0:T(8,128)(2,1)}, bf16[4096,384]{1,0:T(8,128)(2,1)S(1)}, u32[]{:S(2)}, u32[]{:S(2)}) collective-permute-start(bf16[4096,384]{1,0:T(8,128)(2,1)} %get-tuple-element.11), channel_id=1, source_target_pairs={{0,32},{32,0},{1,33},{33,1},{2,34},{34,2},{3,35},{35,3},{4,36},{36... | collective-permute-start | bytes 9437192 | tf_op jit(solution)/shard_map/ppermute | solution.py:132
  59.5 0.0 copy-done.2
  59.6 2.0 %copy.5.op_ref = s32[4096,1]{1,0:T(8,128)} copy(s32[4096,1]{0,1:T(1,128)S(1)} %get-tuple-element.25) | data formatting | bytes 32768 | tf_op jit(solution)/shard_map/broadcast_in_dim;squeeze | solution.py:89
  61.6 0.0 copy-done.1
  61.6 0.1 convert_reduce_fusion.2
  61.6 0.7 fusion.16
  62.3 3.0 %collective-permute-done.4 = bf16[4096,384]{1,0:T(8,128)(2,1)S(1)} collective-permute-done((bf16[4096,384]{1,0:T(8,128)(2,1)}, bf16[4096,384]{1,0:T(8,128)(2,1)S(1)}, u32[]{:S(2)}, u32[]{:S(2)}) %collective-permute-start.4) | collective-permute-done | bytes 3145760 | tf_op jit(solution)/shard_map/ppermute | solution.py:132
  65.4 2.0 %constant_dynamic-update-slice_fusion.5.table_ref = bf16[8192,384]{1,0:T(8,128)(2,1)} fusion(bf16[8192,384]{1,0:T(8,128)(2,1)} %get-tuple-element.12, bf16[4096,384]{1,0:T(8,128)(2,1)S(1)} %collective-permute-done.4), kind=kLoop, calls=%fused_computation.55 | loop fusion | bytes 6291456 | tf_op jit(solution)/shard_map/concatenate | solution.py:133
  67.4 28.1 %shard_map.37 = bf16[4096,384]{1,0:T(8,128)(2,1)} custom-call(s32[4096]{0:T(1024)} %get-tuple-element.39.first_ref, s32[4096]{0:T(1024)} %get-tuple-element.40.second_ref, bf16[8192,384]{1,0:T(8,128)(2,1)} %constant_dynamic-update-slice_fusion.5.table_ref, s32[4096,1]{1,0:T(8,128)} %copy.5.op_ref), custom_call_target="tpu_custom_call" | custom-call | flops 15728640 | bytes 9437184 | tf_op jit(solution)/shard_map/pallas_call | solution.py:79
  95.5 0.0 copy-start
  95.5 3.3 %fusion = (f32[4096]{0:T(1024)S(1)}, f32[4096]{0:T(1024)S(1)}) fusion(bf16[4096,384]{1,0:T(8,128)(2,1)} %shard_map.37), kind=kLoop, calls=%fused_computation.2 | loop fusion | flops 6283264 | bytes 3178496 | tf_op jit(solution)/shard_map/reduce_sum | solution.py:151
  98.8 0.0 copy-done
  98.8 1.2 fusion.1
  100.2 0.6 concatenate.13
  100.9 53.1 %all_to_all.5 = bf16[32,144,128]{2,1,0:T(8,128)(2,1)S(1)} all-to-all(bf16[32,144,128]{2,1,0:T(8,128)(2,1)S(1)} %concatenate.13), channel_id=1, replica_groups=mesh['x'=4,'zh'=2,'c'=2,'y'=8,'zl'=4] {'y','zl'}, dimensions={0} | all-to-all | bytes 2359296 | tf_op jit(solution)/shard_map/all_to_all | solution.py:172
  154.0 0.1 fusion.37
  154.2 0.2 convert_reduce_fusion.1
  154.3 0.9 fusion.4
  (20 shorter events, 0.3 us)
Async XLA Ops:
  19.2 20.6 %collective-permute-start.1 = (bf16[1024,384]{1,0:T(8,128)(2,1)S(1)}, bf16[1024,384]{1,0:T(8,128)(2,1)S(1)}, u32[]{:S(2)}, u32[]{:S(2)}) collective-permute-start(bf16[1024,384]{1,0:T(8,128)(2,1)S(1)} %all_gather.3), channel_id=1, source_target_pairs={{0,128},{128,256},{256,384},{384,0},{1,129},{129,257},{257,385},{3... | collective-permute-start | bytes 2359304 | tf_op jit(solution)/shard_map/ppermute | solution.py:96
  21.6 21.6 %collective-permute-start = (bf16[1024,384]{1,0:T(8,128)(2,1)S(1)}, bf16[1024,384]{1,0:T(8,128)(2,1)S(1)}, u32[]{:S(2)}, u32[]{:S(2)}) collective-permute-start(bf16[1024,384]{1,0:T(8,128)(2,1)S(1)} %all_gather.3), channel_id=1, source_target_pairs={{0,384},{128,0},{256,128},{384,256},{1,385},{129,1},{257,129},{385... | collective-permute-start | bytes 2359304 | tf_op jit(solution)/shard_map/ppermute | solution.py:97
  39.8 11.2 %collective-permute-start.2 = (bf16[512,384]{1,0:T(8,128)(2,1)S(1)}, bf16[512,384]{1,0:T(8,128)(2,1)S(1)}, u32[]{:S(2)}, u32[]{:S(2)}) collective-permute-start(bf16[512,384]{1,0:T(8,128)(2,1)S(1)} %slice.64), channel_id=1, source_target_pairs={{0,128},{128,256},{256,384},{384,0},{1,129},{129,257},{257,385},{3... | collective-permute-start | bytes 1179656 | tf_op jit(solution)/shard_map/ppermute | solution.py:99
  43.3 12.0 %collective-permute-start.3 = (bf16[512,384]{1,0:T(8,128)(2,1)S(1)}, bf16[512,384]{1,0:T(8,128)(2,1)S(1)}, u32[]{:S(2)}, u32[]{:S(2)}) collective-permute-start(bf16[512,384]{1,0:T(8,128)(2,1)S(1)} %slice.65), channel_id=1, source_target_pairs={{0,384},{128,0},{256,128},{384,256},{1,385},{129,1},{257,129},{385... | collective-permute-start | bytes 1179656 | tf_op jit(solution)/shard_map/ppermute | solution.py:100
  47.0 12.5 %copy-start.2 = (s32[3,4096]{1,0:T(4,128)S(1)}, s32[3,4096]{1,0:T(4,128)}, u32[]{:S(2)}) copy-start(s32[3,4096]{1,0:T(4,128)} %param.5) | copy-start | bytes 147460
  52.0 9.6 %copy-start.1 = (bf16[384,128]{1,0:T(8,128)(2,1)S(1)}, bf16[384,128]{1,0:T(8,128)(2,1)}, u32[]{:S(2)}) copy-start(bf16[384,128]{1,0:T(8,128)(2,1)} %param.4) | copy-start | bytes 294916
  57.6 7.8 %collective-permute-start.4 = (bf16[4096,384]{1,0:T(8,128)(2,1)}, bf16[4096,384]{1,0:T(8,128)(2,1)S(1)}, u32[]{:S(2)}, u32[]{:S(2)}) collective-permute-start(bf16[4096,384]{1,0:T(8,128)(2,1)} %get-tuple-element.11), channel_id=1, source_target_pairs={{0,32},{32,0},{1,33},{33,1},{2,34},{34,2},{3,35},{35,3},{4,36},{36... | collective-permute-start | bytes 9437192 | tf_op jit(solution)/shard_map/ppermute | solution.py:132
  95.5 3.3 %copy-start = (bf16[4096,384]{1,0:T(8,128)(2,1)S(1)}, bf16[4096,384]{1,0:T(8,128)(2,1)}, u32[]{:S(2)}) copy-start(bf16[4096,384]{1,0:T(8,128)(2,1)} %shard_map.37) | copy-start | bytes 9437188

commit v14 on v12

--- a/solution.py
+++ b/solution.py
@@ -33,17 +33,21 @@
     return built.astype(jnp.bfloat16)
 
 
-def gather_kernel(first_ref, second_ref, table_ref, op_ref, out_ref, table, first_buf, second_buf):
+def gather_kernel(first_ref, second_ref, own_ref, other_ref, op_ref, out_ref,
+                  table, first_buf, second_buf):
     tile = first_buf.shape[0]
     step = 256
+    half = own_ref.shape[0]
 
     @pl.when(pl.program_id(0) == 0)
     def _():
         def widen(i, carry):
-            rows = pl.ds(pl.multiple_of(i * step, step), step)
-            table[rows, :] = table_ref[rows, :].astype(jnp.float32)
+            start = pl.multiple_of(i * step, step)
+            table[pl.ds(start, step), :] = own_ref[pl.ds(start, step), :].astype(jnp.float32)
+            table[pl.ds(start + half, step), :] = (
+                other_ref[pl.ds(start, step), :].astype(jnp.float32))
             return carry
-        lax.fori_loop(0, table.shape[0] // step, widen, 0)
+        lax.fori_loop(0, half // step, widen, 0)
 
     base = pl.program_id(0) * tile
 
@@ -61,15 +65,17 @@
     out_ref[...] = combine_rows(first_buf[...], second_buf[...], op_ref[...])
 
 
-def build_descriptors(table, first_pos, second_pos, operator_id):
-    n_rows, width = table.shape
+def build_descriptors(own, other, first_pos, second_pos, operator_id):
+    half, width = own.shape
+    n_rows = 2 * half
     pairs = first_pos.shape[0]
     tile = min(GATHER_TILE, pairs)
     grid_spec = pltpu.PrefetchScalarGridSpec(
         num_scalar_prefetch=2,
         grid=(pairs // tile,),
         in_specs=[
-            pl.BlockSpec((n_rows, width), lambda i, p1, p2: (0, 0)),
+            pl.BlockSpec((half, width), lambda i, p1, p2: (0, 0)),
+            pl.BlockSpec((half, width), lambda i, p1, p2: (0, 0)),
             pl.BlockSpec((tile, 1), lambda i, p1, p2: (i, 0)),
         ],
         out_specs=pl.BlockSpec((tile, width), lambda i, p1, p2: (i, 0)),
@@ -86,7 +92,7 @@
         cost_estimate=pl.CostEstimate(
             flops=10 * pairs * width, transcendentals=0,
             bytes_accessed=n_rows * width * 2 + pairs * width * 2),
-    )(first_pos, second_pos, table, operator_id[:, None])
+    )(first_pos, second_pos, own, other, operator_id[:, None])
 
 
 def ring_gather(block, axis, n):
@@ -130,7 +136,6 @@
     rows = lax.all_gather(tier_one, "zh", axis=0, tiled=True)
     rows = ring_gather(rows, "x", n_x)
     other = lax.ppermute(rows, "c", perm=[(0, 1), (1, 0)])
-    rows = jnp.concatenate([rows, other], axis=0)
     my_c = lax.axis_index("c")
     my_x = lax.axis_index("x")
 
@@ -142,7 +147,7 @@
         return ((half * n_x + x_slot) * n_zh + zh) * local_rows + r
 
     built = build_descriptors(
-        rows, position(pair_list[0]), position(pair_list[1]), pair_list[2]
+        rows, other, position(pair_list[0]), position(pair_list[1]), pair_list[2]
     )
 
     product = jnp.dot(built, residuals, preferred_element_type=jnp.float32)

time: 156 us -> 152 us (0.974)
  local copies, waits for them, and re-layouts: 10.8 us -> 3.36 us
  waiting for transfers between devices: 23.7 us -> 26.9 us
    unnamed x10 -> x12, local copies, waits for them, and re-layouts: 4.57 us -> 0.39 us
    ppermute x1, waiting for transfers between devices: 2.73 us -> 4.9 us  [ring_gather(): far_a = lax.ppermute(from_left[:half], axis, perm=fwd)]
    concatenate x1 -> x0, local copies, waits for them, and re-layouts: 2.01 us -> none  [per_device(): rows = jnp.concatenate([rows, other], axis=0)]
  transfers between devices with their start and end apart: 5 -> 5, of which waited for: 4 -> 4; matrix products, arithmetic and copies ran while one was open for 4% -> 2% of each run, Pallas kernels for 0% -> 0%
where the time goes in v14:
time: 152 us; the launch traced here: 151 us
  blocking collectives  72.3 us (48%)
  Pallas kernels  28.1 us (18%)
  waiting for transfers between devices  26.9 us (18%)
  starting transfers between devices  13.7 us (9%)
  other arithmetic  4.43 us (3%)
  local copies, waits for them, and re-layouts  3.36 us (2%)
  matrix products  2.11 us (1%)
    all_to_all x1, blocking collectives, per_device(): arrived = lax.all_to_all(packed, SAMP_AXES, 0, 0, tiled=False)  53.1 us
    pallas_call x1, Pallas kernels, build_descriptors(): pl.pallas_call(gather_kernel, grid_spec=grid_spec, out_shape=jax.ShapeDty...  28.1 us
    all_gather x1, blocking collectives, per_device(): rows = lax.all_gather(tier_one, 'zh', axis=0, tiled=True)  19.2 us
    ppermute x1, waiting for transfers between devices, ring_gather(): from_left = lax.ppermute(block, axis, perm=fwd)  14.7 us
    ppermute x1, waiting for transfers between devices, ring_gather(): far_a = lax.ppermute(from_left[:half], axis, perm=fwd)  4.9 us
    ppermute x1, waiting for transfers between devices, ring_gather(): far_b = lax.ppermute(from_right[half:], axis, perm=bwd)  4.3 us
    ppermute x1, starting transfers between devices, ring_gather(): from_right = lax.ppermute(block, axis, perm=bwd)  3.46 us
    ppermute x1, starting transfers between devices, ring_gather(): far_a = lax.ppermute(from_left[:half], axis, perm=fwd)  3.41 us
  transfers between devices with their start and end apart: 5, of which 4 were waited for; matrix products, arithmetic and copies ran while one was open for 2% of the time, Pallas kernels for 0%

profile of v14, /device:TPU:6, one launch (start us, length us, event | category | flops | bytes accessed | tf_op | source)
XLA Modules:
  0.0 151.2 jit_solution(11630659184200629656)
XLA Ops:
  0.0 19.2 %all_gather.3 = bf16[1024,384]{1,0:T(8,128)(2,1)S(1)} all-gather(bf16[512,384]{1,0:T(8,128)(2,1)} %param.3), channel_id=1, replica_groups=mesh['x'=4,'zh'=2,'c'=2,'y'=8,'zl'=4] {'zh'}, dimensions={0}, use_global_device_ids=true | all-gather | bytes 1179648 | tf_op jit(solution)/shard_map/all_gather | solution.py:136
  19.2 2.4 %collective-permute-start.1 = (bf16[1024,384]{1,0:T(8,128)(2,1)S(1)}, bf16[1024,384]{1,0:T(8,128)(2,1)S(1)}, u32[]{:S(2)}, u32[]{:S(2)}) collective-permute-start(bf16[1024,384]{1,0:T(8,128)(2,1)S(1)} %all_gather.3), channel_id=1, source_target_pairs={{0,128},{128,256},{256,384},{384,0},{1,129},{129,257},{257,385},{3... | collective-permute-start | bytes 2359304 | tf_op jit(solution)/shard_map/ppermute | solution.py:102
  21.6 3.5 %collective-permute-start = (bf16[1024,384]{1,0:T(8,128)(2,1)S(1)}, bf16[1024,384]{1,0:T(8,128)(2,1)S(1)}, u32[]{:S(2)}, u32[]{:S(2)}) collective-permute-start(bf16[1024,384]{1,0:T(8,128)(2,1)S(1)} %all_gather.3), channel_id=1, source_target_pairs={{0,384},{128,0},{256,128},{384,256},{1,385},{129,1},{257,129},{385... | collective-permute-start | bytes 2359304 | tf_op jit(solution)/shard_map/ppermute | solution.py:103
  25.0 14.7 %collective-permute-done.1 = bf16[1024,384]{1,0:T(8,128)(2,1)S(1)} collective-permute-done((bf16[1024,384]{1,0:T(8,128)(2,1)S(1)}, bf16[1024,384]{1,0:T(8,128)(2,1)S(1)}, u32[]{:S(2)}, u32[]{:S(2)}) %collective-permute-start.1) | collective-permute-done | bytes 786464 | tf_op jit(solution)/shard_map/ppermute | solution.py:102
  39.8 3.4 %collective-permute-start.2 = (bf16[512,384]{1,0:T(8,128)(2,1)S(1)}, bf16[512,384]{1,0:T(8,128)(2,1)S(1)}, u32[]{:S(2)}, u32[]{:S(2)}) collective-permute-start(bf16[512,384]{1,0:T(8,128)(2,1)S(1)} %slice.64), channel_id=1, source_target_pairs={{0,128},{128,256},{256,384},{384,0},{1,129},{129,257},{257,385},{3... | collective-permute-start | bytes 1179656 | tf_op jit(solution)/shard_map/ppermute | solution.py:105
  43.2 0.0 collective-permute-done
  43.3 0.0 copy-start.3
  43.3 2.6 %collective-permute-start.3 = (bf16[512,384]{1,0:T(8,128)(2,1)S(1)}, bf16[512,384]{1,0:T(8,128)(2,1)S(1)}, u32[]{:S(2)}, u32[]{:S(2)}) collective-permute-start(bf16[512,384]{1,0:T(8,128)(2,1)S(1)} %slice.65), channel_id=1, source_target_pairs={{0,384},{128,0},{256,128},{384,256},{1,385},{129,1},{257,129},{385... | collective-permute-start | bytes 1179656 | tf_op jit(solution)/shard_map/ppermute | solution.py:106
  45.9 0.1 constant_dynamic-update-slice_fusion.4
  45.9 0.0 copy-start.2
  46.0 0.2 constant_dynamic-update-slice_fusion.3
  46.1 4.9 %collective-permute-done.2 = bf16[512,384]{1,0:T(8,128)(2,1)S(1)} collective-permute-done((bf16[512,384]{1,0:T(8,128)(2,1)S(1)}, bf16[512,384]{1,0:T(8,128)(2,1)S(1)}, u32[]{:S(2)}, u32[]{:S(2)}) %collective-permute-start.2) | collective-permute-done | bytes 393248 | tf_op jit(solution)/shard_map/ppermute | solution.py:105
  51.0 0.1 constant_dynamic-update-slice_fusion.2
  51.1 4.3 %collective-permute-done.3 = bf16[512,384]{1,0:T(8,128)(2,1)S(1)} collective-permute-done((bf16[512,384]{1,0:T(8,128)(2,1)S(1)}, bf16[512,384]{1,0:T(8,128)(2,1)S(1)}, u32[]{:S(2)}, u32[]{:S(2)}) %collective-permute-start.3) | collective-permute-done | bytes 393248 | tf_op jit(solution)/shard_map/ppermute | solution.py:106
  55.4 0.1 constant_dynamic-update-slice_fusion.1
  55.5 0.2 constant_dynamic-update-slice_fusion.own_ref
  55.6 0.0 copy-start.1
  55.6 1.9 %collective-permute-start.4 = (bf16[4096,384]{1,0:T(8,128)(2,1)S(1)}, bf16[4096,384]{1,0:T(8,128)(2,1)}, u32[]{:S(2)}, u32[]{:S(2)}) collective-permute-start(bf16[4096,384]{1,0:T(8,128)(2,1)S(1)} %constant_dynamic-update-slice_fusion.own_ref), channel_id=1, source_target_pairs={{0,32},{32,0},{1,33},{33,1},{2,34},{34,2},{3,35},{35,3},{4,36},{36... | collective-permute-start | bytes 9437192 | tf_op jit(solution)/shard_map/ppermute | solution.py:138
  57.6 0.0 copy-done.3
  57.6 2.0 %copy.5.op_ref = s32[4096,1]{1,0:T(8,128)} copy(s32[4096,1]{0,1:T(1,128)S(1)} %get-tuple-element.15) | data formatting | bytes 32768 | tf_op jit(solution)/shard_map/broadcast_in_dim;squeeze | solution.py:95
  59.6 0.0 copy-done.2
  59.6 0.1 convert_reduce_fusion.2
  59.7 0.7 fusion.16
  60.4 2.9 %collective-permute-done.4.other_ref = bf16[4096,384]{1,0:T(8,128)(2,1)} collective-permute-done((bf16[4096,384]{1,0:T(8,128)(2,1)S(1)}, bf16[4096,384]{1,0:T(8,128)(2,1)}, u32[]{:S(2)}, u32[]{:S(2)}) %collective-permute-start.4) | collective-permute-done | bytes 3145760 | tf_op jit(solution)/shard_map/ppermute | solution.py:138
  63.3 0.0 copy-done.1
  63.3 28.1 %shard_map.37 = bf16[4096,384]{1,0:T(8,128)(2,1)} custom-call(s32[4096]{0:T(1024)} %get-tuple-element.29.first_ref, s32[4096]{0:T(1024)} %get-tuple-element.30.second_ref, bf16[4096,384]{1,0:T(8,128)(2,1)} %copy-done.1, bf16[4096,384]{1,0:T(8,128)(2,1)} %collective-permute-done.4.other_ref, s32[4096,1]{1,0:T(8,128)} %copy.5.op_ref), custom_call_target="tpu_custom_call" | custom-call | flops 15728640 | bytes 9437184 | tf_op jit(solution)/shard_map/pallas_call | solution.py:85
  91.4 0.0 copy-start
  91.4 3.3 %fusion = (f32[4096]{0:T(1024)S(1)}, f32[4096]{0:T(1024)S(1)}) fusion(bf16[4096,384]{1,0:T(8,128)(2,1)} %shard_map.37), kind=kLoop, calls=%fused_computation.2 | loop fusion | flops 6283264 | bytes 3178496 | tf_op jit(solution)/shard_map/reduce_sum | solution.py:156
  94.7 0.0 copy-done
  94.7 1.2 fusion.1
  96.1 0.6 concatenate.8
  96.7 53.1 %all_to_all.5 = bf16[32,144,128]{2,1,0:T(8,128)(2,1)S(1)} all-to-all(bf16[32,144,128]{2,1,0:T(8,128)(2,1)S(1)} %concatenate.8), channel_id=1, replica_groups=mesh['x'=4,'zh'=2,'c'=2,'y'=8,'zl'=4] {'y','zl'}, dimensions={0} | all-to-all | bytes 2359296 | tf_op jit(solution)/shard_map/all_to_all | solution.py:177
  149.9 0.1 fusion.37
  150.1 0.2 convert_reduce_fusion.1
  150.2 0.9 fusion.4
  (20 shorter events, 0.3 us)
Async XLA Ops:
  19.2 20.6 %collective-permute-start.1 = (bf16[1024,384]{1,0:T(8,128)(2,1)S(1)}, bf16[1024,384]{1,0:T(8,128)(2,1)S(1)}, u32[]{:S(2)}, u32[]{:S(2)}) collective-permute-start(bf16[1024,384]{1,0:T(8,128)(2,1)S(1)} %all_gather.3), channel_id=1, source_target_pairs={{0,128},{128,256},{256,384},{384,0},{1,129},{129,257},{257,385},{3... | collective-permute-start | bytes 2359304 | tf_op jit(solution)/shard_map/ppermute | solution.py:102
  21.6 21.6 %collective-permute-start = (bf16[1024,384]{1,0:T(8,128)(2,1)S(1)}, bf16[1024,384]{1,0:T(8,128)(2,1)S(1)}, u32[]{:S(2)}, u32[]{:S(2)}) collective-permute-start(bf16[1024,384]{1,0:T(8,128)(2,1)S(1)} %all_gather.3), channel_id=1, source_target_pairs={{0,384},{128,0},{256,128},{384,256},{1,385},{129,1},{257,129},{385... | collective-permute-start | bytes 2359304 | tf_op jit(solution)/shard_map/ppermute | solution.py:103
  39.8 11.2 %collective-permute-start.2 = (bf16[512,384]{1,0:T(8,128)(2,1)S(1)}, bf16[512,384]{1,0:T(8,128)(2,1)S(1)}, u32[]{:S(2)}, u32[]{:S(2)}) collective-permute-start(bf16[512,384]{1,0:T(8,128)(2,1)S(1)} %slice.64), channel_id=1, source_target_pairs={{0,128},{128,256},{256,384},{384,0},{1,129},{129,257},{257,385},{3... | collective-permute-start | bytes 1179656 | tf_op jit(solution)/shard_map/ppermute | solution.py:105
  43.3 14.3 %copy-start.3 = (s32[3,4096]{1,0:T(4,128)S(1)}, s32[3,4096]{1,0:T(4,128)}, u32[]{:S(2)}) copy-start(s32[3,4096]{1,0:T(4,128)} %param.5) | copy-start | bytes 147460
  43.3 12.1 %collective-permute-start.3 = (bf16[512,384]{1,0:T(8,128)(2,1)S(1)}, bf16[512,384]{1,0:T(8,128)(2,1)S(1)}, u32[]{:S(2)}, u32[]{:S(2)}) collective-permute-start(bf16[512,384]{1,0:T(8,128)(2,1)S(1)} %slice.65), channel_id=1, source_target_pairs={{0,384},{128,0},{256,128},{384,256},{1,385},{129,1},{257,129},{385... | collective-permute-start | bytes 1179656 | tf_op jit(solution)/shard_map/ppermute | solution.py:106
  45.9 13.6 %copy-start.2 = (bf16[384,128]{1,0:T(8,128)(2,1)S(1)}, bf16[384,128]{1,0:T(8,128)(2,1)}, u32[]{:S(2)}) copy-start(bf16[384,128]{1,0:T(8,128)(2,1)} %param.4) | copy-start | bytes 294916
  55.6 7.7 %copy-start.1 = (bf16[4096,384]{1,0:T(8,128)(2,1)}, bf16[4096,384]{1,0:T(8,128)(2,1)S(1)}, u32[]{:S(2)}) copy-start(bf16[4096,384]{1,0:T(8,128)(2,1)S(1)} %constant_dynamic-update-slice_fusion.own_ref) | copy-start | bytes 9437188
  55.6 7.7 %collective-permute-start.4 = (bf16[4096,384]{1,0:T(8,128)(2,1)S(1)}, bf16[4096,384]{1,0:T(8,128)(2,1)}, u32[]{:S(2)}, u32[]{:S(2)}) collective-permute-start(bf16[4096,384]{1,0:T(8,128)(2,1)S(1)} %constant_dynamic-update-slice_fusion.own_ref), channel_id=1, source_target_pairs={{0,32},{32,0},{1,33},{33,1},{2,34},{34,2},{3,35},{35,3},{4,36},{36... | collective-permute-start | bytes 9437192 | tf_op jit(solution)/shard_map/ppermute | solution.py:138
  91.4 3.3 %copy-start = (bf16[4096,384]{1,0:T(8,128)(2,1)S(1)}, bf16[4096,384]{1,0:T(8,128)(2,1)}, u32[]{:S(2)}) copy-start(bf16[4096,384]{1,0:T(8,128)(2,1)} %shard_map.37) | copy-start | bytes 9437188

commit v15 on v14

--- a/solution.py
+++ b/solution.py
@@ -33,8 +33,8 @@
     return built.astype(jnp.bfloat16)
 
 
-def gather_kernel(first_ref, second_ref, own_ref, other_ref, op_ref, out_ref,
-                  table, first_buf, second_buf):
+def gather_kernel(first_ref, second_ref, own_ref, other_ref, op_ref, res_ref, col_ref,
+                  centred_ref, first_ref_out, square_ref_out, table, first_buf, second_buf):
     tile = first_buf.shape[0]
     step = 256
     half = own_ref.shape[0]
@@ -62,12 +62,20 @@
         return carry
 
     lax.fori_loop(0, tile // 8, body, 0)
-    out_ref[...] = combine_rows(first_buf[...], second_buf[...], op_ref[...])
-
-
-def build_descriptors(own, other, first_pos, second_pos, operator_id):
+    built = combine_rows(first_buf[...], second_buf[...], op_ref[...])
+    product = jnp.dot(built, res_ref[...], preferred_element_type=jnp.float32)
+    widened = built.astype(jnp.float32)
+    first_sums = jnp.sum(widened, axis=1, keepdims=True)
+    first_ref_out[...] = first_sums
+    square_ref_out[...] = jnp.sum(widened * widened, axis=1, keepdims=True)
+    local_means = first_sums / res_ref.shape[0]
+    centred_ref[...] = (product - local_means * col_ref[...]).astype(jnp.bfloat16)
+
+
+def build_descriptors(own, other, first_pos, second_pos, operator_id, residuals, col_part):
     half, width = own.shape
     n_rows = 2 * half
+    width_k = residuals.shape[1]
     pairs = first_pos.shape[0]
     tile = min(GATHER_TILE, pairs)
     grid_spec = pltpu.PrefetchScalarGridSpec(
@@ -77,22 +85,32 @@
             pl.BlockSpec((half, width), lambda i, p1, p2: (0, 0)),
             pl.BlockSpec((half, width), lambda i, p1, p2: (0, 0)),
             pl.BlockSpec((tile, 1), lambda i, p1, p2: (i, 0)),
-        ],
-        out_specs=pl.BlockSpec((tile, width), lambda i, p1, p2: (i, 0)),
+            pl.BlockSpec(residuals.shape, lambda i, p1, p2: (0, 0)),
+            pl.BlockSpec((1, width_k), lambda i, p1, p2: (0, 0)),
+        ],
+        out_specs=[
+            pl.BlockSpec((tile, width_k), lambda i, p1, p2: (i, 0)),
+            pl.BlockSpec((tile, 1), lambda i, p1, p2: (i, 0)),
+            pl.BlockSpec((tile, 1), lambda i, p1, p2: (i, 0)),
+        ],
         scratch_shapes=[pltpu.VMEM((n_rows, width), jnp.float32)]
         + [pltpu.VMEM((tile, width), jnp.float32)] * 2,
     )
     return pl.pallas_call(
         gather_kernel,
         grid_spec=grid_spec,
-        out_shape=jax.ShapeDtypeStruct((pairs, width), jnp.bfloat16),
+        out_shape=[
+            jax.ShapeDtypeStruct((pairs, width_k), jnp.bfloat16),
+            jax.ShapeDtypeStruct((pairs, 1), jnp.float32),
+            jax.ShapeDtypeStruct((pairs, 1), jnp.float32),
+        ],
         compiler_params=pltpu.CompilerParams(
             dimension_semantics=("arbitrary",), vmem_limit_bytes=60 * 1024 * 1024
         ),
         cost_estimate=pl.CostEstimate(
-            flops=10 * pairs * width, transcendentals=0,
+            flops=(10 + 2 * width_k) * pairs * width, transcendentals=0,
             bytes_accessed=n_rows * width * 2 + pairs * width * 2),
-    )(first_pos, second_pos, own, other, operator_id[:, None])
+    )(first_pos, second_pos, own, other, operator_id[:, None], residuals, col_part[None, :])
 
 
 def ring_gather(block, axis, n):
@@ -146,19 +164,13 @@
         x_slot = (x - my_x + n_x) % n_x
         return ((half * n_x + x_slot) * n_zh + zh) * local_rows + r
 
-    built = build_descriptors(
-        rows, other, position(pair_list[0]), position(pair_list[1]), pair_list[2]
-    )
-
-    product = jnp.dot(built, residuals, preferred_element_type=jnp.float32)
-    widened = built.astype(jnp.float32)
-    first_sums = jnp.sum(widened, axis=1)
-    square_sums = jnp.sum(widened * widened, axis=1)
     col_part = jnp.sum(residuals.astype(jnp.float32), axis=0)
     local_samples = residuals.shape[0]
 
-    local_means = first_sums / local_samples
-    centred = product - local_means[:, None] * col_part[None, :]
+    centred, first_sums, square_sums = build_descriptors(
+        rows, other, position(pair_list[0]), position(pair_list[1]), pair_list[2],
+        residuals, col_part,
+    )
 
     blocks = local_pairs // width_k
     block_rows = width_k + EXTRA_ROWS
@@ -172,7 +184,7 @@
         axis=1,
     )
     packed = jnp.concatenate(
-        [centred.astype(jnp.bfloat16).reshape(blocks, width_k, width_k), extras], axis=1
+        [centred.reshape(blocks, width_k, width_k), extras], axis=1
     )
     arrived = lax.all_to_all(packed, SAMP_AXES, 0, 0, tiled=False)
     centred_sum = jnp.sum(arrived[:, :width_k].astype(jnp.float32), axis=0)

time: 152 us -> 152 us (level)
    reduce_sum x1 -> x0, other arithmetic: 3.29 us -> none  [per_device(): square_sums = jnp.sum(widened * widened, axis=1)]
    pallas_call x0 -> x2, other arithmetic: none -> 2.96 us  [build_descriptors(): pl.pallas_call(gather_kernel, grid_spec=grid_spec, out_shape=[jax.ShapeDt...]
    pallas_call x1, Pallas kernels: 28.1 us -> 29.6 us  [build_descriptors(): pl.pallas_call(gather_kernel, grid_spec=grid_spec, out_shape=[jax.ShapeDt...]
where the time goes in v15:
time: 152 us; the launch traced here: 151 us
  blocking collectives  72.3 us (48%)
  Pallas kernels  29.6 us (19%)
  waiting for transfers between devices  26.8 us (18%)
  starting transfers between devices  13.7 us (9%)
  other arithmetic  4.09 us (3%)
  local copies, waits for them, and re-layouts  3.4 us (2%)
    all_to_all x1, blocking collectives, per_device(): arrived = lax.all_to_all(packed, SAMP_AXES, 0, 0, tiled=False)  53.1 us
    pallas_call x1, Pallas kernels, build_descriptors(): pl.pallas_call(gather_kernel, grid_spec=grid_spec, out_shape=[jax.ShapeDt...  29.6 us
    all_gather x1, blocking collectives, per_device(): rows = lax.all_gather(tier_one, 'zh', axis=0, tiled=True)  19.2 us
    ppermute x1, waiting for transfers between devices, ring_gather(): from_left = lax.ppermute(block, axis, perm=fwd)  14.7 us
    ppermute x1, waiting for transfers between devices, ring_gather(): far_a = lax.ppermute(from_left[:half], axis, perm=fwd)  4.9 us
    ppermute x1, waiting for transfers between devices, ring_gather(): far_b = lax.ppermute(from_right[half:], axis, perm=bwd)  4.3 us
    ppermute x1, starting transfers between devices, ring_gather(): from_right = lax.ppermute(block, axis, perm=bwd)  3.46 us
    ppermute x1, starting transfers between devices, ring_gather(): far_a = lax.ppermute(from_left[:half], axis, perm=fwd)  3.41 us
  transfers between devices with their start and end apart: 5, of which 4 were waited for; matrix products, arithmetic and copies ran while one was open for 2% of the time, Pallas kernels for 0%

profile of v15, /device:TPU:6, one launch (start us, length us, event | category | flops | bytes accessed | tf_op | source)
XLA Modules:
  0.0 151.2 jit_solution(17328530661180584982)
XLA Ops:
  0.0 19.2 %all_gather.3 = bf16[1024,384]{1,0:T(8,128)(2,1)S(1)} all-gather(bf16[512,384]{1,0:T(8,128)(2,1)} %param.3), channel_id=1, replica_groups=mesh['x'=4,'zh'=2,'c'=2,'y'=8,'zl'=4] {'zh'}, dimensions={0}, use_global_device_ids=true | all-gather | bytes 1179648 | tf_op jit(solution)/shard_map/all_gather | solution.py:154
  19.2 2.4 %collective-permute-start.1 = (bf16[1024,384]{1,0:T(8,128)(2,1)S(1)}, bf16[1024,384]{1,0:T(8,128)(2,1)S(1)}, u32[]{:S(2)}, u32[]{:S(2)}) collective-permute-start(bf16[1024,384]{1,0:T(8,128)(2,1)S(1)} %all_gather.3), channel_id=1, source_target_pairs={{0,128},{128,256},{256,384},{384,0},{1,129},{129,257},{257,385},{3... | collective-permute-start | bytes 2359304 | tf_op jit(solution)/shard_map/ppermute | solution.py:120
  21.6 3.5 %collective-permute-start = (bf16[1024,384]{1,0:T(8,128)(2,1)S(1)}, bf16[1024,384]{1,0:T(8,128)(2,1)S(1)}, u32[]{:S(2)}, u32[]{:S(2)}) collective-permute-start(bf16[1024,384]{1,0:T(8,128)(2,1)S(1)} %all_gather.3), channel_id=1, source_target_pairs={{0,384},{128,0},{256,128},{384,256},{1,385},{129,1},{257,129},{385... | collective-permute-start | bytes 2359304 | tf_op jit(solution)/shard_map/ppermute | solution.py:121
  25.0 14.7 %collective-permute-done.1 = bf16[1024,384]{1,0:T(8,128)(2,1)S(1)} collective-permute-done((bf16[1024,384]{1,0:T(8,128)(2,1)S(1)}, bf16[1024,384]{1,0:T(8,128)(2,1)S(1)}, u32[]{:S(2)}, u32[]{:S(2)}) %collective-permute-start.1) | collective-permute-done | bytes 786464 | tf_op jit(solution)/shard_map/ppermute | solution.py:120
  39.8 3.4 %collective-permute-start.2 = (bf16[512,384]{1,0:T(8,128)(2,1)S(1)}, bf16[512,384]{1,0:T(8,128)(2,1)S(1)}, u32[]{:S(2)}, u32[]{:S(2)}) collective-permute-start(bf16[512,384]{1,0:T(8,128)(2,1)S(1)} %slice.64), channel_id=1, source_target_pairs={{0,128},{128,256},{256,384},{384,0},{1,129},{129,257},{257,385},{3... | collective-permute-start | bytes 1179656 | tf_op jit(solution)/shard_map/ppermute | solution.py:123
  43.2 0.0 collective-permute-done
  43.3 0.0 copy-start.4
  43.3 2.6 %collective-permute-start.3 = (bf16[512,384]{1,0:T(8,128)(2,1)S(1)}, bf16[512,384]{1,0:T(8,128)(2,1)S(1)}, u32[]{:S(2)}, u32[]{:S(2)}) collective-permute-start(bf16[512,384]{1,0:T(8,128)(2,1)S(1)} %slice.65), channel_id=1, source_target_pairs={{0,384},{128,0},{256,128},{384,256},{1,385},{129,1},{257,129},{385... | collective-permute-start | bytes 1179656 | tf_op jit(solution)/shard_map/ppermute | solution.py:124
  45.9 0.1 constant_dynamic-update-slice_fusion.4
  45.9 0.0 copy-start.3
  46.0 0.2 constant_dynamic-update-slice_fusion.3
  46.1 4.9 %collective-permute-done.2 = bf16[512,384]{1,0:T(8,128)(2,1)S(1)} collective-permute-done((bf16[512,384]{1,0:T(8,128)(2,1)S(1)}, bf16[512,384]{1,0:T(8,128)(2,1)S(1)}, u32[]{:S(2)}, u32[]{:S(2)}) %collective-permute-start.2) | collective-permute-done | bytes 393248 | tf_op jit(solution)/shard_map/ppermute | solution.py:123
  51.0 0.1 constant_dynamic-update-slice_fusion.2
  51.1 4.3 %collective-permute-done.3 = bf16[512,384]{1,0:T(8,128)(2,1)S(1)} collective-permute-done((bf16[512,384]{1,0:T(8,128)(2,1)S(1)}, bf16[512,384]{1,0:T(8,128)(2,1)S(1)}, u32[]{:S(2)}, u32[]{:S(2)}) %collective-permute-start.3) | collective-permute-done | bytes 393248 | tf_op jit(solution)/shard_map/ppermute | solution.py:124
  55.4 0.1 constant_dynamic-update-slice_fusion.1
  55.5 0.2 constant_dynamic-update-slice_fusion.own_ref
  55.6 0.0 copy-start
  55.6 1.9 %collective-permute-start.4 = (bf16[4096,384]{1,0:T(8,128)(2,1)S(1)}, bf16[4096,384]{1,0:T(8,128)(2,1)}, u32[]{:S(2)}, u32[]{:S(2)}) collective-permute-start(bf16[4096,384]{1,0:T(8,128)(2,1)S(1)} %constant_dynamic-update-slice_fusion.own_ref), channel_id=1, source_target_pairs={{0,32},{32,0},{1,33},{33,1},{2,34},{34,2},{3,35},{35,3},{4,36},{36... | collective-permute-start | bytes 9437192 | tf_op jit(solution)/shard_map/ppermute | solution.py:156
  57.6 0.0 copy-done.4
  57.6 2.0 %copy.10.op_ref = s32[4096,1]{1,0:T(8,128)} copy(s32[4096,1]{0,1:T(1,128)S(1)} %get-tuple-element.19) | data formatting | bytes 32768 | tf_op jit(solution)/shard_map/broadcast_in_dim;squeeze | solution.py:113
  59.6 0.0 copy-done.3
  59.6 0.1 convert_reduce_fusion.1
  59.7 0.0 copy-start.5
  59.7 0.7 fusion.14
  60.4 2.9 %collective-permute-done.4.other_ref = bf16[4096,384]{1,0:T(8,128)(2,1)} collective-permute-done((bf16[4096,384]{1,0:T(8,128)(2,1)S(1)}, bf16[4096,384]{1,0:T(8,128)(2,1)}, u32[]{:S(2)}, u32[]{:S(2)}) %collective-permute-start.4) | collective-permute-done | bytes 3145760 | tf_op jit(solution)/shard_map/ppermute | solution.py:156
  63.3 0.0 copy-done
  63.3 0.0 copy-done.5
  63.3 29.6 %shard_map.37 = (bf16[4096,128]{1,0:T(8,128)(2,1)}, f32[4096,1]{1,0:T(8,128)}, f32[4096,1]{1,0:T(8,128)}) custom-call(s32[4096]{0:T(1024)} %get-tuple-element.33.first_ref, s32[4096]{0:T(1024)} %get-tuple-element.34.second_ref, bf16[4096,384]{1,0:T(8,128)(2,1)} %copy-done, bf16[4096,384]{1,0:T(8,128)(2,1)} %collective-permute-done.4.other_ref, ...), custom_call_target="tpu_custom_call" | custom-call | flops 418381824 | bytes 9437184 | tf_op jit(solution)/shard_map/pallas_call | solution.py:99
  93.0 0.0 copy-start.1
  93.0 0.0 copy-start.2
  93.0 2.4 %reduce.3 = f32[4096]{0:T(1024)S(1)} reduce(f32[4096,1]{1,0:T(8,128)} %get-tuple-element.9, f32[]{:T(128)} %constant.144), dimensions={1}, to_apply=%get-tuple-element.9.reduce_sub_computation | reduce | bytes 32772 | tf_op jit(solution)/shard_map/pallas_call | solution.py:99
  95.4 0.0 copy-done.1
  95.4 0.6 reduce.4
  96.2 0.0 copy-done.2
  96.2 0.6 concatenate.8
  96.8 53.1 %all_to_all.5 = bf16[32,144,128]{2,1,0:T(8,128)(2,1)S(1)} all-to-all(bf16[32,144,128]{2,1,0:T(8,128)(2,1)S(1)} %concatenate.8), channel_id=1, replica_groups=mesh['x'=4,'zh'=2,'c'=2,'y'=8,'zl'=4] {'y','zl'}, dimensions={0} | all-to-all | bytes 2359296 | tf_op jit(solution)/shard_map/all_to_all | solution.py:189
  150.0 0.1 fusion.35
  150.1 0.2 convert_reduce_fusion
  150.3 0.9 fusion.2
  (19 shorter events, 0.3 us)
Async XLA Ops:
  19.2 20.6 %collective-permute-start.1 = (bf16[1024,384]{1,0:T(8,128)(2,1)S(1)}, bf16[1024,384]{1,0:T(8,128)(2,1)S(1)}, u32[]{:S(2)}, u32[]{:S(2)}) collective-permute-start(bf16[1024,384]{1,0:T(8,128)(2,1)S(1)} %all_gather.3), channel_id=1, source_target_pairs={{0,128},{128,256},{256,384},{384,0},{1,129},{129,257},{257,385},{3... | collective-permute-start | bytes 2359304 | tf_op jit(solution)/shard_map/ppermute | solution.py:120
  21.6 21.6 %collective-permute-start = (bf16[1024,384]{1,0:T(8,128)(2,1)S(1)}, bf16[1024,384]{1,0:T(8,128)(2,1)S(1)}, u32[]{:S(2)}, u32[]{:S(2)}) collective-permute-start(bf16[1024,384]{1,0:T(8,128)(2,1)S(1)} %all_gather.3), channel_id=1, source_target_pairs={{0,384},{128,0},{256,128},{384,256},{1,385},{129,1},{257,129},{385... | collective-permute-start | bytes 2359304 | tf_op jit(solution)/shard_map/ppermute | solution.py:121
  39.8 11.2 %collective-permute-start.2 = (bf16[512,384]{1,0:T(8,128)(2,1)S(1)}, bf16[512,384]{1,0:T(8,128)(2,1)S(1)}, u32[]{:S(2)}, u32[]{:S(2)}) collective-permute-start(bf16[512,384]{1,0:T(8,128)(2,1)S(1)} %slice.64), channel_id=1, source_target_pairs={{0,128},{128,256},{256,384},{384,0},{1,129},{129,257},{257,385},{3... | collective-permute-start | bytes 1179656 | tf_op jit(solution)/shard_map/ppermute | solution.py:123
  43.3 14.3 %copy-start.4 = (s32[3,4096]{1,0:T(4,128)S(1)}, s32[3,4096]{1,0:T(4,128)}, u32[]{:S(2)}) copy-start(s32[3,4096]{1,0:T(4,128)} %param.5) | copy-start | bytes 147460
  43.3 12.1 %collective-permute-start.3 = (bf16[512,384]{1,0:T(8,128)(2,1)S(1)}, bf16[512,384]{1,0:T(8,128)(2,1)S(1)}, u32[]{:S(2)}, u32[]{:S(2)}) collective-permute-start(bf16[512,384]{1,0:T(8,128)(2,1)S(1)} %slice.65), channel_id=1, source_target_pairs={{0,384},{128,0},{256,128},{384,256},{1,385},{129,1},{257,129},{385... | collective-permute-start | bytes 1179656 | tf_op jit(solution)/shard_map/ppermute | solution.py:124
  45.9 13.7 %copy-start.3 = (bf16[384,128]{1,0:T(8,128)(2,1)S(1)}, bf16[384,128]{1,0:T(8,128)(2,1)}, u32[]{:S(2)}) copy-start(bf16[384,128]{1,0:T(8,128)(2,1)} %res_ref.1) | copy-start | bytes 294916
  55.6 7.7 %copy-start = (bf16[4096,384]{1,0:T(8,128)(2,1)}, bf16[4096,384]{1,0:T(8,128)(2,1)S(1)}, u32[]{:S(2)}) copy-start(bf16[4096,384]{1,0:T(8,128)(2,1)S(1)} %constant_dynamic-update-slice_fusion.own_ref) | copy-start | bytes 9437188
  55.6 7.7 %collective-permute-start.4 = (bf16[4096,384]{1,0:T(8,128)(2,1)S(1)}, bf16[4096,384]{1,0:T(8,128)(2,1)}, u32[]{:S(2)}, u32[]{:S(2)}) collective-permute-start(bf16[4096,384]{1,0:T(8,128)(2,1)S(1)} %constant_dynamic-update-slice_fusion.own_ref), channel_id=1, source_target_pairs={{0,32},{32,0},{1,33},{33,1},{2,34},{34,2},{3,35},{35,3},{4,36},{36... | collective-permute-start | bytes 9437192 | tf_op jit(solution)/shard_map/ppermute | solution.py:156
  59.7 3.6 %copy-start.5 = (f32[128]{0:T(128)}, f32[128]{0:T(128)S(1)}, u32[]{:S(2)}) copy-start(f32[128]{0:T(128)S(1)} %convert_reduce_fusion.1) | copy-start | bytes 1540
  93.0 2.4 %copy-start.1 = (f32[4096,1]{1,0:T(8,128)S(1)}, f32[4096,1]{1,0:T(8,128)}, u32[]{:S(2)}) copy-start(f32[4096,1]{1,0:T(8,128)} %get-tuple-element.10) | copy-start | bytes 49156
  93.0 3.2 %copy-start.2 = (bf16[4096,128]{1,0:T(8,128)(2,1)S(1)}, bf16[4096,128]{1,0:T(8,128)(2,1)}, u32[]{:S(2)}) copy-start(bf16[4096,128]{1,0:T(8,128)(2,1)} %get-tuple-element.8) | copy-start | bytes 3145732

commit v16 on v14

--- a/solution.py
+++ b/solution.py
@@ -14,7 +14,7 @@
 FEAT_AXES = ("x", "zh", "c")
 SAMP_AXES = ("y", "zl")
 EXTRA_ROWS = 16
-GATHER_TILE = 512
+GATHER_TILE = 1024
 
 
 def combine_rows(first_rows, second_rows, operator_id):

time: 152 us -> 152 us (level)
  no operation moved by 1% of the time
where the time goes in v16:
time: 152 us; the launch traced here: 151 us
  blocking collectives  72.3 us (48%)
  Pallas kernels  28.1 us (18%)
  waiting for transfers between devices  26.9 us (18%)
  starting transfers between devices  13.7 us (9%)
  other arithmetic  4.43 us (3%)
  local copies, waits for them, and re-layouts  3.36 us (2%)
  matrix products  2.11 us (1%)
    all_to_all x1, blocking collectives, per_device(): arrived = lax.all_to_all(packed, SAMP_AXES, 0, 0, tiled=False)  53.1 us
    pallas_call x1, Pallas kernels, build_descriptors(): pl.pallas_call(gather_kernel, grid_spec=grid_spec, out_shape=jax.ShapeDty...  28.1 us
    all_gather x1, blocking collectives, per_device(): rows = lax.all_gather(tier_one, 'zh', axis=0, tiled=True)  19.2 us
    ppermute x1, waiting for transfers between devices, ring_gather(): from_left = lax.ppermute(block, axis, perm=fwd)  14.7 us
    ppermute x1, waiting for transfers between devices, ring_gather(): far_a = lax.ppermute(from_left[:half], axis, perm=fwd)  4.9 us
    ppermute x1, waiting for transfers between devices, ring_gather(): far_b = lax.ppermute(from_right[half:], axis, perm=bwd)  4.3 us
    ppermute x1, starting transfers between devices, ring_gather(): from_right = lax.ppermute(block, axis, perm=bwd)  3.46 us
    ppermute x1, starting transfers between devices, ring_gather(): far_a = lax.ppermute(from_left[:half], axis, perm=fwd)  3.41 us
  transfers between devices with their start and end apart: 5, of which 4 were waited for; matrix products, arithmetic and copies ran while one was open for 2% of the time, Pallas kernels for 0%

profile of v16, /device:TPU:6, one launch (start us, length us, event | category | flops | bytes accessed | tf_op | source)
XLA Modules:
  0.0 151.2 jit_solution(15511164896249893211)
XLA Ops:
  0.0 19.2 %all_gather.3 = bf16[1024,384]{1,0:T(8,128)(2,1)S(1)} all-gather(bf16[512,384]{1,0:T(8,128)(2,1)} %param.3), channel_id=1, replica_groups=mesh['x'=4,'zh'=2,'c'=2,'y'=8,'zl'=4] {'zh'}, dimensions={0}, use_global_device_ids=true | all-gather | bytes 1179648 | tf_op jit(solution)/shard_map/all_gather | solution.py:136
  19.2 2.4 %collective-permute-start.1 = (bf16[1024,384]{1,0:T(8,128)(2,1)S(1)}, bf16[1024,384]{1,0:T(8,128)(2,1)S(1)}, u32[]{:S(2)}, u32[]{:S(2)}) collective-permute-start(bf16[1024,384]{1,0:T(8,128)(2,1)S(1)} %all_gather.3), channel_id=1, source_target_pairs={{0,128},{128,256},{256,384},{384,0},{1,129},{129,257},{257,385},{3... | collective-permute-start | bytes 2359304 | tf_op jit(solution)/shard_map/ppermute | solution.py:102
  21.6 3.5 %collective-permute-start = (bf16[1024,384]{1,0:T(8,128)(2,1)S(1)}, bf16[1024,384]{1,0:T(8,128)(2,1)S(1)}, u32[]{:S(2)}, u32[]{:S(2)}) collective-permute-start(bf16[1024,384]{1,0:T(8,128)(2,1)S(1)} %all_gather.3), channel_id=1, source_target_pairs={{0,384},{128,0},{256,128},{384,256},{1,385},{129,1},{257,129},{385... | collective-permute-start | bytes 2359304 | tf_op jit(solution)/shard_map/ppermute | solution.py:103
  25.0 14.7 %collective-permute-done.1 = bf16[1024,384]{1,0:T(8,128)(2,1)S(1)} collective-permute-done((bf16[1024,384]{1,0:T(8,128)(2,1)S(1)}, bf16[1024,384]{1,0:T(8,128)(2,1)S(1)}, u32[]{:S(2)}, u32[]{:S(2)}) %collective-permute-start.1) | collective-permute-done | bytes 786464 | tf_op jit(solution)/shard_map/ppermute | solution.py:102
  39.8 3.4 %collective-permute-start.2 = (bf16[512,384]{1,0:T(8,128)(2,1)S(1)}, bf16[512,384]{1,0:T(8,128)(2,1)S(1)}, u32[]{:S(2)}, u32[]{:S(2)}) collective-permute-start(bf16[512,384]{1,0:T(8,128)(2,1)S(1)} %slice.64), channel_id=1, source_target_pairs={{0,128},{128,256},{256,384},{384,0},{1,129},{129,257},{257,385},{3... | collective-permute-start | bytes 1179656 | tf_op jit(solution)/shard_map/ppermute | solution.py:105
  43.2 0.0 collective-permute-done
  43.3 0.0 copy-start.3
  43.3 2.6 %collective-permute-start.3 = (bf16[512,384]{1,0:T(8,128)(2,1)S(1)}, bf16[512,384]{1,0:T(8,128)(2,1)S(1)}, u32[]{:S(2)}, u32[]{:S(2)}) collective-permute-start(bf16[512,384]{1,0:T(8,128)(2,1)S(1)} %slice.65), channel_id=1, source_target_pairs={{0,384},{128,0},{256,128},{384,256},{1,385},{129,1},{257,129},{385... | collective-permute-start | bytes 1179656 | tf_op jit(solution)/shard_map/ppermute | solution.py:106
  45.9 0.1 constant_dynamic-update-slice_fusion.4
  45.9 0.0 copy-start.2
  46.0 0.2 constant_dynamic-update-slice_fusion.3
  46.1 4.9 %collective-permute-done.2 = bf16[512,384]{1,0:T(8,128)(2,1)S(1)} collective-permute-done((bf16[512,384]{1,0:T(8,128)(2,1)S(1)}, bf16[512,384]{1,0:T(8,128)(2,1)S(1)}, u32[]{:S(2)}, u32[]{:S(2)}) %collective-permute-start.2) | collective-permute-done | bytes 393248 | tf_op jit(solution)/shard_map/ppermute | solution.py:105
  51.0 0.1 constant_dynamic-update-slice_fusion.2
  51.1 4.3 %collective-permute-done.3 = bf16[512,384]{1,0:T(8,128)(2,1)S(1)} collective-permute-done((bf16[512,384]{1,0:T(8,128)(2,1)S(1)}, bf16[512,384]{1,0:T(8,128)(2,1)S(1)}, u32[]{:S(2)}, u32[]{:S(2)}) %collective-permute-start.3) | collective-permute-done | bytes 393248 | tf_op jit(solution)/shard_map/ppermute | solution.py:106
  55.4 0.1 constant_dynamic-update-slice_fusion.1
  55.5 0.2 constant_dynamic-update-slice_fusion.own_ref
  55.6 0.0 copy-start.1
  55.6 1.9 %collective-permute-start.4 = (bf16[4096,384]{1,0:T(8,128)(2,1)S(1)}, bf16[4096,384]{1,0:T(8,128)(2,1)}, u32[]{:S(2)}, u32[]{:S(2)}) collective-permute-start(bf16[4096,384]{1,0:T(8,128)(2,1)S(1)} %constant_dynamic-update-slice_fusion.own_ref), channel_id=1, source_target_pairs={{0,32},{32,0},{1,33},{33,1},{2,34},{34,2},{3,35},{35,3},{4,36},{36... | collective-permute-start | bytes 9437192 | tf_op jit(solution)/shard_map/ppermute | solution.py:138
  57.6 0.0 copy-done.3
  57.6 2.0 %copy.5.op_ref = s32[4096,1]{1,0:T(8,128)} copy(s32[4096,1]{0,1:T(1,128)S(1)} %get-tuple-element.15) | data formatting | bytes 32768 | tf_op jit(solution)/shard_map/broadcast_in_dim;squeeze | solution.py:95
  59.6 0.0 copy-done.2
  59.6 0.1 convert_reduce_fusion.2
  59.7 0.7 fusion.16
  60.4 2.9 %collective-permute-done.4.other_ref = bf16[4096,384]{1,0:T(8,128)(2,1)} collective-permute-done((bf16[4096,384]{1,0:T(8,128)(2,1)S(1)}, bf16[4096,384]{1,0:T(8,128)(2,1)}, u32[]{:S(2)}, u32[]{:S(2)}) %collective-permute-start.4) | collective-permute-done | bytes 3145760 | tf_op jit(solution)/shard_map/ppermute | solution.py:138
  63.3 0.0 copy-done.1
  63.3 28.1 %shard_map.37 = bf16[4096,384]{1,0:T(8,128)(2,1)} custom-call(s32[4096]{0:T(1024)} %get-tuple-element.29.first_ref, s32[4096]{0:T(1024)} %get-tuple-element.30.second_ref, bf16[4096,384]{1,0:T(8,128)(2,1)} %copy-done.1, bf16[4096,384]{1,0:T(8,128)(2,1)} %collective-permute-done.4.other_ref, s32[4096,1]{1,0:T(8,128)} %copy.5.op_ref), custom_call_target="tpu_custom_call" | custom-call | flops 15728640 | bytes 9437184 | tf_op jit(solution)/shard_map/pallas_call | solution.py:85
  91.4 0.0 copy-start
  91.5 3.3 %fusion = (f32[4096]{0:T(1024)S(1)}, f32[4096]{0:T(1024)S(1)}) fusion(bf16[4096,384]{1,0:T(8,128)(2,1)} %shard_map.37), kind=kLoop, calls=%fused_computation.2 | loop fusion | flops 6283264 | bytes 3178496 | tf_op jit(solution)/shard_map/reduce_sum | solution.py:156
  94.8 0.0 copy-done
  94.8 1.2 fusion.1
  96.2 0.6 concatenate.8
  96.8 53.1 %all_to_all.5 = bf16[32,144,128]{2,1,0:T(8,128)(2,1)S(1)} all-to-all(bf16[32,144,128]{2,1,0:T(8,128)(2,1)S(1)} %concatenate.8), channel_id=1, replica_groups=mesh['x'=4,'zh'=2,'c'=2,'y'=8,'zl'=4] {'y','zl'}, dimensions={0} | all-to-all | bytes 2359296 | tf_op jit(solution)/shard_map/all_to_all | solution.py:177
  150.0 0.1 fusion.37
  150.1 0.2 convert_reduce_fusion.1
  150.3 0.9 fusion.4
  (20 shorter events, 0.3 us)
Async XLA Ops:
  19.2 20.6 %collective-permute-start.1 = (bf16[1024,384]{1,0:T(8,128)(2,1)S(1)}, bf16[1024,384]{1,0:T(8,128)(2,1)S(1)}, u32[]{:S(2)}, u32[]{:S(2)}) collective-permute-start(bf16[1024,384]{1,0:T(8,128)(2,1)S(1)} %all_gather.3), channel_id=1, source_target_pairs={{0,128},{128,256},{256,384},{384,0},{1,129},{129,257},{257,385},{3... | collective-permute-start | bytes 2359304 | tf_op jit(solution)/shard_map/ppermute | solution.py:102
  21.6 21.6 %collective-permute-start = (bf16[1024,384]{1,0:T(8,128)(2,1)S(1)}, bf16[1024,384]{1,0:T(8,128)(2,1)S(1)}, u32[]{:S(2)}, u32[]{:S(2)}) collective-permute-start(bf16[1024,384]{1,0:T(8,128)(2,1)S(1)} %all_gather.3), channel_id=1, source_target_pairs={{0,384},{128,0},{256,128},{384,256},{1,385},{129,1},{257,129},{385... | collective-permute-start | bytes 2359304 | tf_op jit(solution)/shard_map/ppermute | solution.py:103
  39.8 11.2 %collective-permute-start.2 = (bf16[512,384]{1,0:T(8,128)(2,1)S(1)}, bf16[512,384]{1,0:T(8,128)(2,1)S(1)}, u32[]{:S(2)}, u32[]{:S(2)}) collective-permute-start(bf16[512,384]{1,0:T(8,128)(2,1)S(1)} %slice.64), channel_id=1, source_target_pairs={{0,128},{128,256},{256,384},{384,0},{1,129},{129,257},{257,385},{3... | collective-permute-start | bytes 1179656 | tf_op jit(solution)/shard_map/ppermute | solution.py:105
  43.3 14.3 %copy-start.3 = (s32[3,4096]{1,0:T(4,128)S(1)}, s32[3,4096]{1,0:T(4,128)}, u32[]{:S(2)}) copy-start(s32[3,4096]{1,0:T(4,128)} %param.5) | copy-start | bytes 147460
  43.3 12.1 %collective-permute-start.3 = (bf16[512,384]{1,0:T(8,128)(2,1)S(1)}, bf16[512,384]{1,0:T(8,128)(2,1)S(1)}, u32[]{:S(2)}, u32[]{:S(2)}) collective-permute-start(bf16[512,384]{1,0:T(8,128)(2,1)S(1)} %slice.65), channel_id=1, source_target_pairs={{0,384},{128,0},{256,128},{384,256},{1,385},{129,1},{257,129},{385... | collective-permute-start | bytes 1179656 | tf_op jit(solution)/shard_map/ppermute | solution.py:106
  45.9 13.6 %copy-start.2 = (bf16[384,128]{1,0:T(8,128)(2,1)S(1)}, bf16[384,128]{1,0:T(8,128)(2,1)}, u32[]{:S(2)}) copy-start(bf16[384,128]{1,0:T(8,128)(2,1)} %param.4) | copy-start | bytes 294916
  55.6 7.7 %copy-start.1 = (bf16[4096,384]{1,0:T(8,128)(2,1)}, bf16[4096,384]{1,0:T(8,128)(2,1)S(1)}, u32[]{:S(2)}) copy-start(bf16[4096,384]{1,0:T(8,128)(2,1)S(1)} %constant_dynamic-update-slice_fusion.own_ref) | copy-start | bytes 9437188
  55.6 7.7 %collective-permute-start.4 = (bf16[4096,384]{1,0:T(8,128)(2,1)S(1)}, bf16[4096,384]{1,0:T(8,128)(2,1)}, u32[]{:S(2)}, u32[]{:S(2)}) collective-permute-start(bf16[4096,384]{1,0:T(8,128)(2,1)S(1)} %constant_dynamic-update-slice_fusion.own_ref), channel_id=1, source_target_pairs={{0,32},{32,0},{1,33},{33,1},{2,34},{34,2},{3,35},{35,3},{4,36},{36... | collective-permute-start | bytes 9437192 | tf_op jit(solution)/shard_map/ppermute | solution.py:138
  91.4 3.3 %copy-start = (bf16[4096,384]{1,0:T(8,128)(2,1)S(1)}, bf16[4096,384]{1,0:T(8,128)(2,1)}, u32[]{:S(2)}) copy-start(bf16[4096,384]{1,0:T(8,128)(2,1)} %shard_map.37) | copy-start | bytes 9437188

commit v17 on v14

--- a/solution.py
+++ b/solution.py
@@ -174,7 +174,10 @@
     packed = jnp.concatenate(
         [centred.astype(jnp.bfloat16).reshape(blocks, width_k, width_k), extras], axis=1
     )
-    arrived = lax.all_to_all(packed, SAMP_AXES, 0, 0, tiled=False)
+    by_zl = packed.reshape(n_y, n_zl, block_rows, width_k).transpose(1, 0, 2, 3)
+    arrived = lax.all_to_all(
+        by_zl.reshape(blocks, block_rows, width_k), ("zl", "y"), 0, 0, tiled=False
+    )
     centred_sum = jnp.sum(arrived[:, :width_k].astype(jnp.float32), axis=0)
     pieces = arrived[:, width_k:].astype(jnp.float32)
 

time: 152 us -> 151 us (level)
  no operation moved by 1% of the time
where the time goes in v17:
time: 151 us
  blocking collectives  71.6 us (47%)
  Pallas kernels  28.1 us (19%)
  waiting for transfers between devices  26.9 us (18%)
  starting transfers between devices  13.7 us (9%)
  other arithmetic  4.43 us (3%)
  local copies, waits for them, and re-layouts  3.49 us (2%)
  matrix products  2.11 us (1%)
    all_to_all x1, blocking collectives, per_device(): lax.all_to_all(by_zl.reshape(blocks, block_rows, width_k), ('zl', 'y'), 0...  52.4 us
    pallas_call x1, Pallas kernels, build_descriptors(): pl.pallas_call(gather_kernel, grid_spec=grid_spec, out_shape=jax.ShapeDty...  28.1 us
    all_gather x1, blocking collectives, per_device(): rows = lax.all_gather(tier_one, 'zh', axis=0, tiled=True)  19.2 us
    ppermute x1, waiting for transfers between devices, ring_gather(): from_left = lax.ppermute(block, axis, perm=fwd)  14.7 us
    ppermute x1, waiting for transfers between devices, ring_gather(): far_a = lax.ppermute(from_left[:half], axis, perm=fwd)  4.9 us
    ppermute x1, waiting for transfers between devices, ring_gather(): far_b = lax.ppermute(from_right[half:], axis, perm=bwd)  4.3 us
    ppermute x1, starting transfers between devices, ring_gather(): from_right = lax.ppermute(block, axis, perm=bwd)  3.46 us
    ppermute x1, starting transfers between devices, ring_gather(): far_a = lax.ppermute(from_left[:half], axis, perm=fwd)  3.41 us
  transfers between devices with their start and end apart: 5, of which 4 were waited for; matrix products, arithmetic and copies ran while one was open for 2% of the time, Pallas kernels for 0%

profile of v17, /device:TPU:6, one launch (start us, length us, event | category | flops | bytes accessed | tf_op | source)
XLA Modules:
  0.0 150.6 jit_solution(1670242652616342796)
XLA Ops:
  0.0 19.2 %all_gather.3 = bf16[1024,384]{1,0:T(8,128)(2,1)S(1)} all-gather(bf16[512,384]{1,0:T(8,128)(2,1)} %param.3), channel_id=1, replica_groups=mesh['x'=4,'zh'=2,'c'=2,'y'=8,'zl'=4] {'zh'}, dimensions={0}, use_global_device_ids=true | all-gather | bytes 1179648 | tf_op jit(solution)/shard_map/all_gather | solution.py:136
  19.2 2.4 %collective-permute-start.1 = (bf16[1024,384]{1,0:T(8,128)(2,1)S(1)}, bf16[1024,384]{1,0:T(8,128)(2,1)S(1)}, u32[]{:S(2)}, u32[]{:S(2)}) collective-permute-start(bf16[1024,384]{1,0:T(8,128)(2,1)S(1)} %all_gather.3), channel_id=1, source_target_pairs={{0,128},{128,256},{256,384},{384,0},{1,129},{129,257},{257,385},{3... | collective-permute-start | bytes 2359304 | tf_op jit(solution)/shard_map/ppermute | solution.py:102
  21.6 3.5 %collective-permute-start = (bf16[1024,384]{1,0:T(8,128)(2,1)S(1)}, bf16[1024,384]{1,0:T(8,128)(2,1)S(1)}, u32[]{:S(2)}, u32[]{:S(2)}) collective-permute-start(bf16[1024,384]{1,0:T(8,128)(2,1)S(1)} %all_gather.3), channel_id=1, source_target_pairs={{0,384},{128,0},{256,128},{384,256},{1,385},{129,1},{257,129},{385... | collective-permute-start | bytes 2359304 | tf_op jit(solution)/shard_map/ppermute | solution.py:103
  25.0 14.7 %collective-permute-done.1 = bf16[1024,384]{1,0:T(8,128)(2,1)S(1)} collective-permute-done((bf16[1024,384]{1,0:T(8,128)(2,1)S(1)}, bf16[1024,384]{1,0:T(8,128)(2,1)S(1)}, u32[]{:S(2)}, u32[]{:S(2)}) %collective-permute-start.1) | collective-permute-done | bytes 786464 | tf_op jit(solution)/shard_map/ppermute | solution.py:102
  39.8 3.4 %collective-permute-start.2 = (bf16[512,384]{1,0:T(8,128)(2,1)S(1)}, bf16[512,384]{1,0:T(8,128)(2,1)S(1)}, u32[]{:S(2)}, u32[]{:S(2)}) collective-permute-start(bf16[512,384]{1,0:T(8,128)(2,1)S(1)} %slice.64), channel_id=1, source_target_pairs={{0,128},{128,256},{256,384},{384,0},{1,129},{129,257},{257,385},{3... | collective-permute-start | bytes 1179656 | tf_op jit(solution)/shard_map/ppermute | solution.py:105
  43.2 0.0 collective-permute-done
  43.3 0.0 copy-start.3
  43.3 2.6 %collective-permute-start.3 = (bf16[512,384]{1,0:T(8,128)(2,1)S(1)}, bf16[512,384]{1,0:T(8,128)(2,1)S(1)}, u32[]{:S(2)}, u32[]{:S(2)}) collective-permute-start(bf16[512,384]{1,0:T(8,128)(2,1)S(1)} %slice.65), channel_id=1, source_target_pairs={{0,384},{128,0},{256,128},{384,256},{1,385},{129,1},{257,129},{385... | collective-permute-start | bytes 1179656 | tf_op jit(solution)/shard_map/ppermute | solution.py:106
  45.9 0.1 constant_dynamic-update-slice_fusion.4
  45.9 0.0 copy-start.2
  46.0 0.2 constant_dynamic-update-slice_fusion.3
  46.1 4.9 %collective-permute-done.2 = bf16[512,384]{1,0:T(8,128)(2,1)S(1)} collective-permute-done((bf16[512,384]{1,0:T(8,128)(2,1)S(1)}, bf16[512,384]{1,0:T(8,128)(2,1)S(1)}, u32[]{:S(2)}, u32[]{:S(2)}) %collective-permute-start.2) | collective-permute-done | bytes 393248 | tf_op jit(solution)/shard_map/ppermute | solution.py:105
  51.0 0.1 constant_dynamic-update-slice_fusion.2
  51.1 4.3 %collective-permute-done.3 = bf16[512,384]{1,0:T(8,128)(2,1)S(1)} collective-permute-done((bf16[512,384]{1,0:T(8,128)(2,1)S(1)}, bf16[512,384]{1,0:T(8,128)(2,1)S(1)}, u32[]{:S(2)}, u32[]{:S(2)}) %collective-permute-start.3) | collective-permute-done | bytes 393248 | tf_op jit(solution)/shard_map/ppermute | solution.py:106
  55.4 0.1 constant_dynamic-update-slice_fusion.1
  55.5 0.2 constant_dynamic-update-slice_fusion.own_ref
  55.6 0.0 copy-start.1
  55.6 1.9 %collective-permute-start.4 = (bf16[4096,384]{1,0:T(8,128)(2,1)S(1)}, bf16[4096,384]{1,0:T(8,128)(2,1)}, u32[]{:S(2)}, u32[]{:S(2)}) collective-permute-start(bf16[4096,384]{1,0:T(8,128)(2,1)S(1)} %constant_dynamic-update-slice_fusion.own_ref), channel_id=1, source_target_pairs={{0,32},{32,0},{1,33},{33,1},{2,34},{34,2},{3,35},{35,3},{4,36},{36... | collective-permute-start | bytes 9437192 | tf_op jit(solution)/shard_map/ppermute | solution.py:138
  57.6 0.0 copy-done.3
  57.6 2.0 %copy.14.op_ref = s32[4096,1]{1,0:T(8,128)} copy(s32[4096,1]{0,1:T(1,128)S(1)} %get-tuple-element.15) | data formatting | bytes 32768 | tf_op jit(solution)/shard_map/broadcast_in_dim;squeeze | solution.py:95
  59.6 0.0 copy-done.2
  59.6 0.1 convert_reduce_fusion.2
  59.7 0.7 fusion.16
  60.4 2.9 %collective-permute-done.4.other_ref = bf16[4096,384]{1,0:T(8,128)(2,1)} collective-permute-done((bf16[4096,384]{1,0:T(8,128)(2,1)S(1)}, bf16[4096,384]{1,0:T(8,128)(2,1)}, u32[]{:S(2)}, u32[]{:S(2)}) %collective-permute-start.4) | collective-permute-done | bytes 3145760 | tf_op jit(solution)/shard_map/ppermute | solution.py:138
  63.3 0.0 copy-done.1
  63.3 28.1 %shard_map.37 = bf16[4096,384]{1,0:T(8,128)(2,1)} custom-call(s32[4096]{0:T(1024)} %get-tuple-element.29.first_ref, s32[4096]{0:T(1024)} %get-tuple-element.30.second_ref, bf16[4096,384]{1,0:T(8,128)(2,1)} %copy-done.1, bf16[4096,384]{1,0:T(8,128)(2,1)} %collective-permute-done.4.other_ref, s32[4096,1]{1,0:T(8,128)} %copy.14.op_ref), custom_call_target="tpu_custom_call" | custom-call | flops 15728640 | bytes 9437184 | tf_op jit(solution)/shard_map/pallas_call | solution.py:85
  91.4 0.0 copy-start
  91.4 3.3 %fusion = (f32[4096]{0:T(1024)S(1)}, f32[4096]{0:T(1024)S(1)}) fusion(bf16[4096,384]{1,0:T(8,128)(2,1)} %shard_map.37), kind=kLoop, calls=%fused_computation.2 | loop fusion | flops 6283264 | bytes 3178496 | tf_op jit(solution)/shard_map/reduce_sum | solution.py:156
  94.7 0.0 copy-done
  94.7 1.2 fusion.1
  95.9 0.1 copy.19
  96.2 0.6 concatenate.18
  96.9 52.4 %all_to_all.5 = bf16[32,144,128]{2,1,0:T(8,128)(2,1)S(1)} all-to-all(bf16[32,144,128]{2,1,0:T(8,128)(2,1)S(1)} %bitcast.16), channel_id=1, replica_groups=mesh['x'=4,'zh'=2,'c'=2,'y'=8,'zl'=4] {'zl','y'}, dimensions={0} | all-to-all | bytes 2359296 | tf_op jit(solution)/shard_map/all_to_all | solution.py:178
  149.3 0.1 fusion.37
  149.5 0.2 convert_reduce_fusion.1
  149.7 0.9 fusion.4
  (20 shorter events, 0.3 us)
Async XLA Ops:
  19.2 20.6 %collective-permute-start.1 = (bf16[1024,384]{1,0:T(8,128)(2,1)S(1)}, bf16[1024,384]{1,0:T(8,128)(2,1)S(1)}, u32[]{:S(2)}, u32[]{:S(2)}) collective-permute-start(bf16[1024,384]{1,0:T(8,128)(2,1)S(1)} %all_gather.3), channel_id=1, source_target_pairs={{0,128},{128,256},{256,384},{384,0},{1,129},{129,257},{257,385},{3... | collective-permute-start | bytes 2359304 | tf_op jit(solution)/shard_map/ppermute | solution.py:102
  21.6 21.6 %collective-permute-start = (bf16[1024,384]{1,0:T(8,128)(2,1)S(1)}, bf16[1024,384]{1,0:T(8,128)(2,1)S(1)}, u32[]{:S(2)}, u32[]{:S(2)}) collective-permute-start(bf16[1024,384]{1,0:T(8,128)(2,1)S(1)} %all_gather.3), channel_id=1, source_target_pairs={{0,384},{128,0},{256,128},{384,256},{1,385},{129,1},{257,129},{385... | collective-permute-start | bytes 2359304 | tf_op jit(solution)/shard_map/ppermute | solution.py:103
  39.8 11.2 %collective-permute-start.2 = (bf16[512,384]{1,0:T(8,128)(2,1)S(1)}, bf16[512,384]{1,0:T(8,128)(2,1)S(1)}, u32[]{:S(2)}, u32[]{:S(2)}) collective-permute-start(bf16[512,384]{1,0:T(8,128)(2,1)S(1)} %slice.64), channel_id=1, source_target_pairs={{0,128},{128,256},{256,384},{384,0},{1,129},{129,257},{257,385},{3... | collective-permute-start | bytes 1179656 | tf_op jit(solution)/shard_map/ppermute | solution.py:105
  43.3 14.3 %copy-start.3 = (s32[3,4096]{1,0:T(4,128)S(1)}, s32[3,4096]{1,0:T(4,128)}, u32[]{:S(2)}) copy-start(s32[3,4096]{1,0:T(4,128)} %param.5) | copy-start | bytes 147460
  43.3 12.1 %collective-permute-start.3 = (bf16[512,384]{1,0:T(8,128)(2,1)S(1)}, bf16[512,384]{1,0:T(8,128)(2,1)S(1)}, u32[]{:S(2)}, u32[]{:S(2)}) collective-permute-start(bf16[512,384]{1,0:T(8,128)(2,1)S(1)} %slice.65), channel_id=1, source_target_pairs={{0,384},{128,0},{256,128},{384,256},{1,385},{129,1},{257,129},{385... | collective-permute-start | bytes 1179656 | tf_op jit(solution)/shard_map/ppermute | solution.py:106
  45.9 13.6 %copy-start.2 = (bf16[384,128]{1,0:T(8,128)(2,1)S(1)}, bf16[384,128]{1,0:T(8,128)(2,1)}, u32[]{:S(2)}) copy-start(bf16[384,128]{1,0:T(8,128)(2,1)} %param.4) | copy-start | bytes 294916
  55.6 7.7 %copy-start.1 = (bf16[4096,384]{1,0:T(8,128)(2,1)}, bf16[4096,384]{1,0:T(8,128)(2,1)S(1)}, u32[]{:S(2)}) copy-start(bf16[4096,384]{1,0:T(8,128)(2,1)S(1)} %constant_dynamic-update-slice_fusion.own_ref) | copy-start | bytes 9437188
  55.6 7.7 %collective-permute-start.4 = (bf16[4096,384]{1,0:T(8,128)(2,1)S(1)}, bf16[4096,384]{1,0:T(8,128)(2,1)}, u32[]{:S(2)}, u32[]{:S(2)}) collective-permute-start(bf16[4096,384]{1,0:T(8,128)(2,1)S(1)} %constant_dynamic-update-slice_fusion.own_ref), channel_id=1, source_target_pairs={{0,32},{32,0},{1,33},{33,1},{2,34},{34,2},{3,35},{35,3},{4,36},{36... | collective-permute-start | bytes 9437192 | tf_op jit(solution)/shard_map/ppermute | solution.py:138
  91.4 3.3 %copy-start = (bf16[4096,384]{1,0:T(8,128)(2,1)S(1)}, bf16[4096,384]{1,0:T(8,128)(2,1)}, u32[]{:S(2)}) copy-start(bf16[4096,384]{1,0:T(8,128)(2,1)} %shard_map.37) | copy-start | bytes 9437188

commit v18 on v12

--- a/solution.py
+++ b/solution.py
@@ -33,17 +33,22 @@
     return built.astype(jnp.bfloat16)
 
 
-def gather_kernel(first_ref, second_ref, table_ref, op_ref, out_ref, table, first_buf, second_buf):
+def gather_kernel(first_ref, second_ref, own_ref, near_ref, far_ref, op_ref, out_ref,
+                  table, first_buf, second_buf):
     tile = first_buf.shape[0]
     step = 256
 
     @pl.when(pl.program_id(0) == 0)
     def _():
-        def widen(i, carry):
-            rows = pl.ds(pl.multiple_of(i * step, step), step)
-            table[rows, :] = table_ref[rows, :].astype(jnp.float32)
-            return carry
-        lax.fori_loop(0, table.shape[0] // step, widen, 0)
+        offset = 0
+        for piece in (own_ref, near_ref, far_ref):
+            def widen(i, carry, piece=piece, offset=offset):
+                start = pl.multiple_of(i * step, step)
+                table[pl.ds(start + offset, step), :] = (
+                    piece[pl.ds(start, step), :].astype(jnp.float32))
+                return carry
+            lax.fori_loop(0, piece.shape[0] // step, widen, 0)
+            offset += piece.shape[0]
 
     base = pl.program_id(0) * tile
 
@@ -61,15 +66,18 @@
     out_ref[...] = combine_rows(first_buf[...], second_buf[...], op_ref[...])
 
 
-def build_descriptors(table, first_pos, second_pos, operator_id):
-    n_rows, width = table.shape
+def build_descriptors(own, near, far, first_pos, second_pos, operator_id):
+    half, width = own.shape
+    n_rows = half + near.shape[0] + far.shape[0]
     pairs = first_pos.shape[0]
     tile = min(GATHER_TILE, pairs)
     grid_spec = pltpu.PrefetchScalarGridSpec(
         num_scalar_prefetch=2,
         grid=(pairs // tile,),
         in_specs=[
-            pl.BlockSpec((n_rows, width), lambda i, p1, p2: (0, 0)),
+            pl.BlockSpec(own.shape, lambda i, p1, p2: (0, 0)),
+            pl.BlockSpec(near.shape, lambda i, p1, p2: (0, 0)),
+            pl.BlockSpec(far.shape, lambda i, p1, p2: (0, 0)),
             pl.BlockSpec((tile, 1), lambda i, p1, p2: (i, 0)),
         ],
         out_specs=pl.BlockSpec((tile, width), lambda i, p1, p2: (i, 0)),
@@ -86,7 +94,7 @@
         cost_estimate=pl.CostEstimate(
             flops=10 * pairs * width, transcendentals=0,
             bytes_accessed=n_rows * width * 2 + pairs * width * 2),
-    )(first_pos, second_pos, table, operator_id[:, None])
+    )(first_pos, second_pos, own, near, far, operator_id[:, None])
 
 
 def ring_gather(block, axis, n):
@@ -127,10 +135,11 @@
     n_samp = n_y * n_zl
     sample_count = residuals.shape[0] * n_samp
 
-    rows = lax.all_gather(tier_one, "zh", axis=0, tiled=True)
-    rows = ring_gather(rows, "x", n_x)
-    other = lax.ppermute(rows, "c", perm=[(0, 1), (1, 0)])
-    rows = jnp.concatenate([rows, other], axis=0)
+    pair_rows = lax.all_gather(tier_one, "zh", axis=0, tiled=True)
+    swap = [(0, 1), (1, 0)]
+    other_near = lax.ppermute(pair_rows, "c", perm=swap)
+    rows = ring_gather(pair_rows, "x", n_x)
+    other_far = lax.ppermute(rows[pair_rows.shape[0]:], "c", perm=swap)
     my_c = lax.axis_index("c")
     my_x = lax.axis_index("x")
 
@@ -142,7 +151,7 @@
         return ((half * n_x + x_slot) * n_zh + zh) * local_rows + r
 
     built = build_descriptors(
-        rows, position(pair_list[0]), position(pair_list[1]), pair_list[2]
+        rows, other_near, other_far, position(pair_list[0]), position(pair_list[1]), pair_list[2]
     )
 
     product = jnp.dot(built, residuals, preferred_element_type=jnp.float32)

time: 156 us -> 157 us (level)
  local copies, waits for them, and re-layouts: 10.8 us -> 7.42 us
  starting transfers between devices: 13.6 us -> 16.1 us
  other arithmetic: 4.42 us -> 6.08 us
    ppermute x1 -> x2, waiting for transfers between devices: 3.01 us -> 0.01 us  [the longest x1 0.01 us: per_device(): other_near = lax.ppermute(pair_rows, 'c', perm=swap)]
    ppermute x1, waiting for transfers between devices: 2.73 us -> 5.31 us  [ring_gather(): far_a = lax.ppermute(from_left[:half], axis, perm=fwd)]
    ppermute x1 -> x2, starting transfers between devices: 1.91 us -> 4.32 us  [the longest x1 2.41 us: per_device(): other_near = lax.ppermute(pair_rows, 'c', perm=swap)]
    concatenate x1 -> x0, local copies, waits for them, and re-layouts: 2.01 us -> none  [per_device(): rows = jnp.concatenate([rows, other], axis=0)]
    concatenate x0 -> x1, other arithmetic: none -> 1.65 us  [ring_gather(): return jnp.concatenate([block, from_right, far_a, far_b, from_left], axis=0)]
  transfers between devices with their start and end apart: 5 -> 6, of which waited for: 4 -> 3; matrix products, arithmetic and copies ran while one was open for 4% -> 5% of each run, Pallas kernels for 0% -> 0%
where the time goes in v18:
time: 157 us
  blocking collectives  72.2 us (46%)
  Pallas kernels  28.1 us (18%)
  waiting for transfers between devices  24.3 us (15%)
  starting transfers between devices  16.1 us (10%)
  local copies, waits for them, and re-layouts  7.42 us (5%)
  other arithmetic  6.08 us (4%)
  matrix products  2.11 us (1%)
    all_to_all x1, blocking collectives, per_device(): arrived = lax.all_to_all(packed, SAMP_AXES, 0, 0, tiled=False)  53 us
    pallas_call x1, Pallas kernels, build_descriptors(): pl.pallas_call(gather_kernel, grid_spec=grid_spec, out_shape=jax.ShapeDty...  28.1 us
    all_gather x1, blocking collectives, per_device(): pair_rows = lax.all_gather(tier_one, 'zh', axis=0, tiled=True)  19.2 us
    ppermute x1, waiting for transfers between devices, ring_gather(): from_left = lax.ppermute(block, axis, perm=fwd)  14.7 us
    ppermute x1, waiting for transfers between devices, ring_gather(): far_a = lax.ppermute(from_left[:half], axis, perm=fwd)  5.31 us
    ppermute x1, waiting for transfers between devices, ring_gather(): far_b = lax.ppermute(from_right[half:], axis, perm=bwd)  4.22 us
    unnamed x10, local copies, waits for them, and re-layouts  3.52 us
    ppermute x1, starting transfers between devices, ring_gather(): from_right = lax.ppermute(block, axis, perm=bwd)  3.46 us
  transfers between devices with their start and end apart: 6, of which 3 were waited for; matrix products, arithmetic and copies ran while one was open for 5% of the time, Pallas kernels for 0%

profile of v18, /device:TPU:6, one launch (start us, length us, event | category | flops | bytes accessed | tf_op | source)
XLA Modules:
  0.0 156.6 jit_solution(18080547709034561129)
XLA Ops:
  0.0 19.2 %all_gather.3 = bf16[1024,384]{1,0:T(8,128)(2,1)S(1)} all-gather(bf16[512,384]{1,0:T(8,128)(2,1)} %param.3), channel_id=1, replica_groups=mesh['x'=4,'zh'=2,'c'=2,'y'=8,'zl'=4] {'zh'}, dimensions={0}, use_global_device_ids=true | all-gather | bytes 1179648 | tf_op jit(solution)/shard_map/all_gather | solution.py:138
  19.2 0.0 copy-start.1
  19.2 0.0 copy-start.2
  19.2 2.5 %collective-permute-start.1 = (bf16[1024,384]{1,0:T(8,128)(2,1)S(1)}, bf16[1024,384]{1,0:T(8,128)(2,1)S(1)}, u32[]{:S(2)}, u32[]{:S(2)}) collective-permute-start(bf16[1024,384]{1,0:T(8,128)(2,1)S(1)} %all_gather.3), channel_id=1, source_target_pairs={{0,128},{128,256},{256,384},{384,0},{1,129},{129,257},{257,385},{3... | collective-permute-start | bytes 2359304 | tf_op jit(solution)/shard_map/ppermute | solution.py:104
  21.7 3.5 %collective-permute-start = (bf16[1024,384]{1,0:T(8,128)(2,1)S(1)}, bf16[1024,384]{1,0:T(8,128)(2,1)S(1)}, u32[]{:S(2)}, u32[]{:S(2)}) collective-permute-start(bf16[1024,384]{1,0:T(8,128)(2,1)S(1)} %all_gather.3), channel_id=1, source_target_pairs={{0,384},{128,0},{256,128},{384,256},{1,385},{129,1},{257,129},{385... | collective-permute-start | bytes 2359304 | tf_op jit(solution)/shard_map/ppermute | solution.py:105
  25.2 14.7 %collective-permute-done.1 = bf16[1024,384]{1,0:T(8,128)(2,1)S(1)} collective-permute-done((bf16[1024,384]{1,0:T(8,128)(2,1)S(1)}, bf16[1024,384]{1,0:T(8,128)(2,1)S(1)}, u32[]{:S(2)}, u32[]{:S(2)}) %collective-permute-start.1) | collective-permute-done | bytes 786464 | tf_op jit(solution)/shard_map/ppermute | solution.py:104
  39.9 3.4 %collective-permute-start.2 = (bf16[512,384]{1,0:T(8,128)(2,1)S(1)}, bf16[512,384]{1,0:T(8,128)(2,1)S(1)}, u32[]{:S(2)}, u32[]{:S(2)}) collective-permute-start(bf16[512,384]{1,0:T(8,128)(2,1)S(1)} %slice.66), channel_id=1, source_target_pairs={{0,128},{128,256},{256,384},{384,0},{1,129},{129,257},{257,385},{3... | collective-permute-start | bytes 1179656 | tf_op jit(solution)/shard_map/ppermute | solution.py:107
  43.3 0.0 collective-permute-done
  43.4 2.4 %collective-permute-start.3 = (bf16[512,384]{1,0:T(8,128)(2,1)S(1)}, bf16[512,384]{1,0:T(8,128)(2,1)S(1)}, u32[]{:S(2)}, u32[]{:S(2)}) collective-permute-start(bf16[512,384]{1,0:T(8,128)(2,1)S(1)} %slice.67), channel_id=1, source_target_pairs={{0,384},{128,0},{256,128},{384,256},{1,385},{129,1},{257,129},{385... | collective-permute-start | bytes 1179656 | tf_op jit(solution)/shard_map/ppermute | solution.py:108
  45.8 5.3 %collective-permute-done.2 = bf16[512,384]{1,0:T(8,128)(2,1)S(1)} collective-permute-done((bf16[512,384]{1,0:T(8,128)(2,1)S(1)}, bf16[512,384]{1,0:T(8,128)(2,1)S(1)}, u32[]{:S(2)}, u32[]{:S(2)}) %collective-permute-start.2) | collective-permute-done | bytes 393248 | tf_op jit(solution)/shard_map/ppermute | solution.py:107
  51.2 4.2 %collective-permute-done.3 = bf16[512,384]{1,0:T(8,128)(2,1)S(1)} collective-permute-done((bf16[512,384]{1,0:T(8,128)(2,1)S(1)}, bf16[512,384]{1,0:T(8,128)(2,1)S(1)}, u32[]{:S(2)}, u32[]{:S(2)}) %collective-permute-start.3) | collective-permute-done | bytes 393248 | tf_op jit(solution)/shard_map/ppermute | solution.py:108
  55.4 1.6 %pad_maximum_fusion = bf16[3072,384]{1,0:T(8,128)(2,1)} fusion(bf16[1024,384]{1,0:T(8,128)(2,1)S(1)} %collective-permute-done.1, bf16[512,384]{1,0:T(8,128)(2,1)S(1)} %collective-permute-done.3, bf16[512,384]{1,0:T(8,128)(2,1)S(1)} %collective-permute-done.2, bf16[1024,384]{1,0:T(8,128)(2,1)S(1)} %collective-permute-done), kind=kLoop, calls=%fused_computation.5 | loop fusion | flops 9437184 | bytes 4718592 | tf_op jit(solution)/shard_map/concatenate | solution.py:109
  57.0 1.9 %collective-permute-start.5 = (bf16[3072,384]{1,0:T(8,128)(2,1)}, bf16[3072,384]{1,0:T(8,128)(2,1)}, u32[]{:S(2)}, u32[]{:S(2)}) collective-permute-start(bf16[3072,384]{1,0:T(8,128)(2,1)} %pad_maximum_fusion), channel_id=1, source_target_pairs={{0,32},{32,0},{1,33},{33,1},{2,34},{34,2},{3,35},{35,3},{4,36},{36... | collective-permute-start | bytes 7077896 | tf_op jit(solution)/shard_map/ppermute | solution.py:142
  58.9 2.4 %collective-permute-start.4 = (bf16[1024,384]{1,0:T(8,128)(2,1)S(1)}, bf16[1024,384]{1,0:T(8,128)(2,1)}, u32[]{:S(2)}, u32[]{:S(2)}) collective-permute-start(bf16[1024,384]{1,0:T(8,128)(2,1)S(1)} %all_gather.3), channel_id=1, source_target_pairs={{0,32},{32,0},{1,33},{33,1},{2,34},{34,2},{3,35},{35,3},{4,36},{36... | collective-permute-start | bytes 2359304 | tf_op jit(solution)/shard_map/ppermute | solution.py:140
  61.4 0.0 copy-done.1
  61.4 0.1 convert_reduce_fusion.2
  61.5 0.0 copy-done.2
  61.5 1.0 constant_dynamic-update-slice_fusion.4
  62.5 2.0 %copy.5.op_ref = s32[4096,1]{1,0:T(8,128)} copy(s32[4096,1]{0,1:T(1,128)S(1)} %get-tuple-element.15) | data formatting | bytes 32768 | tf_op jit(solution)/shard_map/broadcast_in_dim;squeeze | solution.py:97
  64.5 0.7 fusion.16
  65.2 1.0 constant_dynamic-update-slice_fusion.3
  66.2 0.8 constant_dynamic-update-slice_fusion.2
  67.0 0.8 constant_dynamic-update-slice_fusion.1
  67.7 1.0 constant_dynamic-update-slice_fusion.own_ref
  68.8 0.0 collective-permute-done.4.near_ref
  68.8 0.0 collective-permute-done.5.far_ref
  68.8 28.1 %shard_map.37 = bf16[4096,384]{1,0:T(8,128)(2,1)} custom-call(s32[4096]{0:T(1024)} %get-tuple-element.29.first_ref, s32[4096]{0:T(1024)} %get-tuple-element.30.second_ref, bf16[4096,384]{1,0:T(8,128)(2,1)} %constant_dynamic-update-slice_fusion.own_ref, bf16[1024,384]{1,0:T(8,128)(2,1)} %collective-permute-done.4.near_ref, ...), custom_call_target="tpu_custom_call" | custom-call | flops 15728640 | bytes 9437184 | tf_op jit(solution)/shard_map/pallas_call | solution.py:87
  96.9 0.0 copy-start
  96.9 3.3 %fusion = (f32[4096]{0:T(1024)S(1)}, f32[4096]{0:T(1024)S(1)}) fusion(bf16[4096,384]{1,0:T(8,128)(2,1)} %shard_map.37), kind=kLoop, calls=%fused_computation.2 | loop fusion | flops 6283264 | bytes 3178496 | tf_op jit(solution)/shard_map/reduce_sum | solution.py:160
  100.2 0.0 copy-done
  100.2 1.2 fusion.1
  101.7 0.6 concatenate.12
  102.3 53.0 %all_to_all.5 = bf16[32,144,128]{2,1,0:T(8,128)(2,1)S(1)} all-to-all(bf16[32,144,128]{2,1,0:T(8,128)(2,1)S(1)} %concatenate.12), channel_id=1, replica_groups=mesh['x'=4,'zh'=2,'c'=2,'y'=8,'zl'=4] {'y','zl'}, dimensions={0} | all-to-all | bytes 2359296 | tf_op jit(solution)/shard_map/all_to_all | solution.py:181
  155.3 0.1 fusion.37
  155.5 0.2 convert_reduce_fusion.1
  155.6 0.9 fusion.4
  (20 shorter events, 0.3 us)
Async XLA Ops:
  19.2 42.2 %copy-start.1 = (bf16[384,128]{1,0:T(8,128)(2,1)S(1)}, bf16[384,128]{1,0:T(8,128)(2,1)}, u32[]{:S(2)}) copy-start(bf16[384,128]{1,0:T(8,128)(2,1)} %param.4) | copy-start | bytes 294916
  19.2 42.3 %copy-start.2 = (s32[3,4096]{1,0:T(4,128)S(1)}, s32[3,4096]{1,0:T(4,128)}, u32[]{:S(2)}) copy-start(s32[3,4096]{1,0:T(4,128)} %param.5) | copy-start | bytes 147460
  19.2 20.7 %collective-permute-start.1 = (bf16[1024,384]{1,0:T(8,128)(2,1)S(1)}, bf16[1024,384]{1,0:T(8,128)(2,1)S(1)}, u32[]{:S(2)}, u32[]{:S(2)}) collective-permute-start(bf16[1024,384]{1,0:T(8,128)(2,1)S(1)} %all_gather.3), channel_id=1, source_target_pairs={{0,128},{128,256},{256,384},{384,0},{1,129},{129,257},{257,385},{3... | collective-permute-start | bytes 2359304 | tf_op jit(solution)/shard_map/ppermute | solution.py:104
  21.7 21.6 %collective-permute-start = (bf16[1024,384]{1,0:T(8,128)(2,1)S(1)}, bf16[1024,384]{1,0:T(8,128)(2,1)S(1)}, u32[]{:S(2)}, u32[]{:S(2)}) collective-permute-start(bf16[1024,384]{1,0:T(8,128)(2,1)S(1)} %all_gather.3), channel_id=1, source_target_pairs={{0,384},{128,0},{256,128},{384,256},{1,385},{129,1},{257,129},{385... | collective-permute-start | bytes 2359304 | tf_op jit(solution)/shard_map/ppermute | solution.py:105
  39.9 11.2 %collective-permute-start.2 = (bf16[512,384]{1,0:T(8,128)(2,1)S(1)}, bf16[512,384]{1,0:T(8,128)(2,1)S(1)}, u32[]{:S(2)}, u32[]{:S(2)}) collective-permute-start(bf16[512,384]{1,0:T(8,128)(2,1)S(1)} %slice.66), channel_id=1, source_target_pairs={{0,128},{128,256},{256,384},{384,0},{1,129},{129,257},{257,385},{3... | collective-permute-start | bytes 1179656 | tf_op jit(solution)/shard_map/ppermute | solution.py:107
  43.4 12.0 %collective-permute-start.3 = (bf16[512,384]{1,0:T(8,128)(2,1)S(1)}, bf16[512,384]{1,0:T(8,128)(2,1)S(1)}, u32[]{:S(2)}, u32[]{:S(2)}) collective-permute-start(bf16[512,384]{1,0:T(8,128)(2,1)S(1)} %slice.67), channel_id=1, source_target_pairs={{0,384},{128,0},{256,128},{384,256},{1,385},{129,1},{257,129},{385... | collective-permute-start | bytes 1179656 | tf_op jit(solution)/shard_map/ppermute | solution.py:108
  57.0 11.7 %collective-permute-start.5 = (bf16[3072,384]{1,0:T(8,128)(2,1)}, bf16[3072,384]{1,0:T(8,128)(2,1)}, u32[]{:S(2)}, u32[]{:S(2)}) collective-permute-start(bf16[3072,384]{1,0:T(8,128)(2,1)} %pad_maximum_fusion), channel_id=1, source_target_pairs={{0,32},{32,0},{1,33},{33,1},{2,34},{34,2},{3,35},{35,3},{4,36},{36... | collective-permute-start | bytes 7077896 | tf_op jit(solution)/shard_map/ppermute | solution.py:142
  58.9 9.8 %collective-permute-start.4 = (bf16[1024,384]{1,0:T(8,128)(2,1)S(1)}, bf16[1024,384]{1,0:T(8,128)(2,1)}, u32[]{:S(2)}, u32[]{:S(2)}) collective-permute-start(bf16[1024,384]{1,0:T(8,128)(2,1)S(1)} %all_gather.3), channel_id=1, source_target_pairs={{0,32},{32,0},{1,33},{33,1},{2,34},{34,2},{3,35},{35,3},{4,36},{36... | collective-permute-start | bytes 2359304 | tf_op jit(solution)/shard_map/ppermute | solution.py:140
  96.9 3.3 %copy-start = (bf16[4096,384]{1,0:T(8,128)(2,1)S(1)}, bf16[4096,384]{1,0:T(8,128)(2,1)}, u32[]{:S(2)}) copy-start(bf16[4096,384]{1,0:T(8,128)(2,1)} %shard_map.37) | copy-start | bytes 9437188
